TPU v7x, 32 devices: a whole 2x2x4 slice. The times are simulated.
32 devices in a mesh: parts: 2 (over y), seq: 4 (over z), section: 2 (over x), tp: 2 (over core).
Axes of the slice: x: 2, y: 2, z: 4, core: 2. Of those that a mesh axis runs over, the one named last changes fastest.
Arguments:
- queries: bfloat16 [2, 2048, 4096], P('section', ('parts', 'seq'), 'tp'), parts along dimension 1, may hold values from -82 to 82
- keys_values: bfloat16 [2, 2, 2048, 512], P('section', None, ('parts', 'seq'), 'tp'), parts along dimension 2, may hold values from -4 to 4
- lengths: int32 [2], P('parts'), parts along dimension 0, may hold values from 769 to 1024, as said below
Outputs:
- attended: bfloat16 [2, 2048, 4096], P('section', ('parts', 'seq'), 'tp'), parts along dimension 1
- window_cache: bfloat16 [2, 2, 4096, 512], P('section', None, ('parts', 'seq'), 'tp'), parts along dimension 2
There are 2 independent parts, one for each index of `parts`. A program takes and returns all parts, laid end to end along the dimension named above; each array names one. Nothing has to cross between parts.
Inputs may be any that keep to these rules, and one draw needn't show every extreme that they name: `lengths`: the first request's length lies in min(2048, 1024 - 256) + 1 to min(2048, 1024 - 256) + 256; the second request's length is 1024.
All inputs are finite; a program needn't handle non-finite values.
Results may differ from a plain program's by a relative error of at most 0.0077.
Values may be sent and summed in bfloat16 or wider, within the bound.
No kernel may reach another device: no remote copies, remote signals or barrier semaphores. Data moves between devices by JAX's collectives and lax.ppermute only.
A program may use at most 64 MiB of HBM per device.

v0:
```python
import math

import jax
import jax.numpy as jnp
from jax import lax
from jax.sharding import PartitionSpec as P

HD = 128
WINDOW = 2048


rope_base = 1000000.0
neg_floor = -1e30


def passed_along(x, axis, by):
    devices = lax.axis_size(axis)
    pairs = [(i, i + by) for i in range(devices) if 0 <= i + by < devices]
    return lax.ppermute(x, axis, pairs)


def rotate(field, positions):
    half_dim = field.shape[-1] // 2
    frequency = jnp.exp(
        jnp.arange(half_dim, dtype=jnp.float32) * (-2.0 * math.log(rope_base) / field.shape[-1])
    )
    angles = positions.astype(jnp.float32)[:, None] * frequency[None, :]
    cosine = jnp.cos(angles)[:, None, :]
    sine_part = jnp.sin(angles)[:, None, :]
    lower_half = field[..., :half_dim]
    upper_half = field[..., half_dim:]
    return jnp.concatenate(
        [
            lower_half * cosine - upper_half * sine_part,
            upper_half * cosine + lower_half * sine_part,
        ],
        axis=-1,
    )


def local(queries, keys_values, lengths):
    seq_len = lengths[0]
    shard_rows = queries.shape[1]
    width = keys_values.shape[-1]
    kv_heads_dev = width // HD
    heads_dev = queries.shape[-1] // HD
    group_size = heads_dev // kv_heads_dev
    seq_index = lax.axis_index("seq")
    seq_count = lax.axis_size("seq")
    first_pos = seq_index * shard_rows
    positions = first_pos + jnp.arange(shard_rows, dtype=jnp.int32)
    scale = 1.0 / math.sqrt(HD)
    rotated_q = rotate(queries[0].reshape(shard_rows, heads_dev, HD).astype(jnp.float32), positions)
    rotated_q = rotated_q.astype(jnp.bfloat16).reshape(shard_rows, kv_heads_dev, group_size, HD)
    rotated_k = rotate(
        keys_values[0, 0].reshape(shard_rows, kv_heads_dev, HD).astype(jnp.float32), positions
    )
    own_block = jnp.stack(
        [rotated_k.astype(jnp.bfloat16).reshape(shard_rows, width), keys_values[0, 1]]
    )

    def attend(state_now, kv_piece, start_pos):
        row_top, totals, numer_acc = state_now
        piece_rows = kv_piece.shape[1]
        key_pos = start_pos + jnp.arange(piece_rows, dtype=jnp.int32)
        key_rows = kv_piece[0].reshape(piece_rows, kv_heads_dev, HD)
        value_rows = kv_piece[1].reshape(piece_rows, kv_heads_dev, HD)
        scores = (
            jnp.einsum("qkgd,skd->kgqs", rotated_q, key_rows, preferred_element_type=jnp.float32)
            * scale
        )
        allowed = (key_pos[None, :] <= positions[:, None]) & (
            key_pos[None, :] > positions[:, None] - WINDOW
        )
        allowed = allowed & (key_pos[None, :] >= 0) & (key_pos[None, :] < seq_len)
        top_new = jnp.maximum(row_top, jnp.max(jnp.where(allowed, scores, neg_floor), axis=-1))
        weights = jnp.where(allowed, jnp.exp(scores - top_new[..., None]), 0.0)
        rescale = jnp.exp(row_top - top_new)
        totals = totals * rescale + jnp.sum(weights, axis=-1)
        update = jnp.einsum(
            "kgqs,skd->qkgd",
            weights.astype(jnp.bfloat16),
            value_rows,
            preferred_element_type=jnp.float32,
        )
        numer_acc = numer_acc * jnp.moveaxis(rescale, 2, 0)[..., None] + update
        return (top_new, totals, numer_acc)

    start_state = (
        jnp.full((kv_heads_dev, group_size, shard_rows), neg_floor, jnp.float32),
        jnp.zeros((kv_heads_dev, group_size, shard_rows), jnp.float32),
        jnp.zeros((shard_rows, kv_heads_dev, group_size, HD), jnp.float32),
    )
    reach_count = min(WINDOW // shard_rows, seq_count - 1)
    tail_start = first_pos - reach_count * shard_rows
    older_blocks = []
    moving = own_block
    for hop in range(reach_count):
        moving = passed_along(moving, "seq", 1)
        older_blocks.insert(0, moving)
    tail_rows = jnp.concatenate(older_blocks + [own_block], axis=1)
    piece_count = tail_rows.shape[1] // shard_rows
    limit_rows = max(1024, shard_rows)
    multiple = max(
        (
            divisor
            for divisor in range(1, piece_count + 1)
            if piece_count % divisor == 0 and divisor * shard_rows <= limit_rows
        )
    )
    key_block = multiple * shard_rows

    def key_step(blk_index, state_now):
        kv_piece = lax.dynamic_slice_in_dim(tail_rows, blk_index * key_block, key_block, 1)
        return attend(state_now, kv_piece, tail_start + blk_index * key_block)

    final_state = lax.fori_loop(0, tail_rows.shape[1] // key_block, key_step, start_state)
    row_top, totals, numer_acc = final_state
    valid = positions < seq_len
    denom = jnp.where(valid[:, None, None], jnp.moveaxis(totals, 2, 0), 1.0)
    result = jnp.where(valid[:, None, None, None], numer_acc / denom[..., None], 0.0)
    attended = result.astype(jnp.bfloat16).reshape(1, shard_rows, heads_dev * HD)
    slot_rows = WINDOW // seq_count
    zero_pad = jnp.zeros((2, WINDOW, width), jnp.bfloat16)
    padded_own = jnp.concatenate([zero_pad, own_block, zero_pad], axis=1)
    begin_row = jnp.clip(seq_len - first_pos, 0, WINDOW + shard_rows)
    outbox = lax.dynamic_slice_in_dim(padded_own, begin_row, WINDOW, 1)
    received = lax.all_to_all(outbox, "seq", split_axis=1, concat_axis=1, tiled=True)
    window_cache = (
        received.reshape(2, seq_count, slot_rows, width)
        .astype(jnp.float32)
        .sum(axis=1)
        .astype(jnp.bfloat16)
    )
    return (attended, window_cache[None])


def solution(mesh):
    return jax.shard_map(
        local,
        mesh=mesh,
        in_specs=(
            P("section", ("parts", "seq"), "tp"),
            P("section", None, ("parts", "seq"), "tp"),
            P("parts"),
        ),
        out_specs=(
            P("section", ("parts", "seq"), "tp"),
            P("section", None, ("parts", "seq"), "tp"),
        ),
        check_vma=False,
    )
```

profile of v0, /device:TPU:20, one launch (start us, length us, event | category | flops | bytes accessed | tf_op | source)
XLA Modules:
  0.0 137.0 jit_solution(13391435506342000637)
XLA Ops:
  0.6 1.0 slice_convert_fusion
  1.6 0.1 copy.62
  1.8 0.1 copy.61
  1.9 0.3 multiply_cosine_fusion
  2.3 0.7 pad_maximum_fusion
  3.0 3.5 %collective-permute-start = (bf16[2,256,256]{1,2,0:T(8,128)(2,1)}, bf16[2,256,256]{1,2,0:T(8,128)(2,1)}, u32[]{:S(2)}, u32[]{:S(2)}) collective-permute-start(bf16[2,256,256]{1,2,0:T(8,128)(2,1)} %pad_maximum_fusion), channel_id=1, source_target_pairs={{0,4},{4,8},{8,12},{1,5},{5,9},{9,13},{2,6},{6,10},{10,14},{3,7},{... | collective-permute-start | bytes 786440 | tf_op jit(solution)/shard_map/ppermute | solution.py:19
  6.5 1.1 copy.53
  8.3 1.1 broadcast_in_dim.84
  9.4 30.1 %fusion.9 = bf16[2,2048,256]{2,0,1:T(2,128)(2,1)} fusion(s32[]{:T(128)S(6)} %min.4, bf16[2,2048,256]{2,0,1:T(2,128)(2,1)S(1)} %broadcast_in_dim.84, bf16[2,256,256]{2,0,1:T(2,128)(2,1)S(1)} %copy.53), kind=kLoop, calls=%fused_computation.13 | loop fusion | flops 2097152 | bytes 4456452 | tf_op jit(solution)/shard_map/concatenate | solution.py:125
  39.5 4.7 %all-to-all-start = ((bf16[2,2048,256]{2,0,1:T(2,128)(2,1)}), bf16[2,2048,256]{2,0,1:T(2,128)(2,1)S(1)}, u32[]{:S(2)}, u32[]{:S(2)}) async-start(bf16[2,2048,256]{2,0,1:T(2,128)(2,1)} %fusion.9), calls=%async_computation | async-start | bytes 4194304 | tf_op jit(solution)/shard_map/all_to_all | solution.py:128
  44.2 0.8 copy.50
  45.0 0.7 copy.48
  45.7 0.2 convert_bitcast_fusion
  46.0 0.4 copy.65
  46.4 0.0 copy-start.1
  46.4 0.7 fusion.28
  47.1 0.0 collective-permute-done
  47.1 3.4 %collective-permute-start.1 = (bf16[2,256,256]{1,2,0:T(8,128)(2,1)}, bf16[2,256,256]{1,2,0:T(8,128)(2,1)S(1)}, u32[]{:S(2)}, u32[]{:S(2)}) collective-permute-start(bf16[2,256,256]{1,2,0:T(8,128)(2,1)} %collective-permute-done), channel_id=1, source_target_pairs={{0,4},{4,8},{8,12},{1,5},{5,9},{9,13},{2,6},{6,10},{10,14},{3,7},{... | collective-permute-start | bytes 786440 | tf_op jit(solution)/shard_map/ppermute | solution.py:19
  50.5 1.4 subtract_convert_fusion
  51.9 43.8 %collective-permute-done.1 = bf16[2,256,256]{1,2,0:T(8,128)(2,1)S(1)} collective-permute-done((bf16[2,256,256]{1,2,0:T(8,128)(2,1)}, bf16[2,256,256]{1,2,0:T(8,128)(2,1)S(1)}, u32[]{:S(2)}, u32[]{:S(2)}) %collective-permute-start.1) | collective-permute-done | bytes 262176 | tf_op jit(solution)/shard_map/ppermute | solution.py:19
  95.7 2.1 %collective-permute-start.2 = (bf16[2,256,256]{1,2,0:T(8,128)(2,1)S(1)}, bf16[2,256,256]{1,2,0:T(8,128)(2,1)S(1)}, u32[]{:S(2)}, u32[]{:S(2)}) collective-permute-start(bf16[2,256,256]{1,2,0:T(8,128)(2,1)S(1)} %collective-permute-done.1), channel_id=1, source_target_pairs={{0,4},{4,8},{8,12},{1,5},{5,9},{9,13},{2,6},{6,10},{10,14},{3,7},{... | collective-permute-start | bytes 786440 | tf_op jit(solution)/shard_map/ppermute | solution.py:19
  97.8 0.9 and_and_fusion
  98.7 5.7 %collective-permute-done.2 = bf16[2,256,256]{1,2,0:T(8,128)(2,1)S(1)} collective-permute-done((bf16[2,256,256]{1,2,0:T(8,128)(2,1)S(1)}, bf16[2,256,256]{1,2,0:T(8,128)(2,1)S(1)}, u32[]{:S(2)}, u32[]{:S(2)}) %collective-permute-start.2) | collective-permute-done | bytes 262176 | tf_op jit(solution)/shard_map/ppermute | solution.py:19
  104.4 1.1 maximum_maximum_fusion
  105.5 0.1 fusion.29
  105.6 7.7 %fusion = (f32[2,8,256]{2,1,0:T(8,128)S(1)}, f32[2,1024,256,8]{2,1,3,0:T(8,128)}) fusion(pred[256,1024]{0,1:T(8,128)(4,1)S(1)} %and_and_fusion, bf16[1024,2,128,1]{0,2,3,1:T(8,128)(2,1)S(1)} %bitcast.64, bf16[256,2,8,64]{3,0,2,1:T(8,128)(2,1)S(1)} %bitcast.63, bf16[256,2,8,64]{3,0,2,1:T(8,128)(2,1)S(1)} %bitcast.62), kind=kOutput, calls=%fused_computation.2 | convolution fusion | flops 1088417792 | bytes 18628608 | tf_op jit(solution)/shard_map/while/body/eval_jaxpr/qkgd,skd->kgqs/dot_general | solution.py:69
  113.3 9.1 %fusion.3 = f32[2,8,256]{2,1,0:T(8,128)S(1)} fusion(f32[2,1024,256,8]{2,1,3,0:T(8,128)} %get-tuple-element.57, f32[2,8,256]{2,1,0:T(8,128)S(1)} %get-tuple-element.53, pred[256,1024]{0,1:T(8,128)(4,1)S(1)} %and_and_fusion), kind=kLoop, calls=%fused_computation.5 | loop fusion | flops 16773120 | bytes 17072128 | tf_op jit(solution)/shard_map/while/body/eval_jaxpr/reduce_sum | solution.py:79
  122.4 9.4 %fusion.12 = bf16[256,2,8,128]{0,3,2,1:T(8,128)(2,1)S(1)} fusion(bf16[1024,2,128,1]{0,2,3,1:T(8,128)(2,1)S(1)} %bitcast.72, f32[2,1024,256,8]{2,1,3,0:T(8,128)} %get-tuple-element.57, f32[2,8,256]{2,1,0:T(8,128)S(1)} %get-tuple-element.53, pred[256,1024]{0,1:T(8,128)(4,1)S(1)} %and_and_fusion, f32[256,2,8]{0,2,1:T(8,128)S(1)} %fusion.19, ...), kind=kOutput, calls=%fused_computation.17 | convolution fusion | flops 1092616192 | bytes 18661632 | tf_op jit(solution)/shard_map/while/body/eval_jaxpr/kgqs,skd->qkgd/dot_general | solution.py:80
  131.8 1.4 %copy.54 = bf16[1,256,2048]{2,1,0:T(8,128)(2,1)} copy(bf16[1,256,2048]{1,2,0:T(8,128)(2,1)S(1)} %bitcast.70) | data formatting | bytes 2097152
  133.2 0.0 all-to-all-done
  133.2 2.9 %reduce_sum.26 = bf16[2,512,256]{2,0,1:T(2,128)(2,1)S(1)} reduce(bf16[2,4,512,256]{3,0,2,1:T(2,128)(2,1)S(1)} %bitcast.61, bf16[]{:T(256)} %constant.50.clone.1), dimensions={1}, to_apply=%region_2.0 | reduce | flops 786432 | bytes 2621442 | tf_op jit(solution)/shard_map/reduce_sum | solution.py:132
  136.2 0.9 copy.55
  (15 shorter events, 0.1 us)
Async XLA Ops:
  3.0 44.1 %collective-permute-start = (bf16[2,256,256]{1,2,0:T(8,128)(2,1)}, bf16[2,256,256]{1,2,0:T(8,128)(2,1)}, u32[]{:S(2)}, u32[]{:S(2)}) collective-permute-start(bf16[2,256,256]{1,2,0:T(8,128)(2,1)} %pad_maximum_fusion), channel_id=1, source_target_pairs={{0,4},{4,8},{8,12},{1,5},{5,9},{9,13},{2,6},{6,10},{10,14},{3,7},{... | collective-permute-start | bytes 786440 | tf_op jit(solution)/shard_map/ppermute | solution.py:19
  39.5 6.2 %copy-start = (bf16[1,256,2048]{2,1,0:T(8,128)(2,1)S(1)}, bf16[1,256,2048]{2,1,0:T(8,128)(2,1)}, u32[]{:S(2)}) copy-start(bf16[1,256,2048]{2,1,0:T(8,128)(2,1)} %param.3) | copy-start | bytes 3145732
  39.5 93.7 %all-to-all-start = ((bf16[2,2048,256]{2,0,1:T(2,128)(2,1)}), bf16[2,2048,256]{2,0,1:T(2,128)(2,1)S(1)}, u32[]{:S(2)}, u32[]{:S(2)}) async-start(bf16[2,2048,256]{2,0,1:T(2,128)(2,1)} %fusion.9), calls=%async_computation | async-start | bytes 4194304 | tf_op jit(solution)/shard_map/all_to_all | solution.py:128
  46.4 4.1 %copy-start.1 = (f32[256,64]{1,0:T(8,128)S(1)}, f32[256,64]{1,0:T(8,128)}, u32[]{:S(2)}) copy-start(f32[256,64]{1,0:T(8,128)} %copy.50) | copy-start | bytes 196612
  46.4 4.1 %copy-start.2 = (f32[256,64]{1,0:T(8,128)S(1)}, f32[256,64]{1,0:T(8,128)}, u32[]{:S(2)}) copy-start(f32[256,64]{1,0:T(8,128)} %copy.48) | copy-start | bytes 196612
  47.1 48.6 %collective-permute-start.1 = (bf16[2,256,256]{1,2,0:T(8,128)(2,1)}, bf16[2,256,256]{1,2,0:T(8,128)(2,1)S(1)}, u32[]{:S(2)}, u32[]{:S(2)}) collective-permute-start(bf16[2,256,256]{1,2,0:T(8,128)(2,1)} %collective-permute-done), channel_id=1, source_target_pairs={{0,4},{4,8},{8,12},{1,5},{5,9},{9,13},{2,6},{6,10},{10,14},{3,7},{... | collective-permute-start | bytes 786440 | tf_op jit(solution)/shard_map/ppermute | solution.py:19
  95.7 8.7 %collective-permute-start.2 = (bf16[2,256,256]{1,2,0:T(8,128)(2,1)S(1)}, bf16[2,256,256]{1,2,0:T(8,128)(2,1)S(1)}, u32[]{:S(2)}, u32[]{:S(2)}) collective-permute-start(bf16[2,256,256]{1,2,0:T(8,128)(2,1)S(1)} %collective-permute-done.1), channel_id=1, source_target_pairs={{0,4},{4,8},{8,12},{1,5},{5,9},{9,13},{2,6},{6,10},{10,14},{3,7},{... | collective-permute-start | bytes 786440 | tf_op jit(solution)/shard_map/ppermute | solution.py:19
where the time goes:
time: 137 us
  waiting for transfers between devices  49.5 us (36%)
  other arithmetic  47.8 us (35%)
  matrix products  17.1 us (12%)
  starting transfers between devices  13.7 us (10%)
  local copies, waits for them, and re-layouts  7.42 us (5%)
  between operations  1.53 us (1%)
    ppermute x3, waiting for transfers between devices, passed_along(): return lax.ppermute(x, axis, pairs)  49.5 us
    concatenate x1, other arithmetic, local(): padded_own = jnp.concatenate([zero_pad, own_block, zero_pad], axis=1)  30.1 us
    dot_general x1, matrix products, attend(): jnp.einsum('kgqs,skd->qkgd', weights.astype(jnp.bfloat16), value_rows, pr...  9.41 us
    reduce_sum x1, other arithmetic, attend(): totals = totals * rescale + jnp.sum(weights, axis=-1)  9.12 us
    ppermute x3, starting transfers between devices, passed_along(): return lax.ppermute(x, axis, pairs)  8.94 us
    dot_general x1, matrix products, attend(): jnp.einsum('qkgd,skd->kgqs', rotated_q, key_rows, preferred_element_type=...  7.66 us
    all_to_all x1, starting transfers between devices, local(): lax.all_to_all(outbox, 'seq', split_axis=1, concat_axis=1, tiled=True)  4.73 us
    reduce_sum x1, other arithmetic, local(): window_cache = received.reshape(2, seq_count, slot_rows, width).astype(jn...  2.93 us
  transfers between devices with their start and end apart: 4, of which 2 were waited for; matrix products, arithmetic and copies ran while one was open for 48% of the time, Pallas kernels for 0%

commit v1 on v0

v1 whole, which is shorter than its diff:
```python
import functools
import math

import jax
import jax.numpy as jnp
from jax import lax
from jax.experimental import pallas as pl
from jax.experimental.pallas import tpu as pltpu
from jax.sharding import PartitionSpec as P

HD = 128
WINDOW = 2048


rope_base = 1000000.0
neg_floor = -1e30


def rotate(field, positions):
    half_dim = field.shape[-1] // 2
    frequency = jnp.exp(
        jnp.arange(half_dim, dtype=jnp.float32) * (-2.0 * math.log(rope_base) / field.shape[-1])
    )
    angles = positions.astype(jnp.float32)[:, None] * frequency[None, :]
    cosine = jnp.cos(angles)[:, None, :]
    sine_part = jnp.sin(angles)[:, None, :]
    lower_half = field[..., :half_dim]
    upper_half = field[..., half_dim:]
    return jnp.concatenate(
        [
            lower_half * cosine - upper_half * sine_part,
            upper_half * cosine + lower_half * sine_part,
        ],
        axis=-1,
    )


def attend_kernel(scalars, q_ref, k_ref, v_ref, o_ref, *, rows, span):
    seq_len = scalars[0]
    first_pos = scalars[1]
    key_start = pl.multiple_of(scalars[2], 256)
    q = q_ref[...]
    k = k_ref[0, pl.ds(key_start, span), :]
    v = v_ref[0, pl.ds(key_start, span), :]
    scores = lax.dot_general(
        q, k, (((1,), (1,)), ((), ())), preferred_element_type=jnp.float32
    ) * (1.0 / math.sqrt(HD))
    query_pos = first_pos + lax.broadcasted_iota(jnp.int32, (rows, span), 0)
    key_pos = key_start + lax.broadcasted_iota(jnp.int32, (rows, span), 1)
    allowed = (key_pos <= query_pos) & (key_pos > query_pos - WINDOW) & (key_pos < seq_len)
    row_top = jnp.max(jnp.where(allowed, scores, neg_floor), axis=-1, keepdims=True)
    weights = jnp.where(allowed, jnp.exp(scores - row_top), 0.0)
    totals = jnp.sum(weights, axis=-1, keepdims=True)
    numer = jnp.dot(weights.astype(jnp.bfloat16), v, preferred_element_type=jnp.float32)
    valid = (first_pos + lax.broadcasted_iota(jnp.int32, (rows, 1), 0)) < seq_len
    denom = jnp.where(valid, totals, 1.0)
    o_ref[...] = jnp.where(valid, numer / denom, 0.0).astype(o_ref.dtype)


def attention(scalars, rotated_q, gathered, heads_dev, group_size, span):
    rows = rotated_q.shape[0]
    tokens = gathered.shape[1]
    kernel = functools.partial(attend_kernel, rows=rows, span=span)
    grid_spec = pltpu.PrefetchScalarGridSpec(
        num_scalar_prefetch=1,
        grid=(heads_dev,),
        in_specs=[
            pl.BlockSpec((rows, HD), lambda h, s: (0, h)),
            pl.BlockSpec((1, tokens, HD), lambda h, s: (0, 0, h // group_size)),
            pl.BlockSpec((1, tokens, HD), lambda h, s: (1, 0, h // group_size)),
        ],
        out_specs=pl.BlockSpec((rows, HD), lambda h, s: (0, h)),
    )
    return pl.pallas_call(
        kernel,
        grid_spec=grid_spec,
        out_shape=jax.ShapeDtypeStruct((rows, heads_dev * HD), jnp.bfloat16),
    )(scalars, rotated_q, gathered, gathered)


def local(queries, keys_values, lengths):
    seq_len = lengths[0]
    shard_rows = queries.shape[1]
    width = keys_values.shape[-1]
    kv_heads_dev = width // HD
    heads_dev = queries.shape[-1] // HD
    group_size = heads_dev // kv_heads_dev
    seq_index = lax.axis_index("seq")
    seq_count = lax.axis_size("seq")
    first_pos = seq_index * shard_rows
    positions = first_pos + jnp.arange(shard_rows, dtype=jnp.int32)
    rotated_q = rotate(queries[0].reshape(shard_rows, heads_dev, HD).astype(jnp.float32), positions)
    rotated_q = rotated_q.astype(jnp.bfloat16).reshape(shard_rows, heads_dev * HD)
    rotated_k = rotate(
        keys_values[0, 0].reshape(shard_rows, kv_heads_dev, HD).astype(jnp.float32), positions
    )
    own_block = jnp.stack(
        [rotated_k.astype(jnp.bfloat16).reshape(shard_rows, width), keys_values[0, 1]]
    )
    gathered = lax.all_gather(own_block, "seq", axis=1, tiled=True)
    tokens = gathered.shape[1]

    reach_count = min(WINDOW // shard_rows, seq_count - 1)
    span = (reach_count + 1) * shard_rows
    key_start = jnp.maximum(first_pos - reach_count * shard_rows, 0)
    scalars = jnp.stack([seq_len, first_pos, key_start]).astype(jnp.int32)
    attended = attention(scalars, rotated_q, gathered, heads_dev, group_size, span)
    attended = attended.reshape(1, shard_rows, heads_dev * HD)

    slot_rows = WINDOW // seq_count
    padded = jnp.concatenate([jnp.zeros((2, WINDOW, width), jnp.bfloat16), gathered], axis=1)
    begin_row = seq_len + seq_index * slot_rows
    window_cache = lax.dynamic_slice_in_dim(padded, begin_row, slot_rows, 1)
    del tokens
    return (attended, window_cache[None])


def solution(mesh):
    return jax.shard_map(
        local,
        mesh=mesh,
        in_specs=(
            P("section", ("parts", "seq"), "tp"),
            P("section", None, ("parts", "seq"), "tp"),
            P("parts"),
        ),
        out_specs=(
            P("section", ("parts", "seq"), "tp"),
            P("section", None, ("parts", "seq"), "tp"),
        ),
        check_vma=False,
    )
```

time: 137 us -> 69.2 us (0.51); the launches traced: 137 us -> 67.9 us
  other arithmetic: 47.8 us -> 5.41 us
  waiting for transfers between devices: 49.5 us -> 24 us
  Pallas kernels: 0 us -> 19.7 us
  matrix products: 17.1 us -> 0 us
  starting transfers between devices: 13.7 us -> 0.04 us
  between operations: 1.53 us -> 14.8 us
  local copies, waits for them, and re-layouts: 7.42 us -> 3.96 us
    ppermute x3 -> x0, waiting for transfers between devices: 49.5 us -> none  [passed_along(): return lax.ppermute(x, axis, pairs)]
    concatenate x2 -> x0, other arithmetic: 31.1 us -> none  [the longest x1 30.1 us: local(): padded_own = jnp.concatenate([zero_pad, own_block, zero_pad], axis=1)]
    all_gather x0 -> x1, waiting for transfers between devices: none -> 24 us  [local(): gathered = lax.all_gather(own_block, 'seq', axis=1, tiled=True)]
    pallas_call x0 -> x1, Pallas kernels: none -> 19.7 us  [attention(): pl.pallas_call(kernel, grid_spec=grid_spec, out_shape=jax.ShapeDtypeStruc...]
    dot_general x2 -> x0, matrix products: 17.1 us -> none  [the longest x1 9.41 us: attend(): jnp.einsum('kgqs,skd->qkgd', weights.astype(jnp.bfloat16), value_rows, pr...]
    reduce_sum x2 -> x0, other arithmetic: 12 us -> none  [the longest x1 9.12 us: attend(): totals = totals * rescale + jnp.sum(weights, axis=-1)]
    ppermute x3 -> x0, starting transfers between devices: 8.94 us -> none  [passed_along(): return lax.ppermute(x, axis, pairs)]
    all_to_all x1 -> x0, starting transfers between devices: 4.73 us -> none  [local(): lax.all_to_all(outbox, 'seq', split_axis=1, concat_axis=1, tiled=True)]
  transfers between devices with their start and end apart: 4 -> 1, of which waited for: 2 -> 1; matrix products, arithmetic and copies ran while one was open for 48% -> 6% of each run, Pallas kernels for 0% -> 0%
where the time goes in v1:
time: 69.2 us; the launch traced here: 67.9 us
  waiting for transfers between devices  24 us (35%)
  Pallas kernels  19.7 us (28%)
  between operations  14.8 us (21%)
  other arithmetic  5.41 us (8%)
  local copies, waits for them, and re-layouts  3.96 us (6%)
    all_gather x1, waiting for transfers between devices, local(): gathered = lax.all_gather(own_block, 'seq', axis=1, tiled=True)  24 us
    pallas_call x1, Pallas kernels, attention(): pl.pallas_call(kernel, grid_spec=grid_spec, out_shape=jax.ShapeDtypeStruc...  19.7 us
    broadcast_in_dim x1, local copies, waits for them, and re-layouts, local(): return (attended, window_cache[None])  2.04 us
    unnamed x4, local copies, waits for them, and re-layouts  1.69 us
  transfers between devices with their start and end apart: 1, of which 1 were waited for; matrix products, arithmetic and copies ran while one was open for 6% of the time, Pallas kernels for 0%

profile of v1, /device:TPU:20, one launch (start us, length us, event | category | flops | bytes accessed | tf_op | source)
XLA Modules:
  0.0 67.9 jit_solution(38796161235878298)
XLA Ops:
  7.2 0.0 copy-start
  7.2 0.0 all-gather.2.cloned.1.call-start
  7.3 1.1 %slice_convert_fusion = (f32[1,1,256,256]{3,2,1,0:T(8,128)S(1)}, bf16[1,256,256]{2,1,0:T(8,128)(2,1)S(1)}) fusion(bf16[1,2,256,256]{3,2,1,0:T(8,128)(2,1)} %param.4), kind=kLoop, calls=%fused_computation.14 | loop fusion | flops 65536 | bytes 655360 | tf_op jit(solution)/shard_map/convert_element_type | solution.py:95
  8.3 0.1 reshape.84
  8.5 0.5 multiply_cosine_fusion
  9.0 0.5 subtract_convert_fusion.1
  9.5 0.4 pad_maximum_fusion.2
  9.9 0.1 convert_element_type.42
  10.0 0.7 %pad_maximum_fusion.1 = bf16[2,256,256]{2,1,0:T(8,128)(2,1)} fusion(bf16[1,256,256]{2,1,0:T(8,128)(2,1)S(1)} %get-tuple-element.7, bf16[1,256,256]{2,1,0:T(8,128)(2,1)S(1)} %convert_element_type.42), kind=kLoop, calls=%fused_computation.7 | loop fusion | flops 131072 | bytes 524288 | tf_op jit(solution)/shard_map/stack | solution.py:97
  10.7 0.0 all-gather.2.cloned.1.call-update
  11.4 0.0 copy-done
  11.4 0.2 convert_bitcast_fusion
  11.6 0.4 copy.5
  12.0 0.8 %subtract_convert_fusion = (bf16[256,16,64]{2,1,0:T(8,128)(2,1)S(1)}, bf16[256,16,64]{2,1,0:T(8,128)(2,1)S(1)}) fusion(f32[256,16,128]{2,1,0:T(8,128)S(1)} %bitcast.19, f32[256,64]{1,0:T(8,128)S(1)} %get-tuple-element.9, f32[256,64]{1,0:T(8,128)S(1)} %get-tuple-element.8), kind=kLoop, calls=%fused_computation.3 | loop fusion | flops 2097152 | bytes 3276800 | tf_op jit(solution)/shard_map/convert.4
  12.8 0.6 pad_maximum_fusion
  13.4 1.3 %copy.8 = bf16[32,8,16,128]{3,1,2,0:T(8,128)(2,1)} copy(bf16[32,8,16,128]{3,2,1,0:T(8,128)(2,1)S(1)} %bitcast.21) | data formatting | bytes 2097152
  14.7 0.7 pad_add_fusion.scalars
  15.3 24.0 %all-gather.2.cloned.1.call-done.k_ref.v_ref = bf16[2,1024,256]{2,1,0:T(8,128)(2,1)} async-done(((bf16[2,256,256]{2,1,0:T(8,128)(2,1)}), bf16[2,1024,256]{2,1,0:T(8,128)(2,1)}) %all-gather.2.cloned.1.call-update) | async-done | bytes 1048592 | tf_op jit(solution)/shard_map/all_gather | solution.py:100
  39.3 2.0 %fusion = bf16[1,2,512,256]{3,2,1,0:T(8,128)(2,1)} fusion(s32[]{:T(128)S(6)} %select_n.3, bf16[2,1024,256]{2,1,0:T(8,128)(2,1)} %all-gather.2.cloned.1.call-done.k_ref.v_ref), kind=kLoop, calls=%fused_computation.6 | loop fusion | bytes 1572868 | tf_op jit(solution)/shard_map/broadcast_in_dim | solution.py:115
  41.4 19.7 %shard_map.50 = bf16[256,2048]{1,0:T(8,128)(2,1)} custom-call(s32[3]{0:T(128)} %pad_add_fusion.scalars, bf16[256,2048]{1,0:T(8,128)(2,1)} %bitcast.20, bf16[2,1024,256]{2,1,0:T(8,128)(2,1)} %all-gather.2.cloned.1.call-done.k_ref.v_ref, bf16[2,1024,256]{2,1,0:T(8,128)(2,1)} %all-gather.2.cloned.1.call-done.k_ref.v_ref), custom_call_target="tpu_custom_call" | custom-call | tf_op jit(solution)/shard_map/pallas_call | solution.py:74
  (2 shorter events, 0.0 us)
Async XLA Ops:
  7.2 4.2 %copy-start = (bf16[1,256,2048]{2,1,0:T(8,128)(2,1)S(1)}, bf16[1,256,2048]{2,1,0:T(8,128)(2,1)}, u32[]{:S(2)}) copy-start(bf16[1,256,2048]{2,1,0:T(8,128)(2,1)} %param.3) | copy-start | bytes 3145732
  7.2 32.1 %all-gather.2.cloned.1.call-start = ((), (), s32[]{:S(2)}) async-start(), calls=%async_computation | async-start | bytes 1310720 | tf_op jit(solution)/shard_map/all_gather | solution.py:100
Sparse Core Ops, SparseCore 0:
  10.8 28.4 all-gather.1

commit v2 on v1

--- a/solution.py
+++ b/solution.py
@@ -97,7 +97,10 @@
     own_block = jnp.stack(
         [rotated_k.astype(jnp.bfloat16).reshape(shard_rows, width), keys_values[0, 1]]
     )
-    gathered = lax.all_gather(own_block, "seq", axis=1, tiled=True)
+    outbox = jnp.broadcast_to(own_block[:, None], (2, seq_count, shard_rows, width))
+    gathered = lax.all_to_all(
+        outbox.reshape(2, seq_count * shard_rows, width), "seq", 1, 1, tiled=True
+    )
     tokens = gathered.shape[1]
 
     reach_count = min(WINDOW // shard_rows, seq_count - 1)

time: 69.2 us -> 58.4 us (0.84)
  the two profiles are of different devices: /device:TPU:20 before, /device:TPU:0 now
where the time goes in v2:
time: 58.4 us; the launch traced here: 58.2 us
  waiting for transfers between devices  21.2 us (36%)
  Pallas kernels  19.7 us (34%)
  starting transfers between devices  6.32 us (11%)
  local copies, waits for them, and re-layouts  4.97 us (9%)
  other arithmetic  4.64 us (8%)
  between operations  1.42 us (2%)
    all_to_all x1, waiting for transfers between devices, local(): lax.all_to_all(outbox.reshape(2, seq_count * shard_rows, width), 'seq', 1...  21.2 us
    pallas_call x1, Pallas kernels, attention(): pl.pallas_call(kernel, grid_spec=grid_spec, out_shape=jax.ShapeDtypeStruc...  19.7 us
    all_to_all x1, starting transfers between devices, local(): lax.all_to_all(outbox.reshape(2, seq_count * shard_rows, width), 'seq', 1...  6.32 us
    unnamed x6, local copies, waits for them, and re-layouts  1.63 us
    broadcast_in_dim x1, local copies, waits for them, and re-layouts, local(): jnp.broadcast_to(own_block[:, None], (2, seq_count, shard_rows, width))  1.51 us
    another operation x2, other arithmetic  1.24 us
    broadcast_in_dim x1, local copies, waits for them, and re-layouts, local(): return (attended, window_cache[None])  1.19 us
  transfers between devices with their start and end apart: 1, of which 1 were waited for; matrix products, arithmetic and copies ran while one was open for 7% of the time, Pallas kernels for 0%

profile of v2, /device:TPU:0, one launch (start us, length us, event | category | flops | bytes accessed | tf_op | source)
XLA Modules:
  0.0 58.2 jit_solution(4305882447227406213)
XLA Ops:
  0.7 1.0 %slice_convert_fusion = (f32[1,1,256,256]{3,2,1,0:T(8,128)S(1)}, bf16[1,256,256]{2,1,0:T(8,128)(2,1)S(1)}) fusion(bf16[1,2,256,256]{3,2,1,0:T(8,128)(2,1)} %param.4), kind=kLoop, calls=%fused_computation.14 | loop fusion | flops 65536 | bytes 655360 | tf_op jit(solution)/shard_map/convert_element_type | solution.py:95
  1.7 0.1 reshape.89
  1.8 0.5 multiply_cosine_fusion
  2.3 0.5 subtract_convert_fusion.1
  2.8 0.4 pad_maximum_fusion.2
  3.2 0.1 convert_element_type.42
  3.3 0.0 copy-start.1
  3.3 0.3 copy.8
  3.6 1.5 %broadcast_in_dim.4 = bf16[2,4,256,256]{3,0,2,1:T(2,128)(2,1)} broadcast(bf16[2,256,256]{2,0,1:T(2,128)(2,1)S(1)} %copy.8), dimensions={0,2,3} | broadcast | bytes 1310720 | tf_op jit(solution)/shard_map/broadcast_in_dim | solution.py:100
  5.1 6.3 %all-to-all-start = ((bf16[2,1024,256]{2,0,1:T(2,128)(2,1)}), bf16[2,1024,256]{2,0,1:T(2,128)(2,1)S(1)}, u32[]{:S(2)}, u32[]{:S(2)}) async-start(bf16[2,1024,256]{2,0,1:T(2,128)(2,1)} %bitcast.3), calls=%async_computation | async-start | bytes 2097152 | tf_op jit(solution)/shard_map/all_to_all | solution.py:101
  12.1 0.0 copy-done.1
  12.1 0.2 convert_bitcast_fusion
  12.4 0.4 copy.12
  12.7 0.8 %subtract_convert_fusion = (bf16[256,16,64]{2,1,0:T(8,128)(2,1)S(1)}, bf16[256,16,64]{2,1,0:T(8,128)(2,1)S(1)}) fusion(f32[256,16,128]{2,1,0:T(8,128)S(1)} %bitcast.20, f32[256,64]{1,0:T(8,128)S(1)} %get-tuple-element.9, f32[256,64]{1,0:T(8,128)S(1)} %get-tuple-element.8), kind=kLoop, calls=%fused_computation.3 | loop fusion | flops 2097152 | bytes 3276800 | tf_op jit(solution)/shard_map/convert.4
  13.5 0.6 pad_maximum_fusion
  14.1 1.2 %copy.15 = bf16[32,8,16,128]{3,1,2,0:T(8,128)(2,1)} copy(bf16[32,8,16,128]{3,2,1,0:T(8,128)(2,1)S(1)} %bitcast.22) | data formatting | bytes 2097152
  15.3 0.7 %pad_add_fusion.scalars = s32[3]{0:T(128)} fusion(s32[1]{0:T(128)} %bitcast.1, s32[1]{0:T(128)} %bitcast, s32[1]{0:T(128)} %copy.16), kind=kLoop, calls=%fused_computation.16 | loop fusion | flops 6 | bytes 24 | tf_op jit(solution)/shard_map/stack | solution.py:109
  16.0 21.2 %all-to-all-done = bf16[2,1024,256]{2,0,1:T(2,128)(2,1)S(1)} async-done(((bf16[2,1024,256]{2,0,1:T(2,128)(2,1)}), bf16[2,1024,256]{2,0,1:T(2,128)(2,1)S(1)}, u32[]{:S(2)}, u32[]{:S(2)}) %all-to-all-start) | async-done | bytes 1048608 | tf_op jit(solution)/shard_map/all_to_all | solution.py:101
  37.2 0.1 copy.9.k_ref.v_ref
  37.3 0.0 copy-start
  37.3 1.2 %fusion = bf16[1,2,512,256]{3,2,1,0:T(8,128)(2,1)} fusion(s32[]{:T(128)S(6)} %select_n.3, bf16[2,1024,256]{2,1,0:T(8,128)(2,1)S(1)} %copy.9.k_ref.v_ref), kind=kLoop, calls=%fused_computation.6 | loop fusion | bytes 1572868 | tf_op jit(solution)/shard_map/broadcast_in_dim | solution.py:118
  38.5 0.0 copy-done
  38.5 19.7 %shard_map.50 = bf16[256,2048]{1,0:T(8,128)(2,1)} custom-call(s32[3]{0:T(128)} %pad_add_fusion.scalars, bf16[256,2048]{1,0:T(8,128)(2,1)} %bitcast.21, bf16[2,1024,256]{2,1,0:T(8,128)(2,1)} %copy-done, bf16[2,1024,256]{2,1,0:T(8,128)(2,1)} %copy-done), custom_call_target="tpu_custom_call" | custom-call | tf_op jit(solution)/shard_map/pallas_call | solution.py:74
  (3 shorter events, 0.0 us)
Async XLA Ops:
  3.3 8.8 %copy-start.1 = (bf16[1,256,2048]{2,1,0:T(8,128)(2,1)S(1)}, bf16[1,256,2048]{2,1,0:T(8,128)(2,1)}, u32[]{:S(2)}) copy-start(bf16[1,256,2048]{2,1,0:T(8,128)(2,1)} %param.3) | copy-start | bytes 3145732
  5.1 32.0 %all-to-all-start = ((bf16[2,1024,256]{2,0,1:T(2,128)(2,1)}), bf16[2,1024,256]{2,0,1:T(2,128)(2,1)S(1)}, u32[]{:S(2)}, u32[]{:S(2)}) async-start(bf16[2,1024,256]{2,0,1:T(2,128)(2,1)} %bitcast.3), calls=%async_computation | async-start | bytes 2097152 | tf_op jit(solution)/shard_map/all_to_all | solution.py:101
  37.3 1.2 %copy-start = (bf16[2,1024,256]{2,1,0:T(8,128)(2,1)}, bf16[2,1024,256]{2,1,0:T(8,128)(2,1)S(1)}, u32[]{:S(2)}) copy-start(bf16[2,1024,256]{2,1,0:T(8,128)(2,1)S(1)} %copy.9.k_ref.v_ref) | copy-start | bytes 3145732

commit v3 on v2

--- a/solution.py
+++ b/solution.py
@@ -35,46 +35,51 @@
     )
 
 
-def attend_kernel(scalars, q_ref, k_ref, v_ref, o_ref, *, rows, span):
+def attend_kernel(scalars, q_ref, k_ref, v_ref, o_ref, bias_ref, *, rows, span, group):
     seq_len = scalars[0]
     first_pos = scalars[1]
     key_start = pl.multiple_of(scalars[2], 256)
-    q = q_ref[...]
-    k = k_ref[0, pl.ds(key_start, span), :]
-    v = v_ref[0, pl.ds(key_start, span), :]
-    scores = lax.dot_general(
-        q, k, (((1,), (1,)), ((), ())), preferred_element_type=jnp.float32
-    ) * (1.0 / math.sqrt(HD))
     query_pos = first_pos + lax.broadcasted_iota(jnp.int32, (rows, span), 0)
     key_pos = key_start + lax.broadcasted_iota(jnp.int32, (rows, span), 1)
     allowed = (key_pos <= query_pos) & (key_pos > query_pos - WINDOW) & (key_pos < seq_len)
-    row_top = jnp.max(jnp.where(allowed, scores, neg_floor), axis=-1, keepdims=True)
-    weights = jnp.where(allowed, jnp.exp(scores - row_top), 0.0)
-    totals = jnp.sum(weights, axis=-1, keepdims=True)
-    numer = jnp.dot(weights.astype(jnp.bfloat16), v, preferred_element_type=jnp.float32)
+    bias_ref[...] = jnp.where(allowed, 0.0, neg_floor)
+    k = k_ref[0, pl.ds(key_start, span), :]
+    v = v_ref[0, pl.ds(key_start, span), :]
     valid = (first_pos + lax.broadcasted_iota(jnp.int32, (rows, 1), 0)) < seq_len
-    denom = jnp.where(valid, totals, 1.0)
-    o_ref[...] = jnp.where(valid, numer / denom, 0.0).astype(o_ref.dtype)
+    scale = 1.0 / math.sqrt(HD)
+    for head in range(group):
+        cols = slice(head * HD, (head + 1) * HD)
+        raw = lax.dot_general(
+            q_ref[:, cols], k, (((1,), (1,)), ((), ())), preferred_element_type=jnp.float32
+        ) + bias_ref[...]
+        row_top = jnp.max(raw, axis=-1, keepdims=True)
+        weights = jnp.exp((raw - row_top) * scale)
+        totals = jnp.sum(weights, axis=-1, keepdims=True)
+        numer = jnp.dot(weights.astype(jnp.bfloat16), v, preferred_element_type=jnp.float32)
+        denom = jnp.where(valid, totals, 1.0)
+        o_ref[:, cols] = jnp.where(valid, numer / denom, 0.0).astype(o_ref.dtype)
 
 
-def attention(scalars, rotated_q, gathered, heads_dev, group_size, span):
+def attention(scalars, rotated_q, gathered, kv_heads_dev, group_size, span):
     rows = rotated_q.shape[0]
     tokens = gathered.shape[1]
-    kernel = functools.partial(attend_kernel, rows=rows, span=span)
+    kernel = functools.partial(attend_kernel, rows=rows, span=span, group=group_size)
+    width = group_size * HD
     grid_spec = pltpu.PrefetchScalarGridSpec(
         num_scalar_prefetch=1,
-        grid=(heads_dev,),
+        grid=(kv_heads_dev,),
         in_specs=[
-            pl.BlockSpec((rows, HD), lambda h, s: (0, h)),
-            pl.BlockSpec((1, tokens, HD), lambda h, s: (0, 0, h // group_size)),
-            pl.BlockSpec((1, tokens, HD), lambda h, s: (1, 0, h // group_size)),
+            pl.BlockSpec((rows, width), lambda j, s: (0, j)),
+            pl.BlockSpec((1, tokens, HD), lambda j, s: (0, 0, j)),
+            pl.BlockSpec((1, tokens, HD), lambda j, s: (1, 0, j)),
         ],
-        out_specs=pl.BlockSpec((rows, HD), lambda h, s: (0, h)),
+        out_specs=pl.BlockSpec((rows, width), lambda j, s: (0, j)),
+        scratch_shapes=[pltpu.VMEM((rows, span), jnp.float32)],
     )
     return pl.pallas_call(
         kernel,
         grid_spec=grid_spec,
-        out_shape=jax.ShapeDtypeStruct((rows, heads_dev * HD), jnp.bfloat16),
+        out_shape=jax.ShapeDtypeStruct((rows, kv_heads_dev * width), jnp.bfloat16),
     )(scalars, rotated_q, gathered, gathered)
 
 
@@ -107,7 +112,7 @@
     span = (reach_count + 1) * shard_rows
     key_start = jnp.maximum(first_pos - reach_count * shard_rows, 0)
     scalars = jnp.stack([seq_len, first_pos, key_start]).astype(jnp.int32)
-    attended = attention(scalars, rotated_q, gathered, heads_dev, group_size, span)
+    attended = attention(scalars, rotated_q, gathered, kv_heads_dev, group_size, span)
     attended = attended.reshape(1, shard_rows, heads_dev * HD)
 
     slot_rows = WINDOW // seq_count

time: 58.4 us -> 49.9 us (0.85)
  Pallas kernels: 19.7 us -> 11.1 us
    pallas_call x1, Pallas kernels: 19.7 us -> 11.1 us  [attention(): pl.pallas_call(kernel, grid_spec=grid_spec, out_shape=jax.ShapeDtypeStruc...]
  transfers between devices with their start and end apart: 1 -> 1, of which waited for: 1 -> 1; matrix products, arithmetic and copies ran while one was open for 7% -> 8% of each run, Pallas kernels for 0% -> 0%
where the time goes in v3:
time: 49.9 us; the launch traced here: 49.6 us
  waiting for transfers between devices  21.2 us (42%)
  Pallas kernels  11.1 us (22%)
  starting transfers between devices  6.32 us (13%)
  local copies, waits for them, and re-layouts  4.99 us (10%)
  other arithmetic  4.64 us (9%)
  between operations  1.42 us (3%)
    all_to_all x1, waiting for transfers between devices, local(): lax.all_to_all(outbox.reshape(2, seq_count * shard_rows, width), 'seq', 1...  21.2 us
    pallas_call x1, Pallas kernels, attention(): pl.pallas_call(kernel, grid_spec=grid_spec, out_shape=jax.ShapeDtypeStruc...  11.1 us
    all_to_all x1, starting transfers between devices, local(): lax.all_to_all(outbox.reshape(2, seq_count * shard_rows, width), 'seq', 1...  6.32 us
    unnamed x6, local copies, waits for them, and re-layouts  1.63 us
    broadcast_in_dim x1, local copies, waits for them, and re-layouts, local(): jnp.broadcast_to(own_block[:, None], (2, seq_count, shard_rows, width))  1.51 us
    another operation x2, other arithmetic  1.24 us
    broadcast_in_dim x1, local copies, waits for them, and re-layouts, local(): return (attended, window_cache[None])  1.21 us
  transfers between devices with their start and end apart: 1, of which 1 were waited for; matrix products, arithmetic and copies ran while one was open for 8% of the time, Pallas kernels for 0%

profile of v3, /device:TPU:0, one launch (start us, length us, event | category | flops | bytes accessed | tf_op | source)
XLA Modules:
  0.0 49.6 jit_solution(9772451535554629587)
XLA Ops:
  0.7 1.0 %slice_convert_fusion = (f32[1,1,256,256]{3,2,1,0:T(8,128)S(1)}, bf16[1,256,256]{2,1,0:T(8,128)(2,1)S(1)}) fusion(bf16[1,2,256,256]{3,2,1,0:T(8,128)(2,1)} %param.4), kind=kLoop, calls=%fused_computation.14 | loop fusion | flops 65536 | bytes 655360 | tf_op jit(solution)/shard_map/convert_element_type | solution.py:100
  1.7 0.1 reshape.89
  1.8 0.5 %multiply_cosine_fusion = (f32[256,64]{1,0:T(8,128)S(1)}, f32[256,64]{1,0:T(8,128)S(1)}) fusion(f32[64]{0:T(128)S(1)} %multiply_exponential_fusion, f32[256]{0:T(256)S(1)} %add_convert_fusion.2), kind=kLoop, calls=%fused_computation.11 | loop fusion | flops 16384 | bytes 132352 | tf_op jit(solution)/shard_map/cos | solution.py:25
  2.3 0.5 subtract_convert_fusion.1
  2.8 0.4 pad_maximum_fusion.2
  3.2 0.1 convert_element_type.42
  3.3 0.0 copy-start.1
  3.3 0.3 copy.8
  3.6 1.5 %broadcast_in_dim.4 = bf16[2,4,256,256]{3,0,2,1:T(2,128)(2,1)} broadcast(bf16[2,256,256]{2,0,1:T(2,128)(2,1)S(1)} %copy.8), dimensions={0,2,3} | broadcast | bytes 1310720 | tf_op jit(solution)/shard_map/broadcast_in_dim | solution.py:105
  5.1 6.3 %all-to-all-start = ((bf16[2,1024,256]{2,0,1:T(2,128)(2,1)}), bf16[2,1024,256]{2,0,1:T(2,128)(2,1)S(1)}, u32[]{:S(2)}, u32[]{:S(2)}) async-start(bf16[2,1024,256]{2,0,1:T(2,128)(2,1)} %bitcast.3), calls=%async_computation | async-start | bytes 2097152 | tf_op jit(solution)/shard_map/all_to_all | solution.py:106
  12.1 0.0 copy-done.1
  12.1 0.2 convert_bitcast_fusion
  12.4 0.4 copy.12
  12.7 0.8 %subtract_convert_fusion = (bf16[256,16,64]{2,1,0:T(8,128)(2,1)S(1)}, bf16[256,16,64]{2,1,0:T(8,128)(2,1)S(1)}) fusion(f32[256,16,128]{2,1,0:T(8,128)S(1)} %bitcast.20, f32[256,64]{1,0:T(8,128)S(1)} %get-tuple-element.9, f32[256,64]{1,0:T(8,128)S(1)} %get-tuple-element.8), kind=kLoop, calls=%fused_computation.3 | loop fusion | flops 2097152 | bytes 3276800 | tf_op jit(solution)/shard_map/convert.4
  13.5 0.6 %pad_maximum_fusion = bf16[256,16,128]{2,1,0:T(8,128)(2,1)S(1)} fusion(bf16[256,16,64]{2,1,0:T(8,128)(2,1)S(1)} %get-tuple-element.3, bf16[256,16,64]{2,1,0:T(8,128)(2,1)S(1)} %get-tuple-element.2), kind=kLoop, calls=%fused_computation.5 | loop fusion | flops 2097152 | bytes 2097152 | tf_op jit(solution)/shard_map/concatenate | solution.py:29
  14.1 1.2 %copy.15 = bf16[32,8,16,128]{3,1,2,0:T(8,128)(2,1)} copy(bf16[32,8,16,128]{3,2,1,0:T(8,128)(2,1)S(1)} %bitcast.22) | data formatting | bytes 2097152
  15.3 0.7 %pad_add_fusion.scalars = s32[3]{0:T(128)} fusion(s32[1]{0:T(128)} %bitcast.1, s32[1]{0:T(128)} %bitcast, s32[1]{0:T(128)} %copy.16), kind=kLoop, calls=%fused_computation.16 | loop fusion | flops 6 | bytes 24 | tf_op jit(solution)/shard_map/stack | solution.py:114
  16.0 21.2 %all-to-all-done = bf16[2,1024,256]{2,0,1:T(2,128)(2,1)S(1)} async-done(((bf16[2,1024,256]{2,0,1:T(2,128)(2,1)}), bf16[2,1024,256]{2,0,1:T(2,128)(2,1)S(1)}, u32[]{:S(2)}, u32[]{:S(2)}) %all-to-all-start) | async-done | bytes 1048608 | tf_op jit(solution)/shard_map/all_to_all | solution.py:106
  37.2 0.1 copy.9.k_ref.v_ref
  37.3 0.0 copy-start
  37.3 1.2 %fusion = bf16[1,2,512,256]{3,2,1,0:T(8,128)(2,1)} fusion(s32[]{:T(128)S(6)} %select_n.3, bf16[2,1024,256]{2,1,0:T(8,128)(2,1)S(1)} %copy.9.k_ref.v_ref), kind=kLoop, calls=%fused_computation.6 | loop fusion | bytes 1572868 | tf_op jit(solution)/shard_map/broadcast_in_dim | solution.py:123
  38.5 0.0 copy-done
  38.5 11.1 %shard_map.50 = bf16[256,2048]{1,0:T(8,128)(2,1)} custom-call(s32[3]{0:T(128)} %pad_add_fusion.scalars, bf16[256,2048]{1,0:T(8,128)(2,1)} %bitcast.21, bf16[2,1024,256]{2,1,0:T(8,128)(2,1)} %copy-done, bf16[2,1024,256]{2,1,0:T(8,128)(2,1)} %copy-done), custom_call_target="tpu_custom_call" | custom-call | tf_op jit(solution)/shard_map/pallas_call | solution.py:79
  (3 shorter events, 0.0 us)
Async XLA Ops:
  3.3 8.8 %copy-start.1 = (bf16[1,256,2048]{2,1,0:T(8,128)(2,1)S(1)}, bf16[1,256,2048]{2,1,0:T(8,128)(2,1)}, u32[]{:S(2)}) copy-start(bf16[1,256,2048]{2,1,0:T(8,128)(2,1)} %param.3) | copy-start | bytes 3145732
  5.1 32.0 %all-to-all-start = ((bf16[2,1024,256]{2,0,1:T(2,128)(2,1)}), bf16[2,1024,256]{2,0,1:T(2,128)(2,1)S(1)}, u32[]{:S(2)}, u32[]{:S(2)}) async-start(bf16[2,1024,256]{2,0,1:T(2,128)(2,1)} %bitcast.3), calls=%async_computation | async-start | bytes 2097152 | tf_op jit(solution)/shard_map/all_to_all | solution.py:106
  37.3 1.2 %copy-start = (bf16[2,1024,256]{2,1,0:T(8,128)(2,1)}, bf16[2,1024,256]{2,1,0:T(8,128)(2,1)S(1)}, u32[]{:S(2)}) copy-start(bf16[2,1024,256]{2,1,0:T(8,128)(2,1)S(1)} %copy.9.k_ref.v_ref) | copy-start | bytes 3145732

commit v4 on v3

v4 whole, which is shorter than its diff:
```python
import functools
import math

import jax
import jax.numpy as jnp
from jax import lax
from jax.experimental import pallas as pl
from jax.experimental.pallas import tpu as pltpu
from jax.sharding import PartitionSpec as P

HD = 128
WINDOW = 2048


rope_base = 1000000.0
neg_floor = -1e30


def rotate(field, positions):
    half_dim = field.shape[-1] // 2
    frequency = jnp.exp(
        jnp.arange(half_dim, dtype=jnp.float32) * (-2.0 * math.log(rope_base) / field.shape[-1])
    )
    angles = positions.astype(jnp.float32)[:, None] * frequency[None, :]
    cosine = jnp.cos(angles)[:, None, :]
    sine_part = jnp.sin(angles)[:, None, :]
    lower_half = field[..., :half_dim]
    upper_half = field[..., half_dim:]
    return jnp.concatenate(
        [
            lower_half * cosine - upper_half * sine_part,
            upper_half * cosine + lower_half * sine_part,
        ],
        axis=-1,
    )


def attend_kernel(scalars, q_ref, *refs, nblk, rows, group, init, final):
    kv_refs = refs[:nblk]
    refs = refs[nblk:]
    if not init:
        m_in, l_in, acc_in = refs[:3]
        refs = refs[3:]
    if final:
        o_ref, bias_ref = refs
    else:
        m_out, l_out, acc_out, bias_ref = refs
    seq_len = scalars[0]
    first_pos = scalars[1]
    key_first = scalars[2]
    blk = kv_refs[0].shape[1]
    span = nblk * blk
    query_pos = first_pos + lax.broadcasted_iota(jnp.int32, (rows, span), 0)
    key_pos = key_first + lax.broadcasted_iota(jnp.int32, (rows, span), 1)
    allowed = (
        (key_pos <= query_pos)
        & (key_pos > query_pos - WINDOW)
        & (key_pos >= 0)
        & (key_pos < seq_len)
    )
    bias_ref[...] = jnp.where(allowed, 0.0, neg_floor)
    valid = (first_pos + lax.broadcasted_iota(jnp.int32, (rows, 1), 0)) < seq_len
    scale = 1.0 / math.sqrt(HD)
    for head in range(group):
        cols = slice(head * HD, (head + 1) * HD)
        q = q_ref[:, cols]
        raws = [
            lax.dot_general(
                q, kv_refs[b][0], (((1,), (1,)), ((), ())), preferred_element_type=jnp.float32
            )
            + bias_ref[:, b * blk:(b + 1) * blk]
            for b in range(nblk)
        ]
        top = functools.reduce(
            jnp.maximum, [jnp.max(r, axis=-1, keepdims=True) for r in raws]
        )
        if not init:
            top_old = m_in[0, :, head:head + 1]
            top = jnp.maximum(top, top_old)
        weights = [jnp.exp((r - top) * scale) for r in raws]
        totals = functools.reduce(
            jnp.add, [jnp.sum(w, axis=-1, keepdims=True) for w in weights]
        )
        numer = functools.reduce(
            jnp.add,
            [
                jnp.dot(w.astype(jnp.bfloat16), kv_refs[b][1], preferred_element_type=jnp.float32)
                for b, w in enumerate(weights)
            ],
        )
        if not init:
            rescale = jnp.exp((top_old - top) * scale)
            totals = l_in[0, :, head:head + 1] * rescale + totals
            numer = acc_in[:, cols] * rescale + numer
        if final:
            denom = jnp.where(valid, totals, 1.0)
            o_ref[:, cols] = jnp.where(valid, numer / denom, 0.0).astype(o_ref.dtype)
        else:
            m_out[0, :, head:head + 1] = top
            l_out[0, :, head:head + 1] = totals
            acc_out[:, cols] = numer


def attend(scalars, rotated_q, blocks, state, kv_heads_dev, group_size, final):
    rows = rotated_q.shape[0]
    nblk = len(blocks)
    blk = blocks[0].shape[1]
    width = group_size * HD
    init = state is None
    kernel = functools.partial(
        attend_kernel, nblk=nblk, rows=rows, group=group_size, init=init, final=final
    )
    acc_spec = pl.BlockSpec((rows, width), lambda j, s: (0, j))
    top_spec = pl.BlockSpec((1, rows, group_size), lambda j, s: (j, 0, 0))
    in_specs = [acc_spec] + [pl.BlockSpec((2, blk, HD), lambda j, s: (0, 0, j))] * nblk
    operands = [rotated_q] + list(blocks)
    if not init:
        in_specs += [top_spec, top_spec, acc_spec]
        operands += list(state)
    top_shape = jax.ShapeDtypeStruct((kv_heads_dev, rows, group_size), jnp.float32)
    if final:
        out_specs = acc_spec
        out_shape = jax.ShapeDtypeStruct((rows, kv_heads_dev * width), jnp.bfloat16)
    else:
        out_specs = [top_spec, top_spec, acc_spec]
        out_shape = [
            top_shape,
            top_shape,
            jax.ShapeDtypeStruct((rows, kv_heads_dev * width), jnp.float32),
        ]
    grid_spec = pltpu.PrefetchScalarGridSpec(
        num_scalar_prefetch=1,
        grid=(kv_heads_dev,),
        in_specs=in_specs,
        out_specs=out_specs,
        scratch_shapes=[pltpu.VMEM((rows, nblk * blk), jnp.float32)],
    )
    return pl.pallas_call(kernel, grid_spec=grid_spec, out_shape=out_shape)(
        scalars, *operands
    )


def passed_along(x, by):
    devices = lax.axis_size("seq")
    pairs = [(i, i + by) for i in range(devices) if 0 <= i + by < devices]
    return lax.ppermute(x, "seq", pairs)


def local(queries, keys_values, lengths):
    seq_len = lengths[0]
    shard_rows = queries.shape[1]
    width = keys_values.shape[-1]
    kv_heads_dev = width // HD
    heads_dev = queries.shape[-1] // HD
    group_size = heads_dev // kv_heads_dev
    seq_index = lax.axis_index("seq")
    seq_count = lax.axis_size("seq")
    tokens = seq_count * shard_rows
    first_pos = seq_index * shard_rows
    positions = first_pos + jnp.arange(shard_rows, dtype=jnp.int32)
    rotated_k = rotate(
        keys_values[0, 0].reshape(shard_rows, kv_heads_dev, HD).astype(jnp.float32), positions
    )
    own_block = jnp.stack(
        [rotated_k.astype(jnp.bfloat16).reshape(shard_rows, width), keys_values[0, 1]]
    )
    reach_count = min(WINDOW // shard_rows, seq_count - 1)
    slot_rows = WINDOW // seq_count
    if WINDOW >= tokens:
        older = []
        moving = own_block
        for hop in range(reach_count):
            moving = passed_along(moving, 1)
            older.append(moving)
        tail = jnp.concatenate(older[::-1] + [own_block], axis=1)
        tail_first = first_pos - reach_count * shard_rows
    else:
        outbox = jnp.broadcast_to(own_block[:, None], (2, seq_count, shard_rows, width))
        tail = lax.all_to_all(
            outbox.reshape(2, tokens, width), "seq", 1, 1, tiled=True
        )
        tail_first = 0
        older = [
            lax.dynamic_slice_in_dim(
                tail, jnp.maximum(seq_index - hop - 1, 0) * shard_rows, shard_rows, 1
            )
            for hop in range(reach_count)
        ]
    rotated_q = rotate(queries[0].reshape(shard_rows, heads_dev, HD).astype(jnp.float32), positions)
    rotated_q = rotated_q.astype(jnp.bfloat16).reshape(shard_rows, heads_dev * HD)

    def scalars_for(first_key):
        return jnp.stack([seq_len, first_pos, first_key]).astype(jnp.int32)

    near = [older[0], own_block] if reach_count >= 1 else [own_block]
    far = older[1:][::-1]
    near_first = first_pos - (len(near) - 1) * shard_rows
    if far:
        state = attend(scalars_for(near_first), rotated_q, near, None, kv_heads_dev, group_size, False)
        far_first = first_pos - reach_count * shard_rows
        attended = attend(
            scalars_for(far_first), rotated_q, far, state, kv_heads_dev, group_size, True
        )
    else:
        attended = attend(scalars_for(near_first), rotated_q, near, None, kv_heads_dev, group_size, True)
    attended = attended.reshape(1, shard_rows, heads_dev * HD)

    padded = jnp.concatenate([jnp.zeros((2, WINDOW, width), jnp.bfloat16), tail], axis=1)
    begin_row = seq_len - tail_first + seq_index * slot_rows
    window_cache = lax.dynamic_slice_in_dim(padded, begin_row, slot_rows, 1)
    return (attended, window_cache[None])


def solution(mesh):
    return jax.shard_map(
        local,
        mesh=mesh,
        in_specs=(
            P("section", ("parts", "seq"), "tp"),
            P("section", None, ("parts", "seq"), "tp"),
            P("parts"),
        ),
        out_specs=(
            P("section", ("parts", "seq"), "tp"),
            P("section", None, ("parts", "seq"), "tp"),
        ),
        check_vma=False,
    )
```

time: 49.9 us -> 51.2 us (1.026)
  waiting for transfers between devices: 21.2 us -> 4.33 us
  starting transfers between devices: 6.32 us -> 15.2 us
  Pallas kernels: 11.1 us -> 18.7 us
  local copies, waits for them, and re-layouts: 4.99 us -> 5.86 us
  other arithmetic: 4.64 us -> 5.33 us
    all_to_all x1 -> x0, waiting for transfers between devices: 21.2 us -> none  [local(): lax.all_to_all(outbox.reshape(2, seq_count * shard_rows, width), 'seq', 1...]
    ppermute x0 -> x3, starting transfers between devices: none -> 15.2 us  [passed_along(): return lax.ppermute(x, 'seq', pairs)]
    pallas_call x1 -> x2, Pallas kernels: 11.1 us -> 18.7 us  [attend(): pl.pallas_call(kernel, grid_spec=grid_spec, out_shape=out_shape)]
    all_to_all x1 -> x0, starting transfers between devices: 6.32 us -> none  [local(): lax.all_to_all(outbox.reshape(2, seq_count * shard_rows, width), 'seq', 1...]
    ppermute x0 -> x3, waiting for transfers between devices: none -> 4.33 us  [passed_along(): return lax.ppermute(x, 'seq', pairs)]
    unnamed x6 -> x12, local copies, waits for them, and re-layouts: 1.63 us -> 4.71 us
    broadcast_in_dim x1 -> x0, local copies, waits for them, and re-layouts: 1.51 us -> none  [local(): jnp.broadcast_to(own_block[:, None], (2, seq_count, shard_rows, width))]
    another operation x3 -> x4, other arithmetic: 1.89 us -> 2.49 us  [the longest x2 1.24 us: scalars_for(): return jnp.stack([seq_len, first_pos, first_key]).astype(jnp.int32)]
  transfers between devices with their start and end apart: 1 -> 3, of which waited for: 1 -> 2; matrix products, arithmetic and copies ran while one was open for 8% -> 9% of each run, Pallas kernels for 0% -> 16%
where the time goes in v4:
time: 51.2 us; the launch traced here: 50.9 us
  Pallas kernels  18.7 us (37%)
  starting transfers between devices  15.2 us (30%)
  local copies, waits for them, and re-layouts  5.86 us (11%)
  other arithmetic  5.33 us (10%)
  waiting for transfers between devices  4.33 us (8%)
  between operations  1.45 us (3%)
    pallas_call x2, Pallas kernels, attend(): pl.pallas_call(kernel, grid_spec=grid_spec, out_shape=out_shape)  18.7 us
    ppermute x3, starting transfers between devices, passed_along(): return lax.ppermute(x, 'seq', pairs)  15.2 us
    unnamed x12, local copies, waits for them, and re-layouts  4.71 us
    ppermute x3, waiting for transfers between devices, passed_along(): return lax.ppermute(x, 'seq', pairs)  4.33 us
    another operation x2, other arithmetic, scalars_for(): return jnp.stack([seq_len, first_pos, first_key]).astype(jnp.int32)  1.24 us
    another operation x2, other arithmetic  1.24 us
    convert_element_type x1, other arithmetic, local(): keys_values[0, 0].reshape(shard_rows, kv_heads_dev, HD).astype(jnp.float32)  1.08 us
  transfers between devices with their start and end apart: 3, of which 2 were waited for; matrix products, arithmetic and copies ran while one was open for 9% of the time, Pallas kernels for 16%

profile of v4, /device:TPU:0, one launch (start us, length us, event | category | flops | bytes accessed | tf_op | source)
XLA Modules:
  0.0 50.9 jit_solution(1627466865217868996)
XLA Ops:
  0.6 0.0 copy-start
  0.7 1.1 %slice_convert_fusion = (f32[1,1,256,256]{3,2,1,0:T(8,128)S(1)}, bf16[1,256,256]{2,1,0:T(8,128)(2,1)S(1)}) fusion(bf16[1,2,256,256]{3,2,1,0:T(8,128)(2,1)} %param.4), kind=kLoop, calls=%fused_computation.14 | loop fusion | flops 65536 | bytes 655360 | tf_op jit(solution)/shard_map/convert_element_type | solution.py:162
  1.8 0.1 reshape.84
  1.9 0.5 %multiply_cosine_fusion = (f32[256,64]{1,0:T(8,128)S(1)}, f32[256,64]{1,0:T(8,128)S(1)}) fusion(f32[64]{0:T(128)S(1)} %multiply_exponential_fusion, f32[256]{0:T(256)S(1)} %add_convert_fusion.2), kind=kLoop, calls=%fused_computation.11 | loop fusion | flops 16384 | bytes 132352 | tf_op jit(solution)/shard_map/cos | solution.py:25
  2.4 0.5 subtract_convert_fusion.1
  2.9 0.4 pad_maximum_fusion.2
  3.3 0.1 convert_element_type.42
  3.4 0.0 copy-start.2
  3.4 4.9 %collective-permute-start = (bf16[2,256,256]{2,1,0:T(8,128)(2,1)S(1)}, bf16[2,256,256]{2,1,0:T(8,128)(2,1)S(1)}, u32[]{:S(2)}, u32[]{:S(2)}) collective-permute-start(bf16[2,256,256]{2,1,0:T(8,128)(2,1)S(1)} %pad_maximum_fusion.1.refs_1_), channel_id=1, source_target_pairs={{0,4},{4,8},{8,12},{1,5},{5,9},{9,13},{2,6},{6,10},{10,14},{3,7},{... | collective-permute-start | bytes 786440 | tf_op jit(solution)/shard_map/ppermute | solution.py:146
  8.4 0.0 copy-done
  8.4 0.2 convert_bitcast_fusion
  8.6 0.4 copy.5
  9.0 0.0 copy-done.2
  9.0 0.8 %subtract_convert_fusion = (bf16[256,16,64]{2,1,0:T(8,128)(2,1)S(1)}, bf16[256,16,64]{2,1,0:T(8,128)(2,1)S(1)}) fusion(f32[256,16,128]{2,1,0:T(8,128)S(1)} %bitcast.20, f32[256,64]{1,0:T(8,128)S(1)} %get-tuple-element.15, f32[256,64]{1,0:T(8,128)S(1)} %get-tuple-element.14), kind=kLoop, calls=%fused_computation.2 | loop fusion | flops 2097152 | bytes 3276800 | tf_op jit(solution)/shard_map/convert.4
  9.8 4.1 %collective-permute-done.refs_0_ = bf16[2,256,256]{2,1,0:T(8,128)(2,1)S(1)} collective-permute-done((bf16[2,256,256]{2,1,0:T(8,128)(2,1)S(1)}, bf16[2,256,256]{2,1,0:T(8,128)(2,1)S(1)}, u32[]{:S(2)}, u32[]{:S(2)}) %collective-permute-start) | collective-permute-done | bytes 262176 | tf_op jit(solution)/shard_map/ppermute | solution.py:146
  13.9 0.0 copy-start.1
  13.9 5.1 %collective-permute-start.1 = (bf16[2,256,256]{2,1,0:T(8,128)(2,1)S(1)}, bf16[2,256,256]{2,1,0:T(8,128)(2,1)}, u32[]{:S(2)}, u32[]{:S(2)}) collective-permute-start(bf16[2,256,256]{2,1,0:T(8,128)(2,1)S(1)} %collective-permute-done.refs_0_), channel_id=1, source_target_pairs={{0,4},{4,8},{8,12},{1,5},{5,9},{9,13},{2,6},{6,10},{10,14},{3,7},{... | collective-permute-start | bytes 786440 | tf_op jit(solution)/shard_map/ppermute | solution.py:146
  19.0 0.6 %pad_maximum_fusion = bf16[256,16,128]{2,1,0:T(8,128)(2,1)S(1)} fusion(bf16[256,16,64]{2,1,0:T(8,128)(2,1)S(1)} %get-tuple-element.9, bf16[256,16,64]{2,1,0:T(8,128)(2,1)S(1)} %get-tuple-element.8), kind=kLoop, calls=%fused_computation.4 | loop fusion | flops 2097152 | bytes 2097152 | tf_op jit(solution)/shard_map/concatenate | solution.py:29
  20.2 1.3 %copy.8 = bf16[32,8,16,128]{3,1,2,0:T(8,128)(2,1)} copy(bf16[32,8,16,128]{3,2,1,0:T(8,128)(2,1)S(1)} %bitcast.23) | data formatting | bytes 2097152
  21.5 0.0 copy-done.1
  21.5 0.6 %pad_add_fusion.2.scalars = s32[3]{0:T(128)} fusion(s32[1]{0:T(128)} %bitcast.3, s32[1]{0:T(128)} %bitcast, s32[1]{0:T(128)} %copy.13), kind=kLoop, calls=%fused_computation.22 | loop fusion | flops 6 | bytes 24 | tf_op jit(solution)/shard_map/stack | solution.py:193
  22.1 0.7 %pad_add_fusion.scalars = s32[3]{0:T(128)} fusion(s32[1]{0:T(128)} %bitcast.1, s32[1]{0:T(128)} %bitcast, s32[1]{0:T(128)} %copy.13), kind=kLoop, calls=%fused_computation.20 | loop fusion | flops 6 | bytes 24 | tf_op jit(solution)/shard_map/stack | solution.py:193
  22.7 0.2 collective-permute-done.1.refs_1_
  23.0 5.2 %collective-permute-start.2 = (bf16[2,256,256]{2,1,0:T(8,128)(2,1)}, bf16[2,256,256]{2,1,0:T(8,128)(2,1)}, u32[]{:S(2)}, u32[]{:S(2)}) collective-permute-start(bf16[2,256,256]{2,1,0:T(8,128)(2,1)} %collective-permute-done.1.refs_1_), channel_id=1, source_target_pairs={{0,4},{4,8},{8,12},{1,5},{5,9},{9,13},{2,6},{6,10},{10,14},{3,7},{... | collective-permute-start | bytes 786440 | tf_op jit(solution)/shard_map/ppermute | solution.py:146
  28.2 0.1 broadcast_dynamic-update-slice_fusion
  28.3 8.3 %shard_map.50 = (f32[2,256,8]{2,1,0:T(8,128)}, f32[2,256,8]{2,1,0:T(8,128)}, f32[256,2048]{1,0:T(8,128)}) custom-call(s32[3]{0:T(128)} %pad_add_fusion.2.scalars, bf16[256,2048]{1,0:T(8,128)(2,1)} %bitcast.21, bf16[2,256,256]{2,1,0:T(8,128)(2,1)} %copy-done.1, bf16[2,256,256]{2,1,0:T(8,128)(2,1)} %copy-done.2), custom_call_target="tpu_custom_call" | custom-call | tf_op jit(solution)/shard_map/pallas_call | solution.py:138
  36.6 0.0 collective-permute-done.2.refs_0_
  36.6 1.0 %constant_dynamic-update-slice_fusion.3 = bf16[2,3072,256]{2,1,0:T(8,128)(2,1)S(1)} fusion(bf16[2,3072,256]{2,1,0:T(8,128)(2,1)S(1)} %broadcast_dynamic-update-slice_fusion, bf16[2,256,256]{2,1,0:T(8,128)(2,1)} %collective-permute-done.2.refs_0_), kind=kLoop, calls=%fused_computation.18 | loop fusion | bytes 524288
  37.5 1.0 %constant_dynamic-update-slice_fusion.2 = bf16[2,3072,256]{2,1,0:T(8,128)(2,1)S(1)} fusion(bf16[2,3072,256]{2,1,0:T(8,128)(2,1)S(1)} %constant_dynamic-update-slice_fusion.3, bf16[2,256,256]{2,1,0:T(8,128)(2,1)} %collective-permute-done.1.refs_1_), kind=kLoop, calls=%fused_computation.17 | loop fusion | bytes 524288
  38.5 1.0 %constant_dynamic-update-slice_fusion.1 = bf16[2,3072,256]{2,1,0:T(8,128)(2,1)S(1)} fusion(bf16[2,3072,256]{2,1,0:T(8,128)(2,1)S(1)} %constant_dynamic-update-slice_fusion.2, bf16[2,256,256]{2,1,0:T(8,128)(2,1)} %copy-done.1), kind=kLoop, calls=%fused_computation.16 | loop fusion | bytes 524288
  39.5 0.9 %dynamic-slice_bitcast_fusion = bf16[1,2,512,256]{3,2,1,0:T(8,128)(2,1)} fusion(bf16[2,3072,256]{2,1,0:T(8,128)(2,1)S(1)} %constant_dynamic-update-slice_fusion, s32[]{:T(128)S(6)} %select_n.3), kind=kLoop, calls=%fused_computation.6 | loop fusion | bytes 1048580 | tf_op jit(solution)/shard_map/broadcast_in_dim | solution.py:211
  40.4 10.5 %shard_map.51 = bf16[256,2048]{1,0:T(8,128)(2,1)} custom-call(s32[3]{0:T(128)} %pad_add_fusion.scalars, bf16[256,2048]{1,0:T(8,128)(2,1)} %bitcast.22, bf16[2,256,256]{2,1,0:T(8,128)(2,1)} %collective-permute-done.2.refs_0_, bf16[2,256,256]{2,1,0:T(8,128)(2,1)} %collective-permute-done.1.refs_1_, f32[2,256,8]{2,1,0:T(8,128)} %get-tuple-element.5.refs_2_, ...), custom_call_target="tpu_custom_call" | custom-call | tf_op jit(solution)/shard_map/pallas_call | solution.py:138
  (4 shorter events, 0.1 us)
Async XLA Ops:
  0.6 7.8 %copy-start = (bf16[1,256,2048]{2,1,0:T(8,128)(2,1)S(1)}, bf16[1,256,2048]{2,1,0:T(8,128)(2,1)}, u32[]{:S(2)}) copy-start(bf16[1,256,2048]{2,1,0:T(8,128)(2,1)} %param.3) | copy-start | bytes 3145732
  3.4 5.6 %copy-start.2 = (bf16[2,256,256]{2,1,0:T(8,128)(2,1)}, bf16[2,256,256]{2,1,0:T(8,128)(2,1)S(1)}, u32[]{:S(2)}) copy-start(bf16[2,256,256]{2,1,0:T(8,128)(2,1)S(1)} %pad_maximum_fusion.1.refs_1_) | copy-start | bytes 786436
  3.4 10.5 %collective-permute-start = (bf16[2,256,256]{2,1,0:T(8,128)(2,1)S(1)}, bf16[2,256,256]{2,1,0:T(8,128)(2,1)S(1)}, u32[]{:S(2)}, u32[]{:S(2)}) collective-permute-start(bf16[2,256,256]{2,1,0:T(8,128)(2,1)S(1)} %pad_maximum_fusion.1.refs_1_), channel_id=1, source_target_pairs={{0,4},{4,8},{8,12},{1,5},{5,9},{9,13},{2,6},{6,10},{10,14},{3,7},{... | collective-permute-start | bytes 786440 | tf_op jit(solution)/shard_map/ppermute | solution.py:146
  13.9 7.6 %copy-start.1 = (bf16[2,256,256]{2,1,0:T(8,128)(2,1)}, bf16[2,256,256]{2,1,0:T(8,128)(2,1)S(1)}, u32[]{:S(2)}) copy-start(bf16[2,256,256]{2,1,0:T(8,128)(2,1)S(1)} %collective-permute-done.refs_0_) | copy-start | bytes 786436
  13.9 9.1 %collective-permute-start.1 = (bf16[2,256,256]{2,1,0:T(8,128)(2,1)S(1)}, bf16[2,256,256]{2,1,0:T(8,128)(2,1)}, u32[]{:S(2)}, u32[]{:S(2)}) collective-permute-start(bf16[2,256,256]{2,1,0:T(8,128)(2,1)S(1)} %collective-permute-done.refs_0_), channel_id=1, source_target_pairs={{0,4},{4,8},{8,12},{1,5},{5,9},{9,13},{2,6},{6,10},{10,14},{3,7},{... | collective-permute-start | bytes 786440 | tf_op jit(solution)/shard_map/ppermute | solution.py:146
  23.0 13.6 %collective-permute-start.2 = (bf16[2,256,256]{2,1,0:T(8,128)(2,1)}, bf16[2,256,256]{2,1,0:T(8,128)(2,1)}, u32[]{:S(2)}, u32[]{:S(2)}) collective-permute-start(bf16[2,256,256]{2,1,0:T(8,128)(2,1)} %collective-permute-done.1.refs_1_), channel_id=1, source_target_pairs={{0,4},{4,8},{8,12},{1,5},{5,9},{9,13},{2,6},{6,10},{10,14},{3,7},{... | collective-permute-start | bytes 786440 | tf_op jit(solution)/shard_map/ppermute | solution.py:146

commit v5 on v3

--- a/solution.py
+++ b/solution.py
@@ -35,7 +35,8 @@
     )
 
 
-def attend_kernel(scalars, q_ref, k_ref, v_ref, o_ref, bias_ref, *, rows, span, group):
+def attend_kernel(scalars, q_ref, k_ref, v_ref, o_ref, bias_ref, raw_ref, w_ref, tot_ref,
+                  *, rows, span, group, chunk):
     seq_len = scalars[0]
     first_pos = scalars[1]
     key_start = pl.multiple_of(scalars[2], 256)
@@ -47,23 +48,34 @@
     v = v_ref[0, pl.ds(key_start, span), :]
     valid = (first_pos + lax.broadcasted_iota(jnp.int32, (rows, 1), 0)) < seq_len
     scale = 1.0 / math.sqrt(HD)
+
+    def softmax_rows(c, carry):
+        r0 = pl.multiple_of(c * chunk, chunk)
+        x = raw_ref[pl.ds(r0, chunk), :] + bias_ref[pl.ds(r0, chunk), :]
+        top = jnp.max(x, axis=-1, keepdims=True)
+        weights = jnp.exp((x - top) * scale)
+        tot_ref[pl.ds(r0, chunk), :] = jnp.sum(weights, axis=-1, keepdims=True)
+        w_ref[pl.ds(r0, chunk), :] = weights.astype(jnp.bfloat16)
+        return carry
+
     for head in range(group):
         cols = slice(head * HD, (head + 1) * HD)
-        raw = lax.dot_general(
+        raw_ref[...] = lax.dot_general(
             q_ref[:, cols], k, (((1,), (1,)), ((), ())), preferred_element_type=jnp.float32
-        ) + bias_ref[...]
-        row_top = jnp.max(raw, axis=-1, keepdims=True)
-        weights = jnp.exp((raw - row_top) * scale)
-        totals = jnp.sum(weights, axis=-1, keepdims=True)
-        numer = jnp.dot(weights.astype(jnp.bfloat16), v, preferred_element_type=jnp.float32)
-        denom = jnp.where(valid, totals, 1.0)
+        )
+        lax.fori_loop(0, rows // chunk, softmax_rows, 0)
+        numer = jnp.dot(w_ref[...], v, preferred_element_type=jnp.float32)
+        denom = jnp.where(valid, tot_ref[...], 1.0)
         o_ref[:, cols] = jnp.where(valid, numer / denom, 0.0).astype(o_ref.dtype)
 
 
 def attention(scalars, rotated_q, gathered, kv_heads_dev, group_size, span):
     rows = rotated_q.shape[0]
     tokens = gathered.shape[1]
-    kernel = functools.partial(attend_kernel, rows=rows, span=span, group=group_size)
+    chunk = 32 if span <= 1024 else 16
+    kernel = functools.partial(
+        attend_kernel, rows=rows, span=span, group=group_size, chunk=chunk
+    )
     width = group_size * HD
     grid_spec = pltpu.PrefetchScalarGridSpec(
         num_scalar_prefetch=1,
@@ -74,7 +86,12 @@
             pl.BlockSpec((1, tokens, HD), lambda j, s: (1, 0, j)),
         ],
         out_specs=pl.BlockSpec((rows, width), lambda j, s: (0, j)),
-        scratch_shapes=[pltpu.VMEM((rows, span), jnp.float32)],
+        scratch_shapes=[
+            pltpu.VMEM((rows, span), jnp.float32),
+            pltpu.VMEM((rows, span), jnp.float32),
+            pltpu.VMEM((rows, span), jnp.bfloat16),
+            pltpu.VMEM((rows, 1), jnp.float32),
+        ],
     )
     return pl.pallas_call(
         kernel,

time: 49.9 us -> 72.9 us (1.46)
  Pallas kernels: 11.1 us -> 34.1 us
    pallas_call x1, Pallas kernels: 11.1 us -> 34.1 us  [attention(): pl.pallas_call(kernel, grid_spec=grid_spec, out_shape=jax.ShapeDtypeStruc...]
  transfers between devices with their start and end apart: 1 -> 1, of which waited for: 1 -> 1; matrix products, arithmetic and copies ran while one was open for 8% -> 5% of each run, Pallas kernels for 0% -> 0%
where the time goes in v5:
time: 72.9 us; the launch traced here: 72.6 us
  Pallas kernels  34.1 us (47%)
  waiting for transfers between devices  21.2 us (29%)
  starting transfers between devices  6.32 us (9%)
  local copies, waits for them, and re-layouts  4.99 us (7%)
  other arithmetic  4.64 us (6%)
  between operations  1.42 us (2%)
    pallas_call x1, Pallas kernels, attention(): pl.pallas_call(kernel, grid_spec=grid_spec, out_shape=jax.ShapeDtypeStruc...  34.1 us
    all_to_all x1, waiting for transfers between devices, local(): lax.all_to_all(outbox.reshape(2, seq_count * shard_rows, width), 'seq', 1...  21.2 us
    all_to_all x1, starting transfers between devices, local(): lax.all_to_all(outbox.reshape(2, seq_count * shard_rows, width), 'seq', 1...  6.32 us
    unnamed x6, local copies, waits for them, and re-layouts  1.63 us
    broadcast_in_dim x1, local copies, waits for them, and re-layouts, local(): jnp.broadcast_to(own_block[:, None], (2, seq_count, shard_rows, width))  1.51 us
  transfers between devices with their start and end apart: 1, of which 1 were waited for; matrix products, arithmetic and copies ran while one was open for 5% of the time, Pallas kernels for 0%

profile of v5, /device:TPU:0, one launch (start us, length us, event | category | flops | bytes accessed | tf_op | source)
XLA Modules:
  0.0 72.6 jit_solution(13084817931287599229)
XLA Ops:
  0.7 1.0 %slice_convert_fusion = (f32[1,1,256,256]{3,2,1,0:T(8,128)S(1)}, bf16[1,256,256]{2,1,0:T(8,128)(2,1)S(1)}) fusion(bf16[1,2,256,256]{3,2,1,0:T(8,128)(2,1)} %param.4), kind=kLoop, calls=%fused_computation.14 | loop fusion | flops 65536 | bytes 655360 | tf_op jit(solution)/shard_map/convert_element_type | solution.py:117
  1.7 0.1 reshape.89
  1.8 0.5 multiply_cosine_fusion
  2.3 0.5 subtract_convert_fusion.1
  2.8 0.4 pad_maximum_fusion.2
  3.2 0.1 convert_element_type.42
  3.3 0.0 copy-start.1
  3.3 0.3 copy.8
  3.6 1.5 %broadcast_in_dim.4 = bf16[2,4,256,256]{3,0,2,1:T(2,128)(2,1)} broadcast(bf16[2,256,256]{2,0,1:T(2,128)(2,1)S(1)} %copy.8), dimensions={0,2,3} | broadcast | bytes 1310720 | tf_op jit(solution)/shard_map/broadcast_in_dim | solution.py:122
  5.1 6.3 %all-to-all-start = ((bf16[2,1024,256]{2,0,1:T(2,128)(2,1)}), bf16[2,1024,256]{2,0,1:T(2,128)(2,1)S(1)}, u32[]{:S(2)}, u32[]{:S(2)}) async-start(bf16[2,1024,256]{2,0,1:T(2,128)(2,1)} %bitcast.3), calls=%async_computation | async-start | bytes 2097152 | tf_op jit(solution)/shard_map/all_to_all | solution.py:123
  12.1 0.0 copy-done.1
  12.1 0.2 convert_bitcast_fusion
  12.4 0.4 copy.12
  12.7 0.8 %subtract_convert_fusion = (bf16[256,16,64]{2,1,0:T(8,128)(2,1)S(1)}, bf16[256,16,64]{2,1,0:T(8,128)(2,1)S(1)}) fusion(f32[256,16,128]{2,1,0:T(8,128)S(1)} %bitcast.20, f32[256,64]{1,0:T(8,128)S(1)} %get-tuple-element.9, f32[256,64]{1,0:T(8,128)S(1)} %get-tuple-element.8), kind=kLoop, calls=%fused_computation.3 | loop fusion | flops 2097152 | bytes 3276800 | tf_op jit(solution)/shard_map/convert.4
  13.5 0.6 pad_maximum_fusion
  14.1 1.2 %copy.15 = bf16[32,8,16,128]{3,1,2,0:T(8,128)(2,1)} copy(bf16[32,8,16,128]{3,2,1,0:T(8,128)(2,1)S(1)} %bitcast.22) | data formatting | bytes 2097152
  15.3 0.7 pad_add_fusion.scalars
  16.0 21.2 %all-to-all-done = bf16[2,1024,256]{2,0,1:T(2,128)(2,1)S(1)} async-done(((bf16[2,1024,256]{2,0,1:T(2,128)(2,1)}), bf16[2,1024,256]{2,0,1:T(2,128)(2,1)S(1)}, u32[]{:S(2)}, u32[]{:S(2)}) %all-to-all-start) | async-done | bytes 1048608 | tf_op jit(solution)/shard_map/all_to_all | solution.py:123
  37.2 0.1 copy.9.k_ref.v_ref
  37.3 0.0 copy-start
  37.3 1.2 %fusion = bf16[1,2,512,256]{3,2,1,0:T(8,128)(2,1)} fusion(s32[]{:T(128)S(6)} %select_n.3, bf16[2,1024,256]{2,1,0:T(8,128)(2,1)S(1)} %copy.9.k_ref.v_ref), kind=kLoop, calls=%fused_computation.6 | loop fusion | bytes 1572868 | tf_op jit(solution)/shard_map/broadcast_in_dim | solution.py:140
  38.5 0.0 copy-done
  38.5 34.1 %shard_map.50 = bf16[256,2048]{1,0:T(8,128)(2,1)} custom-call(s32[3]{0:T(128)} %pad_add_fusion.scalars, bf16[256,2048]{1,0:T(8,128)(2,1)} %bitcast.21, bf16[2,1024,256]{2,1,0:T(8,128)(2,1)} %copy-done, bf16[2,1024,256]{2,1,0:T(8,128)(2,1)} %copy-done), custom_call_target="tpu_custom_call" | custom-call | tf_op jit(solution)/shard_map/pallas_call | solution.py:96
  (3 shorter events, 0.0 us)
Async XLA Ops:
  3.3 8.8 %copy-start.1 = (bf16[1,256,2048]{2,1,0:T(8,128)(2,1)S(1)}, bf16[1,256,2048]{2,1,0:T(8,128)(2,1)}, u32[]{:S(2)}) copy-start(bf16[1,256,2048]{2,1,0:T(8,128)(2,1)} %param.3) | copy-start | bytes 3145732
  5.1 32.0 %all-to-all-start = ((bf16[2,1024,256]{2,0,1:T(2,128)(2,1)}), bf16[2,1024,256]{2,0,1:T(2,128)(2,1)S(1)}, u32[]{:S(2)}, u32[]{:S(2)}) async-start(bf16[2,1024,256]{2,0,1:T(2,128)(2,1)} %bitcast.3), calls=%async_computation | async-start | bytes 2097152 | tf_op jit(solution)/shard_map/all_to_all | solution.py:123
  37.3 1.2 %copy-start = (bf16[2,1024,256]{2,1,0:T(8,128)(2,1)}, bf16[2,1024,256]{2,1,0:T(8,128)(2,1)S(1)}, u32[]{:S(2)}) copy-start(bf16[2,1024,256]{2,1,0:T(8,128)(2,1)S(1)} %copy.9.k_ref.v_ref) | copy-start | bytes 3145732

commit v6 on v4

--- a/solution.py
+++ b/solution.py
@@ -172,8 +172,16 @@
         for hop in range(reach_count):
             moving = passed_along(moving, 1)
             older.append(moving)
-        tail = jnp.concatenate(older[::-1] + [own_block], axis=1)
-        tail_first = first_pos - reach_count * shard_rows
+        shortest = min(WINDOW, tokens - shard_rows) + 1
+        cache_hops = 0
+        for index in range(seq_count):
+            if tokens - WINDOW + (index + 1) * slot_rows - 1 < 0:
+                continue
+            lowest = max(0, (shortest - WINDOW + index * slot_rows) // shard_rows)
+            cache_hops = max(cache_hops, index - lowest)
+        cache_hops = min(cache_hops, reach_count)
+        tail = jnp.concatenate(older[:cache_hops][::-1] + [own_block], axis=1)
+        tail_first = first_pos - cache_hops * shard_rows
     else:
         outbox = jnp.broadcast_to(own_block[:, None], (2, seq_count, shard_rows, width))
         tail = lax.all_to_all(
@@ -192,18 +200,21 @@
     def scalars_for(first_key):
         return jnp.stack([seq_len, first_pos, first_key]).astype(jnp.int32)
 
-    near = [older[0], own_block] if reach_count >= 1 else [own_block]
-    far = older[1:][::-1]
-    near_first = first_pos - (len(near) - 1) * shard_rows
-    if far:
-        state = attend(scalars_for(near_first), rotated_q, near, None, kv_heads_dev, group_size, False)
-        far_first = first_pos - reach_count * shard_rows
-        attended = attend(
-            scalars_for(far_first), rotated_q, far, state, kv_heads_dev, group_size, True
-        )
-    else:
-        attended = attend(scalars_for(near_first), rotated_q, near, None, kv_heads_dev, group_size, True)
-    attended = attended.reshape(1, shard_rows, heads_dev * HD)
+    stages = [[own_block]]
+    if reach_count >= 2:
+        stages.append(older[:reach_count - 1][::-1])
+    if reach_count >= 1:
+        stages.append([older[-1]])
+    state = None
+    for number, stage in enumerate(stages):
+        final = number == len(stages) - 1
+        first_key = first_pos - shard_rows * (
+            0 if number == 0 else (reach_count - 1 if not final else reach_count)
+        )
+        state = attend(
+            scalars_for(first_key), rotated_q, stage, state, kv_heads_dev, group_size, final
+        )
+    attended = state.reshape(1, shard_rows, heads_dev * HD)
 
     padded = jnp.concatenate([jnp.zeros((2, WINDOW, width), jnp.bfloat16), tail], axis=1)
     begin_row = seq_len - tail_first + seq_index * slot_rows

time: 51.2 us -> 60.4 us (1.18)
  the two profiles are of different devices: /device:TPU:0 before, /device:TPU:20 now
where the time goes in v6:
time: 60.4 us; the launch traced here: 59.6 us
  Pallas kernels  27.3 us (45%)
  other arithmetic  11.3 us (19%)
  starting transfers between devices  10.6 us (18%)
  waiting for transfers between devices  6.4 us (11%)
  local copies, waits for them, and re-layouts  2.66 us (4%)
  between operations  1.43 us (2%)
    pallas_call x3, Pallas kernels, attend(): pl.pallas_call(kernel, grid_spec=grid_spec, out_shape=out_shape)  27.3 us
    ppermute x3, starting transfers between devices, passed_along(): return lax.ppermute(x, 'seq', pairs)  10.6 us
    ppermute x3, waiting for transfers between devices, passed_along(): return lax.ppermute(x, 'seq', pairs)  6.4 us
    broadcast_in_dim x1, other arithmetic, local(): return (attended, window_cache[None])  2.43 us
    unnamed x12, local copies, waits for them, and re-layouts  2.35 us
    another operation x2, other arithmetic  2.21 us
    concatenate x2, other arithmetic, rotate(): jnp.concatenate([lower_half * cosine - upper_half * sine_part, upper_half...  2.16 us
    another operation x3, other arithmetic, scalars_for(): return jnp.stack([seq_len, first_pos, first_key]).astype(jnp.int32)  1.87 us
  transfers between devices with their start and end apart: 3, of which 2 were waited for; matrix products, arithmetic and copies ran while one was open for 16% of the time, Pallas kernels for 26%

profile of v6, /device:TPU:20, one launch (start us, length us, event | category | flops | bytes accessed | tf_op | source)
XLA Modules:
  0.0 59.6 jit_solution(2515063257093007114)
XLA Ops:
  0.6 0.0 copy-start.2
  0.7 1.1 %slice_convert_fusion = (f32[1,1,256,256]{3,2,1,0:T(8,128)S(1)}, bf16[1,256,256]{2,1,0:T(8,128)(2,1)S(1)}) fusion(bf16[1,2,256,256]{3,2,1,0:T(8,128)(2,1)} %param.4), kind=kLoop, calls=%fused_computation.21 | loop fusion | flops 65536 | bytes 655360 | tf_op jit(solution)/shard_map/convert_element_type | solution.py:162
  1.8 0.1 reshape.84
  1.9 0.5 multiply_cosine_fusion
  2.4 0.5 subtract_convert_fusion.1
  2.9 0.4 pad_maximum_fusion.2
  3.3 0.1 convert_element_type.42
  3.4 0.0 copy-start
  3.4 0.7 %pad_maximum_fusion.1.refs_0_ = bf16[2,256,256]{2,1,0:T(8,128)(2,1)} fusion(bf16[1,256,256]{2,1,0:T(8,128)(2,1)S(1)} %get-tuple-element.19, bf16[1,256,256]{2,1,0:T(8,128)(2,1)S(1)} %convert_element_type.42), kind=kLoop, calls=%fused_computation.14 | loop fusion | flops 131072 | bytes 524288 | tf_op jit(solution)/shard_map/stack | solution.py:164
  4.1 3.5 %collective-permute-start = (bf16[2,256,256]{2,1,0:T(8,128)(2,1)}, bf16[2,256,256]{2,1,0:T(8,128)(2,1)}, u32[]{:S(2)}, u32[]{:S(2)}) collective-permute-start(bf16[2,256,256]{2,1,0:T(8,128)(2,1)} %pad_maximum_fusion.1.refs_0_), channel_id=1, source_target_pairs={{0,4},{4,8},{8,12},{1,5},{5,9},{9,13},{2,6},{6,10},{10,14},{3,7},{... | collective-permute-start | bytes 786440 | tf_op jit(solution)/shard_map/ppermute | solution.py:146
  7.6 0.0 copy-done.2
  7.6 0.2 convert_bitcast_fusion
  7.9 0.4 copy.5
  8.3 0.0 copy-done
  8.9 0.6 pad_add_fusion.3.scalars
  9.5 1.7 %subtract_convert_fusion = (bf16[256,16,64]{2,1,0:T(8,128)(2,1)S(1)}, bf16[256,16,64]{2,1,0:T(8,128)(2,1)}) fusion(f32[256,16,128]{2,1,0:T(8,128)S(1)} %bitcast.20, f32[256,64]{1,0:T(8,128)S(1)} %get-tuple-element.21, f32[256,64]{1,0:T(8,128)S(1)} %get-tuple-element.20), kind=kLoop, calls=%fused_computation.6 | loop fusion | flops 2097152 | bytes 3276800 | tf_op jit(solution)/shard_map/convert.4
  11.3 3.1 %collective-permute-done.refs_1_ = bf16[2,256,256]{2,1,0:T(8,128)(2,1)} collective-permute-done((bf16[2,256,256]{2,1,0:T(8,128)(2,1)}, bf16[2,256,256]{2,1,0:T(8,128)(2,1)}, u32[]{:S(2)}, u32[]{:S(2)}) %collective-permute-start) | collective-permute-done | bytes 262176 | tf_op jit(solution)/shard_map/ppermute | solution.py:146
  14.4 3.5 %collective-permute-start.1 = (bf16[2,256,256]{2,1,0:T(8,128)(2,1)}, bf16[2,256,256]{2,1,0:T(8,128)(2,1)S(1)}, u32[]{:S(2)}, u32[]{:S(2)}) collective-permute-start(bf16[2,256,256]{2,1,0:T(8,128)(2,1)} %collective-permute-done.refs_1_), channel_id=1, source_target_pairs={{0,4},{4,8},{8,12},{1,5},{5,9},{9,13},{2,6},{6,10},{10,14},{3,7},{... | collective-permute-start | bytes 786440 | tf_op jit(solution)/shard_map/ppermute | solution.py:146
  17.9 0.6 %pad_add_fusion.2.scalars = s32[3]{0:T(128)} fusion(s32[1]{0:T(128)} %bitcast.3, s32[1]{0:T(128)} %bitcast, s32[1]{0:T(128)} %copy.9), kind=kLoop, calls=%fused_computation.26 | loop fusion | flops 6 | bytes 24 | tf_op jit(solution)/shard_map/stack | solution.py:201
  18.5 0.1 pad_dynamic-slice_fusion.4
  18.6 1.8 %pad_maximum_fusion = bf16[256,16,128]{2,1,0:T(8,128)(2,1)S(1)} fusion(bf16[256,16,64]{2,1,0:T(8,128)(2,1)} %get-tuple-element.15, bf16[256,16,64]{2,1,0:T(8,128)(2,1)S(1)} %get-tuple-element.14), kind=kLoop, calls=%fused_computation.8 | loop fusion | flops 2097152 | bytes 2097152 | tf_op jit(solution)/shard_map/concatenate | solution.py:29
  20.4 3.3 %collective-permute-done.1.refs_0_ = bf16[2,256,256]{2,1,0:T(8,128)(2,1)S(1)} collective-permute-done((bf16[2,256,256]{2,1,0:T(8,128)(2,1)}, bf16[2,256,256]{2,1,0:T(8,128)(2,1)S(1)}, u32[]{:S(2)}, u32[]{:S(2)}) %collective-permute-start.1) | collective-permute-done | bytes 262176 | tf_op jit(solution)/shard_map/ppermute | solution.py:146
  23.6 3.7 %collective-permute-start.2 = (bf16[2,256,256]{2,1,0:T(8,128)(2,1)S(1)}, bf16[2,256,256]{2,1,0:T(8,128)(2,1)S(1)}, u32[]{:S(2)}, u32[]{:S(2)}) collective-permute-start(bf16[2,256,256]{2,1,0:T(8,128)(2,1)S(1)} %collective-permute-done.1.refs_0_), channel_id=1, source_target_pairs={{0,4},{4,8},{8,12},{1,5},{5,9},{9,13},{2,6},{6,10},{10,14},{3,7},{... | collective-permute-start | bytes 786440 | tf_op jit(solution)/shard_map/ppermute | solution.py:146
  27.3 0.7 %pad_add_fusion.scalars = s32[3]{0:T(128)} fusion(s32[1]{0:T(128)} %bitcast.1, s32[1]{0:T(128)} %bitcast, s32[1]{0:T(128)} %copy.9), kind=kLoop, calls=%fused_computation.24 | loop fusion | flops 6 | bytes 24 | tf_op jit(solution)/shard_map/stack | solution.py:201
  28.0 1.2 %copy.8 = bf16[32,8,16,128]{3,1,2,0:T(8,128)(2,1)} copy(bf16[32,8,16,128]{3,2,1,0:T(8,128)(2,1)S(1)} %bitcast.24) | data formatting | bytes 2097152
  29.2 5.1 %shard_map.50 = (f32[2,256,8]{2,1,0:T(8,128)}, f32[2,256,8]{2,1,0:T(8,128)}, f32[256,2048]{1,0:T(8,128)}) custom-call(s32[3]{0:T(128)} %pad_add_fusion.3.scalars, bf16[256,2048]{1,0:T(8,128)(2,1)} %bitcast.21, bf16[2,256,256]{2,1,0:T(8,128)(2,1)} %pad_maximum_fusion.1.refs_0_), custom_call_target="tpu_custom_call" | custom-call | tf_op jit(solution)/shard_map/pallas_call | solution.py:138
  34.3 0.0 copy-done.3
  34.3 10.2 %shard_map.51 = (f32[2,256,8]{2,1,0:T(8,128)}, f32[2,256,8]{2,1,0:T(8,128)}, f32[256,2048]{1,0:T(8,128)}) custom-call(s32[3]{0:T(128)} %pad_add_fusion.2.scalars, bf16[256,2048]{1,0:T(8,128)(2,1)} %bitcast.22, bf16[2,256,256]{2,1,0:T(8,128)(2,1)} %copy-done.3, bf16[2,256,256]{2,1,0:T(8,128)(2,1)} %collective-permute-done.refs_1_, ...), custom_call_target="tpu_custom_call" | custom-call | tf_op jit(solution)/shard_map/pallas_call | solution.py:138
  44.5 2.4 %fusion.4 = bf16[1,2,512,256]{3,2,1,0:T(8,128)(2,1)} fusion(s32[]{:T(128)S(6)} %select_n.3, bf16[1,256,256]{2,1,0:T(8,128)(2,1)S(1)} %get-tuple-element.19, bf16[1,256,256]{2,1,0:T(8,128)(2,1)S(1)} %copy-done.1, bf16[2,256,256]{2,1,0:T(8,128)(2,1)} %collective-permute-done.refs_1_, bf16[2,256,256]{2,1,0:T(8,128)(2,1)} %copy-done.3, ...), kind=kLoop, calls=%fused_computation.13 | loop fusion | flops 2621440 | bytes 1311748 | tf_op jit(solution)/shard_map/broadcast_in_dim | solution.py:222
  46.9 0.0 collective-permute-done.2.refs_0_
  46.9 0.7 %copy-done.4 = bf16[2,256,256]{2,1,0:T(8,128)(2,1)} copy-done((bf16[2,256,256]{2,1,0:T(8,128)(2,1)}, bf16[2,256,256]{2,1,0:T(8,128)(2,1)S(1)}, u32[]{:S(2)}) %copy-start.4) | copy-done | bytes 262168
  47.6 12.0 %shard_map.52 = bf16[256,2048]{1,0:T(8,128)(2,1)} custom-call(s32[3]{0:T(128)} %pad_add_fusion.scalars, bf16[256,2048]{1,0:T(8,128)(2,1)} %bitcast.23, bf16[2,256,256]{2,1,0:T(8,128)(2,1)} %copy-done.4, f32[2,256,8]{2,1,0:T(8,128)} %get-tuple-element.11.refs_1_, f32[2,256,8]{2,1,0:T(8,128)} %get-tuple-element.12.refs_2_, f32[256,2048]{1,0:T(8,128)} %get-tuple-element.13.refs_3_), custom_call_target="tpu_custom_call" | custom-call | tf_op jit(solution)/shard_map/pallas_call | solution.py:138
  (7 shorter events, 0.0 us)
Async XLA Ops:
  0.6 7.0 %copy-start.2 = (bf16[1,256,2048]{2,1,0:T(8,128)(2,1)S(1)}, bf16[1,256,2048]{2,1,0:T(8,128)(2,1)}, u32[]{:S(2)}) copy-start(bf16[1,256,2048]{2,1,0:T(8,128)(2,1)} %param.3) | copy-start | bytes 3145732
  3.4 4.9 %copy-start = (bf16[1,256,256]{2,1,0:T(8,128)(2,1)}, bf16[1,256,256]{2,1,0:T(8,128)(2,1)S(1)}, u32[]{:S(2)}) copy-start(bf16[1,256,256]{2,1,0:T(8,128)(2,1)S(1)} %convert_element_type.42) | copy-start | bytes 393220
  4.1 10.2 %collective-permute-start = (bf16[2,256,256]{2,1,0:T(8,128)(2,1)}, bf16[2,256,256]{2,1,0:T(8,128)(2,1)}, u32[]{:S(2)}, u32[]{:S(2)}) collective-permute-start(bf16[2,256,256]{2,1,0:T(8,128)(2,1)} %pad_maximum_fusion.1.refs_0_), channel_id=1, source_target_pairs={{0,4},{4,8},{8,12},{1,5},{5,9},{9,13},{2,6},{6,10},{10,14},{3,7},{... | collective-permute-start | bytes 786440 | tf_op jit(solution)/shard_map/ppermute | solution.py:146
  14.4 9.3 %collective-permute-start.1 = (bf16[2,256,256]{2,1,0:T(8,128)(2,1)}, bf16[2,256,256]{2,1,0:T(8,128)(2,1)S(1)}, u32[]{:S(2)}, u32[]{:S(2)}) collective-permute-start(bf16[2,256,256]{2,1,0:T(8,128)(2,1)} %collective-permute-done.refs_1_), channel_id=1, source_target_pairs={{0,4},{4,8},{8,12},{1,5},{5,9},{9,13},{2,6},{6,10},{10,14},{3,7},{... | collective-permute-start | bytes 786440 | tf_op jit(solution)/shard_map/ppermute | solution.py:146
  23.6 10.6 %copy-start.3 = (bf16[2,256,256]{2,1,0:T(8,128)(2,1)}, bf16[2,256,256]{2,1,0:T(8,128)(2,1)S(1)}, u32[]{:S(2)}) copy-start(bf16[2,256,256]{2,1,0:T(8,128)(2,1)S(1)} %collective-permute-done.1.refs_0_) | copy-start | bytes 786436
  23.6 23.3 %collective-permute-start.2 = (bf16[2,256,256]{2,1,0:T(8,128)(2,1)S(1)}, bf16[2,256,256]{2,1,0:T(8,128)(2,1)S(1)}, u32[]{:S(2)}, u32[]{:S(2)}) collective-permute-start(bf16[2,256,256]{2,1,0:T(8,128)(2,1)S(1)} %collective-permute-done.1.refs_0_), channel_id=1, source_target_pairs={{0,4},{4,8},{8,12},{1,5},{5,9},{9,13},{2,6},{6,10},{10,14},{3,7},{... | collective-permute-start | bytes 786440 | tf_op jit(solution)/shard_map/ppermute | solution.py:146
  34.3 10.2 %copy-start.1 = (bf16[1,256,256]{2,1,0:T(8,128)(2,1)S(1)}, bf16[1,256,256]{2,1,0:T(8,128)(2,1)}, u32[]{:S(2)}) copy-start(bf16[1,256,256]{2,1,0:T(8,128)(2,1)} %copy-done) | copy-start | bytes 393220
  46.9 0.7 %copy-start.4 = (bf16[2,256,256]{2,1,0:T(8,128)(2,1)}, bf16[2,256,256]{2,1,0:T(8,128)(2,1)S(1)}, u32[]{:S(2)}) copy-start(bf16[2,256,256]{2,1,0:T(8,128)(2,1)S(1)} %collective-permute-done.2.refs_0_) | copy-start | bytes 786436

commit v7 on v3

--- a/solution.py
+++ b/solution.py
@@ -40,8 +40,13 @@
     first_pos = scalars[1]
     key_start = pl.multiple_of(scalars[2], 256)
     query_pos = first_pos + lax.broadcasted_iota(jnp.int32, (rows, span), 0)
-    key_pos = key_start + lax.broadcasted_iota(jnp.int32, (rows, span), 1)
-    allowed = (key_pos <= query_pos) & (key_pos > query_pos - WINDOW) & (key_pos < seq_len)
+    key_pos = scalars[3] + lax.broadcasted_iota(jnp.int32, (rows, span), 1)
+    allowed = (
+        (key_pos <= query_pos)
+        & (key_pos > query_pos - WINDOW)
+        & (key_pos >= 0)
+        & (key_pos < seq_len)
+    )
     bias_ref[...] = jnp.where(allowed, 0.0, neg_floor)
     k = k_ref[0, pl.ds(key_start, span), :]
     v = v_ref[0, pl.ds(key_start, span), :]
@@ -83,6 +88,12 @@
     )(scalars, rotated_q, gathered, gathered)
 
 
+def passed_along(x, by):
+    devices = lax.axis_size("seq")
+    pairs = [(i, i + by) for i in range(devices) if 0 <= i + by < devices]
+    return lax.ppermute(x, "seq", pairs)
+
+
 def local(queries, keys_values, lengths):
     seq_len = lengths[0]
     shard_rows = queries.shape[1]
@@ -92,6 +103,7 @@
     group_size = heads_dev // kv_heads_dev
     seq_index = lax.axis_index("seq")
     seq_count = lax.axis_size("seq")
+    tokens = seq_count * shard_rows
     first_pos = seq_index * shard_rows
     positions = first_pos + jnp.arange(shard_rows, dtype=jnp.int32)
     rotated_q = rotate(queries[0].reshape(shard_rows, heads_dev, HD).astype(jnp.float32), positions)
@@ -102,24 +114,32 @@
     own_block = jnp.stack(
         [rotated_k.astype(jnp.bfloat16).reshape(shard_rows, width), keys_values[0, 1]]
     )
-    outbox = jnp.broadcast_to(own_block[:, None], (2, seq_count, shard_rows, width))
-    gathered = lax.all_to_all(
-        outbox.reshape(2, seq_count * shard_rows, width), "seq", 1, 1, tiled=True
-    )
-    tokens = gathered.shape[1]
-
     reach_count = min(WINDOW // shard_rows, seq_count - 1)
     span = (reach_count + 1) * shard_rows
-    key_start = jnp.maximum(first_pos - reach_count * shard_rows, 0)
-    scalars = jnp.stack([seq_len, first_pos, key_start]).astype(jnp.int32)
-    attended = attention(scalars, rotated_q, gathered, kv_heads_dev, group_size, span)
+    if WINDOW >= tokens:
+        shifted = [own_block]
+        for hop in range(1, reach_count + 1):
+            shifted.insert(0, passed_along(own_block, hop))
+        held = jnp.concatenate(shifted, axis=1)
+        held_first = first_pos - reach_count * shard_rows
+        key_index = jnp.zeros((), jnp.int32)
+        key_first = held_first
+    else:
+        outbox = jnp.broadcast_to(own_block[:, None], (2, seq_count, shard_rows, width))
+        held = lax.all_to_all(
+            outbox.reshape(2, tokens, width), "seq", 1, 1, tiled=True
+        )
+        held_first = 0
+        key_index = jnp.maximum(first_pos - reach_count * shard_rows, 0)
+        key_first = key_index
+    scalars = jnp.stack([seq_len, first_pos, key_index, key_first]).astype(jnp.int32)
+    attended = attention(scalars, rotated_q, held, kv_heads_dev, group_size, span)
     attended = attended.reshape(1, shard_rows, heads_dev * HD)
 
     slot_rows = WINDOW // seq_count
-    padded = jnp.concatenate([jnp.zeros((2, WINDOW, width), jnp.bfloat16), gathered], axis=1)
-    begin_row = seq_len + seq_index * slot_rows
+    padded = jnp.concatenate([jnp.zeros((2, WINDOW, width), jnp.bfloat16), held], axis=1)
+    begin_row = seq_len - held_first + seq_index * slot_rows
     window_cache = lax.dynamic_slice_in_dim(padded, begin_row, slot_rows, 1)
-    del tokens
     return (attended, window_cache[None])
 
 

time: 49.9 us -> 48.2 us (0.966)
  the two profiles are of different devices: /device:TPU:0 before, /device:TPU:20 now
where the time goes in v7:
time: 48.2 us; the launch traced here: 47.8 us
  waiting for transfers between devices  15.2 us (32%)
  Pallas kernels  11.2 us (23%)
  local copies, waits for them, and re-layouts  7.44 us (15%)
  other arithmetic  6.44 us (13%)
  starting transfers between devices  6.07 us (13%)
  between operations  1.42 us (3%)
    ppermute x3, waiting for transfers between devices, passed_along(): return lax.ppermute(x, 'seq', pairs)  15.2 us
    pallas_call x1, Pallas kernels, attention(): pl.pallas_call(kernel, grid_spec=grid_spec, out_shape=jax.ShapeDtypeStruc...  11.2 us
    ppermute x3, starting transfers between devices, passed_along(): return lax.ppermute(x, 'seq', pairs)  6.07 us
    unnamed x8, local copies, waits for them, and re-layouts  5.26 us
    broadcast_in_dim x1, local copies, waits for them, and re-layouts, local(): return (attended, window_cache[None])  1.96 us
    another operation x2, other arithmetic  1.24 us
    convert_element_type x1, other arithmetic, local(): keys_values[0, 0].reshape(shard_rows, kv_heads_dev, HD).astype(jnp.float32)  1.08 us
    concatenate x1, other arithmetic, local(): held = jnp.concatenate(shifted, axis=1)  1.03 us
  transfers between devices with their start and end apart: 3, of which 2 were waited for; matrix products, arithmetic and copies ran while one was open for 14% of the time, Pallas kernels for 0%

profile of v7, /device:TPU:20, one launch (start us, length us, event | category | flops | bytes accessed | tf_op | source)
XLA Modules:
  0.0 47.8 jit_solution(11814790562452894719)
XLA Ops:
  0.6 0.0 copy-start
  0.7 1.1 %slice_convert_fusion = (f32[1,1,256,256]{3,2,1,0:T(8,128)S(1)}, bf16[1,256,256]{2,1,0:T(8,128)(2,1)S(1)}) fusion(bf16[1,2,256,256]{3,2,1,0:T(8,128)(2,1)} %param.4), kind=kLoop, calls=%fused_computation.15 | loop fusion | flops 65536 | bytes 655360 | tf_op jit(solution)/shard_map/convert_element_type | solution.py:112
  1.8 0.1 reshape.84
  1.9 0.5 %multiply_cosine_fusion = (f32[256,64]{1,0:T(8,128)S(1)}, f32[256,64]{1,0:T(8,128)S(1)}) fusion(f32[64]{0:T(128)S(1)} %multiply_exponential_fusion, f32[256]{0:T(256)S(1)} %add_convert_fusion.2), kind=kLoop, calls=%fused_computation.12 | loop fusion | flops 16384 | bytes 132352 | tf_op jit(solution)/shard_map/cos | solution.py:25
  2.4 0.5 subtract_convert_fusion.1
  2.9 0.4 pad_maximum_fusion.2
  3.3 0.1 convert_element_type.42
  3.4 0.7 %collective-permute-start = (bf16[2,256,256]{2,1,0:T(8,128)(2,1)S(1)}, bf16[2,256,256]{2,1,0:T(8,128)(2,1)S(1)}, u32[]{:S(2)}, u32[]{:S(2)}) collective-permute-start(bf16[2,256,256]{2,1,0:T(8,128)(2,1)S(1)} %pad_maximum_fusion.1), channel_id=1, source_target_pairs={{0,12},{1,13},{2,14},{3,15},{16,28},{17,29},{18,30},{19,31}} | collective-permute-start | bytes 786440 | tf_op jit(solution)/shard_map/ppermute | solution.py:94
  4.1 1.3 %collective-permute-start.1 = (bf16[2,256,256]{2,1,0:T(8,128)(2,1)S(1)}, bf16[2,256,256]{2,1,0:T(8,128)(2,1)S(1)}, u32[]{:S(2)}, u32[]{:S(2)}) collective-permute-start(bf16[2,256,256]{2,1,0:T(8,128)(2,1)S(1)} %pad_maximum_fusion.1), channel_id=1, source_target_pairs={{0,8},{4,12},{1,9},{5,13},{2,10},{6,14},{3,11},{7,15},{16,24},{20,... | collective-permute-start | bytes 786440 | tf_op jit(solution)/shard_map/ppermute | solution.py:94
  5.4 4.1 %collective-permute-start.2 = (bf16[2,256,256]{2,1,0:T(8,128)(2,1)S(1)}, bf16[2,256,256]{2,1,0:T(8,128)(2,1)S(1)}, u32[]{:S(2)}, u32[]{:S(2)}) collective-permute-start(bf16[2,256,256]{2,1,0:T(8,128)(2,1)S(1)} %pad_maximum_fusion.1), channel_id=1, source_target_pairs={{0,4},{4,8},{8,12},{1,5},{5,9},{9,13},{2,6},{6,10},{10,14},{3,7},{... | collective-permute-start | bytes 786440 | tf_op jit(solution)/shard_map/ppermute | solution.py:94
  9.5 0.0 copy-done
  9.5 0.2 convert_bitcast_fusion
  9.8 0.4 copy.5
  10.2 0.8 %subtract_convert_fusion = (bf16[256,16,64]{2,1,0:T(8,128)(2,1)S(1)}, bf16[256,16,64]{2,1,0:T(8,128)(2,1)S(1)}) fusion(f32[256,16,128]{2,1,0:T(8,128)S(1)} %bitcast.19, f32[256,64]{1,0:T(8,128)S(1)} %get-tuple-element.9, f32[256,64]{1,0:T(8,128)S(1)} %get-tuple-element.8), kind=kLoop, calls=%fused_computation.2 | loop fusion | flops 2097152 | bytes 3276800 | tf_op jit(solution)/shard_map/convert.4
  10.9 1.4 %broadcast_dynamic-update-slice_fusion = bf16[2,3072,256]{2,1,0:T(8,128)(2,1)} fusion(), kind=kLoop, calls=%fused_computation.6 | loop fusion | bytes 2097152
  12.4 0.6 %pad_maximum_fusion = bf16[256,16,128]{2,1,0:T(8,128)(2,1)S(1)} fusion(bf16[256,16,64]{2,1,0:T(8,128)(2,1)S(1)} %get-tuple-element.3, bf16[256,16,64]{2,1,0:T(8,128)(2,1)S(1)} %get-tuple-element.2), kind=kLoop, calls=%fused_computation.4 | loop fusion | flops 2097152 | bytes 2097152 | tf_op jit(solution)/shard_map/concatenate | solution.py:29
  13.6 0.6 %pad_add_fusion.scalars = s32[4]{0:T(128)} fusion(s32[1]{0:T(128)} %bitcast.1, s32[1]{0:T(128)} %constant.6.clone.1, s32[1]{0:T(128)} %bitcast, s32[1]{0:T(128)} %copy.13), kind=kLoop, calls=%fused_computation.21 | loop fusion | flops 12 | bytes 32 | tf_op jit(solution)/shard_map/stack | solution.py:135
  14.2 1.3 %copy.8 = bf16[32,8,16,128]{3,1,2,0:T(8,128)(2,1)} copy(bf16[32,8,16,128]{3,2,1,0:T(8,128)(2,1)S(1)} %bitcast.21) | data formatting | bytes 2097152
  15.5 0.0 collective-permute-done
  15.5 0.7 %constant_dynamic-update-slice_fusion.3 = bf16[2,3072,256]{2,1,0:T(8,128)(2,1)} fusion(bf16[2,3072,256]{2,1,0:T(8,128)(2,1)} %broadcast_dynamic-update-slice_fusion, bf16[2,256,256]{2,1,0:T(8,128)(2,1)S(1)} %collective-permute-done), kind=kLoop, calls=%fused_computation.19 | loop fusion | bytes 524288
  16.2 5.9 %collective-permute-done.1 = bf16[2,256,256]{2,1,0:T(8,128)(2,1)S(1)} collective-permute-done((bf16[2,256,256]{2,1,0:T(8,128)(2,1)S(1)}, bf16[2,256,256]{2,1,0:T(8,128)(2,1)S(1)}, u32[]{:S(2)}, u32[]{:S(2)}) %collective-permute-start.1) | collective-permute-done | bytes 262176 | tf_op jit(solution)/shard_map/ppermute | solution.py:94
  22.1 0.7 %constant_dynamic-update-slice_fusion.2 = bf16[2,3072,256]{2,1,0:T(8,128)(2,1)} fusion(bf16[2,3072,256]{2,1,0:T(8,128)(2,1)} %constant_dynamic-update-slice_fusion.3, bf16[2,256,256]{2,1,0:T(8,128)(2,1)S(1)} %collective-permute-done.1), kind=kLoop, calls=%fused_computation.18 | loop fusion | bytes 524288
  22.8 9.3 %collective-permute-done.2 = bf16[2,256,256]{2,1,0:T(8,128)(2,1)S(1)} collective-permute-done((bf16[2,256,256]{2,1,0:T(8,128)(2,1)S(1)}, bf16[2,256,256]{2,1,0:T(8,128)(2,1)S(1)}, u32[]{:S(2)}, u32[]{:S(2)}) %collective-permute-start.2) | collective-permute-done | bytes 262176 | tf_op jit(solution)/shard_map/ppermute | solution.py:94
  32.2 0.7 %constant_dynamic-update-slice_fusion.1 = bf16[2,3072,256]{2,1,0:T(8,128)(2,1)} fusion(bf16[2,3072,256]{2,1,0:T(8,128)(2,1)} %constant_dynamic-update-slice_fusion.2, bf16[2,256,256]{2,1,0:T(8,128)(2,1)S(1)} %collective-permute-done.2), kind=kLoop, calls=%fused_computation.17 | loop fusion | bytes 524288
  32.9 0.7 %constant_dynamic-update-slice_fusion = bf16[2,3072,256]{2,1,0:T(8,128)(2,1)} fusion(bf16[2,3072,256]{2,1,0:T(8,128)(2,1)} %constant_dynamic-update-slice_fusion.1, bf16[1,256,256]{2,1,0:T(8,128)(2,1)S(1)} %get-tuple-element.7, bf16[1,256,256]{2,1,0:T(8,128)(2,1)S(1)} %convert_element_type.42), kind=kLoop, calls=%fused_computation.16 | loop fusion | flops 524288 | bytes 524288 | tf_op jit(solution)/shard_map/concatenate | solution.py:140
  33.6 2.0 %dynamic-slice_bitcast_fusion = bf16[1,2,512,256]{3,2,1,0:T(8,128)(2,1)} fusion(bf16[2,3072,256]{2,1,0:T(8,128)(2,1)} %constant_dynamic-update-slice_fusion, s32[]{:T(128)S(6)} %select_n.3), kind=kLoop, calls=%fused_computation.7 | loop fusion | bytes 1048580 | tf_op jit(solution)/shard_map/broadcast_in_dim | solution.py:143
  35.6 1.0 %maximum_maximum_fusion.k_ref.v_ref = bf16[2,1024,256]{2,1,0:T(8,128)(2,1)} fusion(bf16[1,256,256]{2,1,0:T(8,128)(2,1)S(1)} %get-tuple-element.7, bf16[1,256,256]{2,1,0:T(8,128)(2,1)S(1)} %convert_element_type.42, bf16[2,256,256]{2,1,0:T(8,128)(2,1)S(1)} %collective-permute-done.2, bf16[2,256,256]{2,1,0:T(8,128)(2,1)S(1)} %collective-permute-done.1, ...), kind=kLoop, calls=%fused_computation.5 | loop fusion | flops 5242880 | bytes 2097152 | tf_op jit(solution)/shard_map/concatenate | solution.py:123
  36.6 11.2 %shard_map.50 = bf16[256,2048]{1,0:T(8,128)(2,1)} custom-call(s32[4]{0:T(128)} %pad_add_fusion.scalars, bf16[256,2048]{1,0:T(8,128)(2,1)} %bitcast.20, bf16[2,1024,256]{2,1,0:T(8,128)(2,1)} %maximum_maximum_fusion.k_ref.v_ref, bf16[2,1024,256]{2,1,0:T(8,128)(2,1)} %maximum_maximum_fusion.k_ref.v_ref), custom_call_target="tpu_custom_call" | custom-call | tf_op jit(solution)/shard_map/pallas_call | solution.py:84
  (3 shorter events, 0.0 us)
Async XLA Ops:
  0.6 8.9 %copy-start = (bf16[1,256,2048]{2,1,0:T(8,128)(2,1)S(1)}, bf16[1,256,2048]{2,1,0:T(8,128)(2,1)}, u32[]{:S(2)}) copy-start(bf16[1,256,2048]{2,1,0:T(8,128)(2,1)} %param.3) | copy-start | bytes 3145732
  3.4 12.1 %collective-permute-start = (bf16[2,256,256]{2,1,0:T(8,128)(2,1)S(1)}, bf16[2,256,256]{2,1,0:T(8,128)(2,1)S(1)}, u32[]{:S(2)}, u32[]{:S(2)}) collective-permute-start(bf16[2,256,256]{2,1,0:T(8,128)(2,1)S(1)} %pad_maximum_fusion.1), channel_id=1, source_target_pairs={{0,12},{1,13},{2,14},{3,15},{16,28},{17,29},{18,30},{19,31}} | collective-permute-start | bytes 786440 | tf_op jit(solution)/shard_map/ppermute | solution.py:94
  4.1 18.0 %collective-permute-start.1 = (bf16[2,256,256]{2,1,0:T(8,128)(2,1)S(1)}, bf16[2,256,256]{2,1,0:T(8,128)(2,1)S(1)}, u32[]{:S(2)}, u32[]{:S(2)}) collective-permute-start(bf16[2,256,256]{2,1,0:T(8,128)(2,1)S(1)} %pad_maximum_fusion.1), channel_id=1, source_target_pairs={{0,8},{4,12},{1,9},{5,13},{2,10},{6,14},{3,11},{7,15},{16,24},{20,... | collective-permute-start | bytes 786440 | tf_op jit(solution)/shard_map/ppermute | solution.py:94
  5.4 26.8 %collective-permute-start.2 = (bf16[2,256,256]{2,1,0:T(8,128)(2,1)S(1)}, bf16[2,256,256]{2,1,0:T(8,128)(2,1)S(1)}, u32[]{:S(2)}, u32[]{:S(2)}) collective-permute-start(bf16[2,256,256]{2,1,0:T(8,128)(2,1)S(1)} %pad_maximum_fusion.1), channel_id=1, source_target_pairs={{0,4},{4,8},{8,12},{1,5},{5,9},{9,13},{2,6},{6,10},{10,14},{3,7},{... | collective-permute-start | bytes 786440 | tf_op jit(solution)/shard_map/ppermute | solution.py:94

commit v8 on v7

--- a/solution.py
+++ b/solution.py
@@ -35,7 +35,9 @@
     )
 
 
-def attend_kernel(scalars, q_ref, k_ref, v_ref, o_ref, bias_ref, *, rows, span, group):
+def attend_kernel(scalars, q_ref, *refs, rows, span, group, nparts):
+    part_refs = refs[:nparts]
+    o_ref, bias_ref = refs[nparts:]
     seq_len = scalars[0]
     first_pos = scalars[1]
     key_start = pl.multiple_of(scalars[2], 256)
@@ -48,8 +50,12 @@
         & (key_pos < seq_len)
     )
     bias_ref[...] = jnp.where(allowed, 0.0, neg_floor)
-    k = k_ref[0, pl.ds(key_start, span), :]
-    v = v_ref[0, pl.ds(key_start, span), :]
+    if nparts == 1:
+        k = part_refs[0][0, pl.ds(key_start, span), :]
+        v = part_refs[0][1, pl.ds(key_start, span), :]
+    else:
+        k = jnp.concatenate([p[0] for p in part_refs], axis=0)
+        v = jnp.concatenate([p[1] for p in part_refs], axis=0)
     valid = (first_pos + lax.broadcasted_iota(jnp.int32, (rows, 1), 0)) < seq_len
     scale = 1.0 / math.sqrt(HD)
     for head in range(group):
@@ -65,19 +71,18 @@
         o_ref[:, cols] = jnp.where(valid, numer / denom, 0.0).astype(o_ref.dtype)
 
 
-def attention(scalars, rotated_q, gathered, kv_heads_dev, group_size, span):
+def attention(scalars, rotated_q, parts, kv_heads_dev, group_size, span):
     rows = rotated_q.shape[0]
-    tokens = gathered.shape[1]
-    kernel = functools.partial(attend_kernel, rows=rows, span=span, group=group_size)
+    nparts = len(parts)
+    kernel = functools.partial(
+        attend_kernel, rows=rows, span=span, group=group_size, nparts=nparts
+    )
     width = group_size * HD
     grid_spec = pltpu.PrefetchScalarGridSpec(
         num_scalar_prefetch=1,
         grid=(kv_heads_dev,),
-        in_specs=[
-            pl.BlockSpec((rows, width), lambda j, s: (0, j)),
-            pl.BlockSpec((1, tokens, HD), lambda j, s: (0, 0, j)),
-            pl.BlockSpec((1, tokens, HD), lambda j, s: (1, 0, j)),
-        ],
+        in_specs=[pl.BlockSpec((rows, width), lambda j, s: (0, j))]
+        + [pl.BlockSpec((2, p.shape[1], HD), lambda j, s: (0, 0, j)) for p in parts],
         out_specs=pl.BlockSpec((rows, width), lambda j, s: (0, j)),
         scratch_shapes=[pltpu.VMEM((rows, span), jnp.float32)],
     )
@@ -85,7 +90,7 @@
         kernel,
         grid_spec=grid_spec,
         out_shape=jax.ShapeDtypeStruct((rows, kv_heads_dev * width), jnp.bfloat16),
-    )(scalars, rotated_q, gathered, gathered)
+    )(scalars, rotated_q, *parts)
 
 
 def passed_along(x, by):
@@ -116,27 +121,37 @@
     )
     reach_count = min(WINDOW // shard_rows, seq_count - 1)
     span = (reach_count + 1) * shard_rows
+    slot_rows = WINDOW // seq_count
     if WINDOW >= tokens:
         shifted = [own_block]
         for hop in range(1, reach_count + 1):
             shifted.insert(0, passed_along(own_block, hop))
-        held = jnp.concatenate(shifted, axis=1)
-        held_first = first_pos - reach_count * shard_rows
+        parts = shifted
         key_index = jnp.zeros((), jnp.int32)
-        key_first = held_first
+        key_first = first_pos - reach_count * shard_rows
+        shortest = min(WINDOW, tokens - shard_rows) + 1
+        cache_hops = 0
+        for index in range(seq_count):
+            if tokens - WINDOW + (index + 1) * slot_rows - 1 < 0:
+                continue
+            lowest = max(0, (shortest - WINDOW + index * slot_rows) // shard_rows)
+            cache_hops = max(cache_hops, index - lowest)
+        cache_hops = min(cache_hops, reach_count)
+        held = jnp.concatenate(shifted[reach_count - cache_hops:], axis=1)
+        held_first = first_pos - cache_hops * shard_rows
     else:
         outbox = jnp.broadcast_to(own_block[:, None], (2, seq_count, shard_rows, width))
         held = lax.all_to_all(
             outbox.reshape(2, tokens, width), "seq", 1, 1, tiled=True
         )
+        parts = [held]
         held_first = 0
         key_index = jnp.maximum(first_pos - reach_count * shard_rows, 0)
         key_first = key_index
     scalars = jnp.stack([seq_len, first_pos, key_index, key_first]).astype(jnp.int32)
-    attended = attention(scalars, rotated_q, held, kv_heads_dev, group_size, span)
+    attended = attention(scalars, rotated_q, parts, kv_heads_dev, group_size, span)
     attended = attended.reshape(1, shard_rows, heads_dev * HD)
 
-    slot_rows = WINDOW // seq_count
     padded = jnp.concatenate([jnp.zeros((2, WINDOW, width), jnp.bfloat16), held], axis=1)
     begin_row = seq_len - held_first + seq_index * slot_rows
     window_cache = lax.dynamic_slice_in_dim(padded, begin_row, slot_rows, 1)

time: 48.2 us -> 45.9 us (0.952)
  local copies, waits for them, and re-layouts: 7.44 us -> 1.97 us
  waiting for transfers between devices: 15.2 us -> 18 us
    unnamed x8 -> x10, local copies, waits for them, and re-layouts: 5.26 us -> 1.65 us
    ppermute x3, waiting for transfers between devices: 15.2 us -> 18 us  [passed_along(): return lax.ppermute(x, 'seq', pairs)]
    broadcast_in_dim x0 -> x1, other arithmetic: none -> 2.05 us  [local(): return (attended, window_cache[None])]
    broadcast_in_dim x1, local copies, waits for them, and re-layouts: 1.96 us -> 0.01 us  [local(): jnp.zeros((2, WINDOW, width), jnp.bfloat16)]
    concatenate x2 -> x0, other arithmetic: 1.76 us -> none  [the longest x1 1.03 us: local(): held = jnp.concatenate(shifted, axis=1)]
  transfers between devices with their start and end apart: 3 -> 3, of which waited for: 2 -> 2; matrix products, arithmetic and copies ran while one was open for 14% -> 13% of each run, Pallas kernels for 0% -> 0%
where the time goes in v8:
time: 45.9 us; the launch traced here: 45.5 us
  waiting for transfers between devices  18 us (39%)
  Pallas kernels  11.2 us (24%)
  other arithmetic  6.77 us (15%)
  starting transfers between devices  6.08 us (13%)
  local copies, waits for them, and re-layouts  1.97 us (4%)
  between operations  1.45 us (3%)
    ppermute x3, waiting for transfers between devices, passed_along(): return lax.ppermute(x, 'seq', pairs)  18 us
    pallas_call x1, Pallas kernels, attention(): pl.pallas_call(kernel, grid_spec=grid_spec, out_shape=jax.ShapeDtypeStruc...  11.2 us
    ppermute x3, starting transfers between devices, passed_along(): return lax.ppermute(x, 'seq', pairs)  6.08 us
    broadcast_in_dim x1, other arithmetic, local(): return (attended, window_cache[None])  2.05 us
    unnamed x10, local copies, waits for them, and re-layouts  1.65 us
    another operation x2, other arithmetic  1.24 us
    convert_element_type x1, other arithmetic, local(): keys_values[0, 0].reshape(shard_rows, kv_heads_dev, HD).astype(jnp.float32)  1.08 us
    concatenate x2, other arithmetic, rotate(): jnp.concatenate([lower_half * cosine - upper_half * sine_part, upper_half...  0.94 us
  transfers between devices with their start and end apart: 3, of which 2 were waited for; matrix products, arithmetic and copies ran while one was open for 13% of the time, Pallas kernels for 0%

profile of v8, /device:TPU:20, one launch (start us, length us, event | category | flops | bytes accessed | tf_op | source)
XLA Modules:
  0.0 45.5 jit_solution(3138178199016662387)
XLA Ops:
  0.6 0.0 copy-start
  0.7 1.1 %slice_convert_fusion = (f32[1,1,256,256]{3,2,1,0:T(8,128)S(1)}, bf16[1,256,256]{2,1,0:T(8,128)(2,1)S(1)}) fusion(bf16[1,2,256,256]{3,2,1,0:T(8,128)(2,1)} %param.4), kind=kLoop, calls=%fused_computation.21 | loop fusion | flops 65536 | bytes 655360 | tf_op jit(solution)/shard_map/convert_element_type | solution.py:117
  1.8 0.1 reshape.84
  1.9 0.5 %multiply_cosine_fusion = (f32[256,64]{1,0:T(8,128)S(1)}, f32[256,64]{1,0:T(8,128)S(1)}) fusion(f32[64]{0:T(128)S(1)} %multiply_exponential_fusion, f32[256]{0:T(256)S(1)} %add_convert_fusion.2), kind=kLoop, calls=%fused_computation.18 | loop fusion | flops 16384 | bytes 132352 | tf_op jit(solution)/shard_map/cos | solution.py:25
  2.4 0.5 %subtract_convert_fusion.1 = (bf16[256,2,64]{2,1,0:T(2,128)(2,1)S(1)}, bf16[256,2,64]{2,1,0:T(2,128)(2,1)S(1)}) fusion(f32[256,2,128]{2,1,0:T(2,128)S(1)} %reshape.84, f32[256,64]{1,0:T(8,128)S(1)} %get-tuple-element.9, f32[256,64]{1,0:T(8,128)S(1)} %get-tuple-element.8), kind=kLoop, calls=%fused_computation.16 | loop fusion | flops 262144 | bytes 524288 | tf_op jit(solution)/shard_map/convert.2
  2.9 0.4 pad_maximum_fusion.2
  3.3 0.1 convert_element_type.42
  3.4 0.0 copy-start.1
  3.4 1.4 %collective-permute-start = (bf16[2,256,256]{2,1,0:T(8,128)(2,1)S(1)}, bf16[2,256,256]{2,1,0:T(8,128)(2,1)}, u32[]{:S(2)}, u32[]{:S(2)}) collective-permute-start(bf16[2,256,256]{2,1,0:T(8,128)(2,1)S(1)} %pad_maximum_fusion.1.refs_3_), channel_id=1, source_target_pairs={{0,12},{1,13},{2,14},{3,15},{16,28},{17,29},{18,30},{19,31}} | collective-permute-start | bytes 786440 | tf_op jit(solution)/shard_map/ppermute | solution.py:99
  4.8 1.3 %collective-permute-start.1 = (bf16[2,256,256]{2,1,0:T(8,128)(2,1)S(1)}, bf16[2,256,256]{2,1,0:T(8,128)(2,1)S(1)}, u32[]{:S(2)}, u32[]{:S(2)}) collective-permute-start(bf16[2,256,256]{2,1,0:T(8,128)(2,1)S(1)} %pad_maximum_fusion.1.refs_3_), channel_id=1, source_target_pairs={{0,8},{4,12},{1,9},{5,13},{2,10},{6,14},{3,11},{7,15},{16,24},{20,... | collective-permute-start | bytes 786440 | tf_op jit(solution)/shard_map/ppermute | solution.py:99
  6.1 3.4 %collective-permute-start.2 = (bf16[2,256,256]{2,1,0:T(8,128)(2,1)S(1)}, bf16[2,256,256]{2,1,0:T(8,128)(2,1)S(1)}, u32[]{:S(2)}, u32[]{:S(2)}) collective-permute-start(bf16[2,256,256]{2,1,0:T(8,128)(2,1)S(1)} %pad_maximum_fusion.1.refs_3_), channel_id=1, source_target_pairs={{0,4},{4,8},{8,12},{1,5},{5,9},{9,13},{2,6},{6,10},{10,14},{3,7},{... | collective-permute-start | bytes 786440 | tf_op jit(solution)/shard_map/ppermute | solution.py:99
  10.2 0.0 copy-done
  10.2 0.2 convert_bitcast_fusion
  10.4 0.4 copy.5
  10.8 0.0 copy-done.1
  10.8 0.8 %subtract_convert_fusion = (bf16[256,16,64]{2,1,0:T(8,128)(2,1)S(1)}, bf16[256,16,64]{2,1,0:T(8,128)(2,1)S(1)}) fusion(f32[256,16,128]{2,1,0:T(8,128)S(1)} %bitcast.19, f32[256,64]{1,0:T(8,128)S(1)} %get-tuple-element.9, f32[256,64]{1,0:T(8,128)S(1)} %get-tuple-element.8), kind=kLoop, calls=%fused_computation.6 | loop fusion | flops 2097152 | bytes 3276800 | tf_op jit(solution)/shard_map/convert.4
  11.6 0.1 pad_dynamic-slice_fusion.4
  11.7 0.6 %pad_maximum_fusion = bf16[256,16,128]{2,1,0:T(8,128)(2,1)S(1)} fusion(bf16[256,16,64]{2,1,0:T(8,128)(2,1)S(1)} %get-tuple-element.3, bf16[256,16,64]{2,1,0:T(8,128)(2,1)S(1)} %get-tuple-element.2), kind=kLoop, calls=%fused_computation.8 | loop fusion | flops 2097152 | bytes 2097152 | tf_op jit(solution)/shard_map/concatenate | solution.py:29
  12.3 0.7 %pad_add_fusion.scalars = s32[4]{0:T(128)} fusion(s32[1]{0:T(128)} %bitcast.1, s32[1]{0:T(128)} %constant.7.clone.1, s32[1]{0:T(128)} %bitcast, s32[1]{0:T(128)} %copy.9), kind=kLoop, calls=%fused_computation.24 | loop fusion | flops 12 | bytes 32 | tf_op jit(solution)/shard_map/stack | solution.py:151
  13.0 1.2 %copy.8 = bf16[32,8,16,128]{3,1,2,0:T(8,128)(2,1)} copy(bf16[32,8,16,128]{3,2,1,0:T(8,128)(2,1)S(1)} %bitcast.20) | data formatting | bytes 2097152
  14.2 7.9 %collective-permute-done.1.refs_1_ = bf16[2,256,256]{2,1,0:T(8,128)(2,1)S(1)} collective-permute-done((bf16[2,256,256]{2,1,0:T(8,128)(2,1)S(1)}, bf16[2,256,256]{2,1,0:T(8,128)(2,1)S(1)}, u32[]{:S(2)}, u32[]{:S(2)}) %collective-permute-start.1) | collective-permute-done | bytes 262176 | tf_op jit(solution)/shard_map/ppermute | solution.py:99
  22.1 0.0 copy-start.2
  22.1 10.0 %collective-permute-done.2.refs_2_ = bf16[2,256,256]{2,1,0:T(8,128)(2,1)S(1)} collective-permute-done((bf16[2,256,256]{2,1,0:T(8,128)(2,1)S(1)}, bf16[2,256,256]{2,1,0:T(8,128)(2,1)S(1)}, u32[]{:S(2)}, u32[]{:S(2)}) %collective-permute-start.2) | collective-permute-done | bytes 262176 | tf_op jit(solution)/shard_map/ppermute | solution.py:99
  32.2 0.0 copy-start.3
  32.2 2.0 %fusion.4 = bf16[1,2,512,256]{3,2,1,0:T(8,128)(2,1)} fusion(s32[]{:T(128)S(6)} %select_n.3, bf16[1,256,256]{2,1,0:T(8,128)(2,1)S(1)} %get-tuple-element.7, bf16[1,256,256]{2,1,0:T(8,128)(2,1)S(1)} %convert_element_type.42, bf16[2,256,256]{2,1,0:T(8,128)(2,1)S(1)} %collective-permute-done.2.refs_2_, ...), kind=kLoop, calls=%fused_computation.13 | loop fusion | flops 2621440 | bytes 1311748 | tf_op jit(solution)/shard_map/broadcast_in_dim | solution.py:158
  34.2 0.0 collective-permute-done.refs_0_
  34.2 0.0 copy-done.2
  34.2 0.0 copy-done.3
  34.2 11.2 %shard_map.50 = bf16[256,2048]{1,0:T(8,128)(2,1)} custom-call(s32[4]{0:T(128)} %pad_add_fusion.scalars, bf16[256,2048]{1,0:T(8,128)(2,1)} %bitcast.21, bf16[2,256,256]{2,1,0:T(8,128)(2,1)} %collective-permute-done.refs_0_, bf16[2,256,256]{2,1,0:T(8,128)(2,1)} %copy-done.2, bf16[2,256,256]{2,1,0:T(8,128)(2,1)} %copy-done.3, bf16[2,256,256]{2,1,0:T(8,128)(2,1)} %copy-done.1), custom_call_target="tpu_custom_call" | custom-call | tf_op jit(solution)/shard_map/pallas_call | solution.py:89
  (4 shorter events, 0.0 us)
Async XLA Ops:
  0.6 9.5 %copy-start = (bf16[1,256,2048]{2,1,0:T(8,128)(2,1)S(1)}, bf16[1,256,2048]{2,1,0:T(8,128)(2,1)}, u32[]{:S(2)}) copy-start(bf16[1,256,2048]{2,1,0:T(8,128)(2,1)} %param.3) | copy-start | bytes 3145732
  3.4 7.4 %copy-start.1 = (bf16[2,256,256]{2,1,0:T(8,128)(2,1)}, bf16[2,256,256]{2,1,0:T(8,128)(2,1)S(1)}, u32[]{:S(2)}) copy-start(bf16[2,256,256]{2,1,0:T(8,128)(2,1)S(1)} %pad_maximum_fusion.1.refs_3_) | copy-start | bytes 786436
  3.4 30.8 %collective-permute-start = (bf16[2,256,256]{2,1,0:T(8,128)(2,1)S(1)}, bf16[2,256,256]{2,1,0:T(8,128)(2,1)}, u32[]{:S(2)}, u32[]{:S(2)}) collective-permute-start(bf16[2,256,256]{2,1,0:T(8,128)(2,1)S(1)} %pad_maximum_fusion.1.refs_3_), channel_id=1, source_target_pairs={{0,12},{1,13},{2,14},{3,15},{16,28},{17,29},{18,30},{19,31}} | collective-permute-start | bytes 786440 | tf_op jit(solution)/shard_map/ppermute | solution.py:99
  4.8 17.3 %collective-permute-start.1 = (bf16[2,256,256]{2,1,0:T(8,128)(2,1)S(1)}, bf16[2,256,256]{2,1,0:T(8,128)(2,1)S(1)}, u32[]{:S(2)}, u32[]{:S(2)}) collective-permute-start(bf16[2,256,256]{2,1,0:T(8,128)(2,1)S(1)} %pad_maximum_fusion.1.refs_3_), channel_id=1, source_target_pairs={{0,8},{4,12},{1,9},{5,13},{2,10},{6,14},{3,11},{7,15},{16,24},{20,... | collective-permute-start | bytes 786440 | tf_op jit(solution)/shard_map/ppermute | solution.py:99
  6.1 26.1 %collective-permute-start.2 = (bf16[2,256,256]{2,1,0:T(8,128)(2,1)S(1)}, bf16[2,256,256]{2,1,0:T(8,128)(2,1)S(1)}, u32[]{:S(2)}, u32[]{:S(2)}) collective-permute-start(bf16[2,256,256]{2,1,0:T(8,128)(2,1)S(1)} %pad_maximum_fusion.1.refs_3_), channel_id=1, source_target_pairs={{0,4},{4,8},{8,12},{1,5},{5,9},{9,13},{2,6},{6,10},{10,14},{3,7},{... | collective-permute-start | bytes 786440 | tf_op jit(solution)/shard_map/ppermute | solution.py:99
  22.1 12.1 %copy-start.2 = (bf16[2,256,256]{2,1,0:T(8,128)(2,1)}, bf16[2,256,256]{2,1,0:T(8,128)(2,1)S(1)}, u32[]{:S(2)}) copy-start(bf16[2,256,256]{2,1,0:T(8,128)(2,1)S(1)} %collective-permute-done.1.refs_1_) | copy-start | bytes 786436
  32.2 2.1 %copy-start.3 = (bf16[2,256,256]{2,1,0:T(8,128)(2,1)}, bf16[2,256,256]{2,1,0:T(8,128)(2,1)S(1)}, u32[]{:S(2)}) copy-start(bf16[2,256,256]{2,1,0:T(8,128)(2,1)S(1)} %collective-permute-done.2.refs_2_) | copy-start | bytes 786436

commit v9 on v8

--- a/solution.py
+++ b/solution.py
@@ -152,9 +152,9 @@
     attended = attention(scalars, rotated_q, parts, kv_heads_dev, group_size, span)
     attended = attended.reshape(1, shard_rows, heads_dev * HD)
 
-    padded = jnp.concatenate([jnp.zeros((2, WINDOW, width), jnp.bfloat16), held], axis=1)
-    begin_row = seq_len - held_first + seq_index * slot_rows
-    window_cache = lax.dynamic_slice_in_dim(padded, begin_row, slot_rows, 1)
+    padded = jnp.concatenate([jnp.zeros((2, slot_rows, width), jnp.bfloat16), held], axis=1)
+    begin_row = seq_len - WINDOW - held_first + seq_index * slot_rows + slot_rows
+    window_cache = lax.dynamic_slice_in_dim(padded, jnp.maximum(begin_row, 0), slot_rows, 1)
     return (attended, window_cache[None])
 
 

time: 45.9 us -> 45.9 us (level)
  no operation moved by 1% of the time
where the time goes in v9:
time: 45.9 us; the launch traced here: 45.5 us
  waiting for transfers between devices  18 us (39%)
  Pallas kernels  11.2 us (24%)
  other arithmetic  6.77 us (15%)
  starting transfers between devices  6.08 us (13%)
  local copies, waits for them, and re-layouts  1.96 us (4%)
  between operations  1.45 us (3%)
    ppermute x3, waiting for transfers between devices, passed_along(): return lax.ppermute(x, 'seq', pairs)  18 us
    pallas_call x1, Pallas kernels, attention(): pl.pallas_call(kernel, grid_spec=grid_spec, out_shape=jax.ShapeDtypeStruc...  11.2 us
    ppermute x3, starting transfers between devices, passed_along(): return lax.ppermute(x, 'seq', pairs)  6.08 us
    broadcast_in_dim x1, other arithmetic, local(): return (attended, window_cache[None])  2.05 us
    unnamed x10, local copies, waits for them, and re-layouts  1.65 us
    another operation x2, other arithmetic  1.24 us
    convert_element_type x1, other arithmetic, local(): keys_values[0, 0].reshape(shard_rows, kv_heads_dev, HD).astype(jnp.float32)  1.08 us
    concatenate x2, other arithmetic, rotate(): jnp.concatenate([lower_half * cosine - upper_half * sine_part, upper_half...  0.94 us
  transfers between devices with their start and end apart: 3, of which 2 were waited for; matrix products, arithmetic and copies ran while one was open for 13% of the time, Pallas kernels for 0%

profile of v9, /device:TPU:20, one launch (start us, length us, event | category | flops | bytes accessed | tf_op | source)
XLA Modules:
  0.0 45.5 jit_solution(9441184149507915410)
XLA Ops:
  0.6 0.0 copy-start
  0.7 1.1 %slice_convert_fusion = (f32[1,1,256,256]{3,2,1,0:T(8,128)S(1)}, bf16[1,256,256]{2,1,0:T(8,128)(2,1)S(1)}) fusion(bf16[1,2,256,256]{3,2,1,0:T(8,128)(2,1)} %param.4), kind=kLoop, calls=%fused_computation.21 | loop fusion | flops 65536 | bytes 655360 | tf_op jit(solution)/shard_map/convert_element_type | solution.py:117
  1.8 0.1 reshape.86
  1.9 0.5 %multiply_cosine_fusion = (f32[256,64]{1,0:T(8,128)S(1)}, f32[256,64]{1,0:T(8,128)S(1)}) fusion(f32[64]{0:T(128)S(1)} %multiply_exponential_fusion, f32[256]{0:T(256)S(1)} %add_convert_fusion.2), kind=kLoop, calls=%fused_computation.18 | loop fusion | flops 16384 | bytes 132352 | tf_op jit(solution)/shard_map/cos | solution.py:25
  2.4 0.5 %subtract_convert_fusion.1 = (bf16[256,2,64]{2,1,0:T(2,128)(2,1)S(1)}, bf16[256,2,64]{2,1,0:T(2,128)(2,1)S(1)}) fusion(f32[256,2,128]{2,1,0:T(2,128)S(1)} %reshape.86, f32[256,64]{1,0:T(8,128)S(1)} %get-tuple-element.9, f32[256,64]{1,0:T(8,128)S(1)} %get-tuple-element.8), kind=kLoop, calls=%fused_computation.16 | loop fusion | flops 262144 | bytes 524288 | tf_op jit(solution)/shard_map/convert.2
  2.9 0.4 pad_maximum_fusion.2
  3.3 0.1 convert_element_type.42
  3.4 0.0 copy-start.1
  3.4 1.4 %collective-permute-start = (bf16[2,256,256]{2,1,0:T(8,128)(2,1)S(1)}, bf16[2,256,256]{2,1,0:T(8,128)(2,1)}, u32[]{:S(2)}, u32[]{:S(2)}) collective-permute-start(bf16[2,256,256]{2,1,0:T(8,128)(2,1)S(1)} %pad_maximum_fusion.1.refs_3_), channel_id=1, source_target_pairs={{0,12},{1,13},{2,14},{3,15},{16,28},{17,29},{18,30},{19,31}} | collective-permute-start | bytes 786440 | tf_op jit(solution)/shard_map/ppermute | solution.py:99
  4.8 1.3 %collective-permute-start.1 = (bf16[2,256,256]{2,1,0:T(8,128)(2,1)S(1)}, bf16[2,256,256]{2,1,0:T(8,128)(2,1)S(1)}, u32[]{:S(2)}, u32[]{:S(2)}) collective-permute-start(bf16[2,256,256]{2,1,0:T(8,128)(2,1)S(1)} %pad_maximum_fusion.1.refs_3_), channel_id=1, source_target_pairs={{0,8},{4,12},{1,9},{5,13},{2,10},{6,14},{3,11},{7,15},{16,24},{20,... | collective-permute-start | bytes 786440 | tf_op jit(solution)/shard_map/ppermute | solution.py:99
  6.1 3.4 %collective-permute-start.2 = (bf16[2,256,256]{2,1,0:T(8,128)(2,1)S(1)}, bf16[2,256,256]{2,1,0:T(8,128)(2,1)S(1)}, u32[]{:S(2)}, u32[]{:S(2)}) collective-permute-start(bf16[2,256,256]{2,1,0:T(8,128)(2,1)S(1)} %pad_maximum_fusion.1.refs_3_), channel_id=1, source_target_pairs={{0,4},{4,8},{8,12},{1,5},{5,9},{9,13},{2,6},{6,10},{10,14},{3,7},{... | collective-permute-start | bytes 786440 | tf_op jit(solution)/shard_map/ppermute | solution.py:99
  10.2 0.0 copy-done
  10.2 0.2 convert_bitcast_fusion
  10.4 0.4 copy.5
  10.8 0.0 copy-done.1
  10.8 0.8 %subtract_convert_fusion = (bf16[256,16,64]{2,1,0:T(8,128)(2,1)S(1)}, bf16[256,16,64]{2,1,0:T(8,128)(2,1)S(1)}) fusion(f32[256,16,128]{2,1,0:T(8,128)S(1)} %bitcast.18, f32[256,64]{1,0:T(8,128)S(1)} %get-tuple-element.9, f32[256,64]{1,0:T(8,128)S(1)} %get-tuple-element.8), kind=kLoop, calls=%fused_computation.2 | loop fusion | flops 2097152 | bytes 3276800 | tf_op jit(solution)/shard_map/convert.4
  11.6 0.1 pad_dynamic-slice_fusion.4
  11.7 0.6 %pad_maximum_fusion = bf16[256,16,128]{2,1,0:T(8,128)(2,1)S(1)} fusion(bf16[256,16,64]{2,1,0:T(8,128)(2,1)S(1)} %get-tuple-element.3, bf16[256,16,64]{2,1,0:T(8,128)(2,1)S(1)} %get-tuple-element.2), kind=kLoop, calls=%fused_computation.8 | loop fusion | flops 2097152 | bytes 2097152 | tf_op jit(solution)/shard_map/concatenate | solution.py:29
  12.3 0.7 %pad_add_fusion.scalars = s32[4]{0:T(128)} fusion(s32[1]{0:T(128)} %bitcast.1, s32[1]{0:T(128)} %constant.20.clone.1, s32[1]{0:T(128)} %bitcast, s32[1]{0:T(128)S(6)} %copy.9), kind=kLoop, calls=%fused_computation.24 | loop fusion | flops 12 | bytes 32 | tf_op jit(solution)/shard_map/stack | solution.py:151
  13.0 1.2 %copy.8 = bf16[32,8,16,128]{3,1,2,0:T(8,128)(2,1)} copy(bf16[32,8,16,128]{3,2,1,0:T(8,128)(2,1)S(1)} %bitcast.19) | data formatting | bytes 2097152
  14.2 7.9 %collective-permute-done.1.refs_1_ = bf16[2,256,256]{2,1,0:T(8,128)(2,1)S(1)} collective-permute-done((bf16[2,256,256]{2,1,0:T(8,128)(2,1)S(1)}, bf16[2,256,256]{2,1,0:T(8,128)(2,1)S(1)}, u32[]{:S(2)}, u32[]{:S(2)}) %collective-permute-start.1) | collective-permute-done | bytes 262176 | tf_op jit(solution)/shard_map/ppermute | solution.py:99
  22.1 0.0 copy-start.2
  22.1 10.0 %collective-permute-done.2.refs_2_ = bf16[2,256,256]{2,1,0:T(8,128)(2,1)S(1)} collective-permute-done((bf16[2,256,256]{2,1,0:T(8,128)(2,1)S(1)}, bf16[2,256,256]{2,1,0:T(8,128)(2,1)S(1)}, u32[]{:S(2)}, u32[]{:S(2)}) %collective-permute-start.2) | collective-permute-done | bytes 262176 | tf_op jit(solution)/shard_map/ppermute | solution.py:99
  32.2 0.0 copy-start.3
  32.2 2.0 %fusion.3 = bf16[1,2,512,256]{3,2,1,0:T(8,128)(2,1)} fusion(s32[]{:T(128)S(6)} %max.3, bf16[2,256,256]{2,1,0:T(8,128)(2,1)S(1)} %collective-permute-done.1.refs_1_, bf16[2,256,256]{2,1,0:T(8,128)(2,1)S(1)} %collective-permute-done.2.refs_2_, bf16[1,256,256]{2,1,0:T(8,128)(2,1)S(1)} %convert_element_type.42, bf16[1,256,256]{2,1,0:T(8,128)(2,1)S(1)} %get-tuple-element.7, ...), kind=kLoop, calls=%fused_computation.12 | loop fusion | flops 2621440 | bytes 1311748 | tf_op jit(solution)/shard_map/broadcast_in_dim | solution.py:158
  34.2 0.0 collective-permute-done.refs_0_
  34.2 0.0 copy-done.2
  34.2 0.0 copy-done.3
  34.2 11.2 %shard_map.50 = bf16[256,2048]{1,0:T(8,128)(2,1)} custom-call(s32[4]{0:T(128)} %pad_add_fusion.scalars, bf16[256,2048]{1,0:T(8,128)(2,1)} %bitcast.20, bf16[2,256,256]{2,1,0:T(8,128)(2,1)} %collective-permute-done.refs_0_, bf16[2,256,256]{2,1,0:T(8,128)(2,1)} %copy-done.2, bf16[2,256,256]{2,1,0:T(8,128)(2,1)} %copy-done.3, bf16[2,256,256]{2,1,0:T(8,128)(2,1)} %copy-done.1), custom_call_target="tpu_custom_call" | custom-call | tf_op jit(solution)/shard_map/pallas_call | solution.py:89
  (4 shorter events, 0.0 us)
Async XLA Ops:
  0.6 9.5 %copy-start = (bf16[1,256,2048]{2,1,0:T(8,128)(2,1)S(1)}, bf16[1,256,2048]{2,1,0:T(8,128)(2,1)}, u32[]{:S(2)}) copy-start(bf16[1,256,2048]{2,1,0:T(8,128)(2,1)} %param.3) | copy-start | bytes 3145732
  3.4 7.4 %copy-start.1 = (bf16[2,256,256]{2,1,0:T(8,128)(2,1)}, bf16[2,256,256]{2,1,0:T(8,128)(2,1)S(1)}, u32[]{:S(2)}) copy-start(bf16[2,256,256]{2,1,0:T(8,128)(2,1)S(1)} %pad_maximum_fusion.1.refs_3_) | copy-start | bytes 786436
  3.4 30.8 %collective-permute-start = (bf16[2,256,256]{2,1,0:T(8,128)(2,1)S(1)}, bf16[2,256,256]{2,1,0:T(8,128)(2,1)}, u32[]{:S(2)}, u32[]{:S(2)}) collective-permute-start(bf16[2,256,256]{2,1,0:T(8,128)(2,1)S(1)} %pad_maximum_fusion.1.refs_3_), channel_id=1, source_target_pairs={{0,12},{1,13},{2,14},{3,15},{16,28},{17,29},{18,30},{19,31}} | collective-permute-start | bytes 786440 | tf_op jit(solution)/shard_map/ppermute | solution.py:99
  4.8 17.3 %collective-permute-start.1 = (bf16[2,256,256]{2,1,0:T(8,128)(2,1)S(1)}, bf16[2,256,256]{2,1,0:T(8,128)(2,1)S(1)}, u32[]{:S(2)}, u32[]{:S(2)}) collective-permute-start(bf16[2,256,256]{2,1,0:T(8,128)(2,1)S(1)} %pad_maximum_fusion.1.refs_3_), channel_id=1, source_target_pairs={{0,8},{4,12},{1,9},{5,13},{2,10},{6,14},{3,11},{7,15},{16,24},{20,... | collective-permute-start | bytes 786440 | tf_op jit(solution)/shard_map/ppermute | solution.py:99
  6.1 26.1 %collective-permute-start.2 = (bf16[2,256,256]{2,1,0:T(8,128)(2,1)S(1)}, bf16[2,256,256]{2,1,0:T(8,128)(2,1)S(1)}, u32[]{:S(2)}, u32[]{:S(2)}) collective-permute-start(bf16[2,256,256]{2,1,0:T(8,128)(2,1)S(1)} %pad_maximum_fusion.1.refs_3_), channel_id=1, source_target_pairs={{0,4},{4,8},{8,12},{1,5},{5,9},{9,13},{2,6},{6,10},{10,14},{3,7},{... | collective-permute-start | bytes 786440 | tf_op jit(solution)/shard_map/ppermute | solution.py:99
  22.1 12.1 %copy-start.2 = (bf16[2,256,256]{2,1,0:T(8,128)(2,1)}, bf16[2,256,256]{2,1,0:T(8,128)(2,1)S(1)}, u32[]{:S(2)}) copy-start(bf16[2,256,256]{2,1,0:T(8,128)(2,1)S(1)} %collective-permute-done.1.refs_1_) | copy-start | bytes 786436
  32.2 2.1 %copy-start.3 = (bf16[2,256,256]{2,1,0:T(8,128)(2,1)}, bf16[2,256,256]{2,1,0:T(8,128)(2,1)S(1)}, u32[]{:S(2)}) copy-start(bf16[2,256,256]{2,1,0:T(8,128)(2,1)S(1)} %collective-permute-done.2.refs_2_) | copy-start | bytes 786436

commit v10 on v9

--- a/solution.py
+++ b/solution.py
@@ -33,6 +33,23 @@
         ],
         axis=-1,
     )
+
+
+def rotate_flat(field, positions):
+    rows, width = field.shape
+    half_dim = HD // 2
+    frequency = jnp.exp(
+        jnp.arange(half_dim, dtype=jnp.float32) * (-2.0 * math.log(rope_base) / HD)
+    )
+    angles = positions.astype(jnp.float32)[:, None] * frequency[None, :]
+    cosine = jnp.cos(angles)
+    sine_part = jnp.sin(angles)
+    heads = width // HD
+    cos_full = jnp.tile(jnp.concatenate([cosine, cosine], axis=1), (1, heads))
+    sin_signed = jnp.tile(jnp.concatenate([-sine_part, sine_part], axis=1), (1, heads))
+    wide = field.astype(jnp.float32)
+    swapped = jnp.roll(wide.reshape(rows, heads, HD), half_dim, axis=-1).reshape(rows, width)
+    return wide * cos_full + swapped * sin_signed
 
 
 def attend_kernel(scalars, q_ref, *refs, rows, span, group, nparts):
@@ -113,12 +130,8 @@
     positions = first_pos + jnp.arange(shard_rows, dtype=jnp.int32)
     rotated_q = rotate(queries[0].reshape(shard_rows, heads_dev, HD).astype(jnp.float32), positions)
     rotated_q = rotated_q.astype(jnp.bfloat16).reshape(shard_rows, heads_dev * HD)
-    rotated_k = rotate(
-        keys_values[0, 0].reshape(shard_rows, kv_heads_dev, HD).astype(jnp.float32), positions
-    )
-    own_block = jnp.stack(
-        [rotated_k.astype(jnp.bfloat16).reshape(shard_rows, width), keys_values[0, 1]]
-    )
+    rotated_k = rotate_flat(keys_values[0, 0], positions)
+    own_block = jnp.stack([rotated_k.astype(jnp.bfloat16), keys_values[0, 1]])
     reach_count = min(WINDOW // shard_rows, seq_count - 1)
     span = (reach_count + 1) * shard_rows
     slot_rows = WINDOW // seq_count

time: 45.9 us -> 46.3 us (level)
  local copies, waits for them, and re-layouts: 1.96 us -> 2.73 us
  other arithmetic: 6.77 us -> 6.3 us
    neg x0 -> x1, other arithmetic: none -> 0.54 us  [rotate_flat(): -sine_part]
    cos x1 -> x0, other arithmetic: 0.53 us -> none  [rotate(): cosine = jnp.cos(angles)[:, None, :]]
    another operation x3 -> x2, other arithmetic: 1.27 us -> 0.79 us
    concatenate x2 -> x1, other arithmetic: 0.94 us -> 0.58 us  [rotate(): jnp.concatenate([lower_half * cosine - upper_half * sine_part, upper_half...]
    convert_element_type x1 -> x2, other arithmetic: 1.08 us -> 1.04 us  [the longest x1 1 us: rotate_flat(): wide = field.astype(jnp.float32)]
    unnamed x10 -> x12, local copies, waits for them, and re-layouts: 1.65 us -> 1.65 us
where the time goes in v10:
time: 46.3 us; the launch traced here: 45.9 us
  waiting for transfers between devices  18.1 us (39%)
  Pallas kernels  11.2 us (24%)
  other arithmetic  6.3 us (14%)
  starting transfers between devices  6.08 us (13%)
  local copies, waits for them, and re-layouts  2.73 us (6%)
  between operations  1.49 us (3%)
    ppermute x3, waiting for transfers between devices, passed_along(): return lax.ppermute(x, 'seq', pairs)  18.1 us
    pallas_call x1, Pallas kernels, attention(): pl.pallas_call(kernel, grid_spec=grid_spec, out_shape=jax.ShapeDtypeStruc...  11.2 us
    ppermute x3, starting transfers between devices, passed_along(): return lax.ppermute(x, 'seq', pairs)  6.08 us
    broadcast_in_dim x1, other arithmetic, local(): return (attended, window_cache[None])  2.05 us
    unnamed x12, local copies, waits for them, and re-layouts  1.65 us
    convert_element_type x1, other arithmetic, rotate_flat(): wide = field.astype(jnp.float32)  1 us
  transfers between devices with their start and end apart: 3, of which 2 were waited for; matrix products, arithmetic and copies ran while one was open for 13% of the time, Pallas kernels for 0%

profile of v10, /device:TPU:20, one launch (start us, length us, event | category | flops | bytes accessed | tf_op | source)
XLA Modules:
  0.0 45.9 jit_solution(4044426522344108163)
XLA Ops:
  0.7 1.0 %slice_convert_fusion = (f32[1,1,256,256]{3,2,1,0:T(8,128)S(1)}, bf16[1,256,256]{2,1,0:T(8,128)(2,1)S(1)}) fusion(bf16[1,2,256,256]{3,2,1,0:T(8,128)(2,1)} %param.4), kind=kLoop, calls=%fused_computation.24 | loop fusion | flops 65536 | bytes 655360 | tf_op jit(solution)/shard_map/convert_element_type | solution.py:50
  1.7 0.1 reshape.137
  1.8 0.0 copy-start.4
  1.8 0.3 fusion.8
  2.2 0.5 %fusion.7 = (f32[256,64]{1,0:T(8,128)S(1)}, f32[256,64]{1,0:T(8,128)S(1)}, f32[256,64]{1,0:T(8,128)S(1)}) fusion(f32[64]{0:T(128)S(1)} %multiply_exponential_fusion, f32[256]{0:T(256)S(1)} %add_convert_fusion.1), kind=kLoop, calls=%fused_computation.25 | loop fusion | flops 32768 | bytes 197888 | tf_op jit(solution)/shard_map/neg | solution.py:49
  2.7 0.0 copy-start
  2.7 0.1 pad_maximum_fusion.2
  2.9 0.4 maximum_multiply_fusion
  3.2 0.2 mul.105
  3.4 0.1 tile.6
  3.5 0.2 tile.7
  3.7 0.0 copy-done.4
  3.8 0.0 copy-start.1
  3.9 1.4 %collective-permute-start = (bf16[2,256,256]{2,1,0:T(8,128)(2,1)S(1)}, bf16[2,256,256]{2,1,0:T(8,128)(2,1)}, u32[]{:S(2)}, u32[]{:S(2)}) collective-permute-start(bf16[2,256,256]{2,1,0:T(8,128)(2,1)S(1)} %pad_maximum_fusion.1.refs_3_), channel_id=1, source_target_pairs={{0,12},{1,13},{2,14},{3,15},{16,28},{17,29},{18,30},{19,31}} | collective-permute-start | bytes 786440 | tf_op jit(solution)/shard_map/ppermute | solution.py:116
  5.2 1.3 %collective-permute-start.1 = (bf16[2,256,256]{2,1,0:T(8,128)(2,1)S(1)}, bf16[2,256,256]{2,1,0:T(8,128)(2,1)S(1)}, u32[]{:S(2)}, u32[]{:S(2)}) collective-permute-start(bf16[2,256,256]{2,1,0:T(8,128)(2,1)S(1)} %pad_maximum_fusion.1.refs_3_), channel_id=1, source_target_pairs={{0,8},{4,12},{1,9},{5,13},{2,10},{6,14},{3,11},{7,15},{16,24},{20,... | collective-permute-start | bytes 786440 | tf_op jit(solution)/shard_map/ppermute | solution.py:116
  6.5 3.4 %collective-permute-start.2 = (bf16[2,256,256]{2,1,0:T(8,128)(2,1)S(1)}, bf16[2,256,256]{2,1,0:T(8,128)(2,1)S(1)}, u32[]{:S(2)}, u32[]{:S(2)}) collective-permute-start(bf16[2,256,256]{2,1,0:T(8,128)(2,1)S(1)} %pad_maximum_fusion.1.refs_3_), channel_id=1, source_target_pairs={{0,4},{4,8},{8,12},{1,5},{5,9},{9,13},{2,6},{6,10},{10,14},{3,7},{... | collective-permute-start | bytes 786440 | tf_op jit(solution)/shard_map/ppermute | solution.py:116
  10.6 0.0 copy-done
  10.6 0.2 convert_bitcast_fusion
  10.9 0.4 copy.5
  11.2 0.0 copy-done.1
  11.3 0.8 %subtract_convert_fusion = (bf16[256,16,64]{2,1,0:T(8,128)(2,1)S(1)}, bf16[256,16,64]{2,1,0:T(8,128)(2,1)S(1)}) fusion(f32[256,16,128]{2,1,0:T(8,128)S(1)} %bitcast.24, f32[256,64]{1,0:T(8,128)S(1)} %get-tuple-element.9, f32[256,64]{1,0:T(8,128)S(1)} %get-tuple-element.10), kind=kLoop, calls=%fused_computation.2 | loop fusion | flops 2097152 | bytes 3276800 | tf_op jit(solution)/shard_map/convert.3
  12.1 0.1 pad_dynamic-slice_fusion.4
  12.1 0.6 %pad_maximum_fusion = bf16[256,16,128]{2,1,0:T(8,128)(2,1)S(1)} fusion(bf16[256,16,64]{2,1,0:T(8,128)(2,1)S(1)} %get-tuple-element.3, bf16[256,16,64]{2,1,0:T(8,128)(2,1)S(1)} %get-tuple-element.2), kind=kLoop, calls=%fused_computation.8 | loop fusion | flops 2097152 | bytes 2097152 | tf_op jit(solution)/shard_map/concatenate | solution.py:29
  12.7 0.6 %pad_add_fusion.scalars = s32[4]{0:T(128)} fusion(s32[1]{0:T(128)} %bitcast.1, s32[1]{0:T(128)} %constant.20.clone.1, s32[1]{0:T(128)} %bitcast, s32[1]{0:T(128)S(6)} %copy.9), kind=kLoop, calls=%fused_computation.28 | loop fusion | flops 12 | bytes 32 | tf_op jit(solution)/shard_map/stack | solution.py:164
  13.3 1.2 %copy.8 = bf16[32,8,16,128]{3,1,2,0:T(8,128)(2,1)} copy(bf16[32,8,16,128]{3,2,1,0:T(8,128)(2,1)S(1)} %bitcast.25) | data formatting | bytes 2097152
  14.5 8.0 %collective-permute-done.1.refs_1_ = bf16[2,256,256]{2,1,0:T(8,128)(2,1)S(1)} collective-permute-done((bf16[2,256,256]{2,1,0:T(8,128)(2,1)S(1)}, bf16[2,256,256]{2,1,0:T(8,128)(2,1)S(1)}, u32[]{:S(2)}, u32[]{:S(2)}) %collective-permute-start.1) | collective-permute-done | bytes 262176 | tf_op jit(solution)/shard_map/ppermute | solution.py:116
  22.6 10.0 %collective-permute-done.2.refs_2_ = bf16[2,256,256]{2,1,0:T(8,128)(2,1)S(1)} collective-permute-done((bf16[2,256,256]{2,1,0:T(8,128)(2,1)S(1)}, bf16[2,256,256]{2,1,0:T(8,128)(2,1)S(1)}, u32[]{:S(2)}, u32[]{:S(2)}) %collective-permute-start.2) | collective-permute-done | bytes 262176 | tf_op jit(solution)/shard_map/ppermute | solution.py:116
  32.6 2.0 %fusion.3 = bf16[1,2,512,256]{3,2,1,0:T(8,128)(2,1)} fusion(s32[]{:T(128)S(6)} %max.3, bf16[2,256,256]{2,1,0:T(8,128)(2,1)S(1)} %collective-permute-done.1.refs_1_, bf16[2,256,256]{2,1,0:T(8,128)(2,1)S(1)} %collective-permute-done.2.refs_2_, bf16[1,256,256]{2,1,0:T(8,128)(2,1)S(1)} %fusion.6, bf16[1,256,256]{2,1,0:T(8,128)(2,1)S(1)} %get-tuple-element.7, ...), kind=kLoop, calls=%fused_computation.12 | loop fusion | flops 2621440 | bytes 1311748 | tf_op jit(solution)/shard_map/broadcast_in_dim | solution.py:171
  34.7 0.0 collective-permute-done.refs_0_
  34.7 0.0 copy-done.2
  34.7 0.0 copy-done.3
  34.7 11.2 %shard_map.50 = bf16[256,2048]{1,0:T(8,128)(2,1)} custom-call(s32[4]{0:T(128)} %pad_add_fusion.scalars, bf16[256,2048]{1,0:T(8,128)(2,1)} %bitcast.26, bf16[2,256,256]{2,1,0:T(8,128)(2,1)} %collective-permute-done.refs_0_, bf16[2,256,256]{2,1,0:T(8,128)(2,1)} %copy-done.2, bf16[2,256,256]{2,1,0:T(8,128)(2,1)} %copy-done.3, bf16[2,256,256]{2,1,0:T(8,128)(2,1)} %copy-done.1), custom_call_target="tpu_custom_call" | custom-call | tf_op jit(solution)/shard_map/pallas_call | solution.py:106
  (7 shorter events, 0.1 us)
Async XLA Ops:
  1.8 1.9 %copy-start.4 = (bf16[1,2,256,256]{3,2,1,0:T(8,128)(2,1)S(1)}, bf16[1,2,256,256]{3,2,1,0:T(8,128)(2,1)}, u32[]{:S(2)}) copy-start(bf16[1,2,256,256]{3,2,1,0:T(8,128)(2,1)} %param.4) | copy-start | bytes 786436
  2.7 7.9 %copy-start = (bf16[1,256,2048]{2,1,0:T(8,128)(2,1)S(1)}, bf16[1,256,2048]{2,1,0:T(8,128)(2,1)}, u32[]{:S(2)}) copy-start(bf16[1,256,2048]{2,1,0:T(8,128)(2,1)} %param.3) | copy-start | bytes 3145732
  3.8 7.4 %copy-start.1 = (bf16[2,256,256]{2,1,0:T(8,128)(2,1)}, bf16[2,256,256]{2,1,0:T(8,128)(2,1)S(1)}, u32[]{:S(2)}) copy-start(bf16[2,256,256]{2,1,0:T(8,128)(2,1)S(1)} %pad_maximum_fusion.1.refs_3_) | copy-start | bytes 786436
  3.9 30.8 %collective-permute-start = (bf16[2,256,256]{2,1,0:T(8,128)(2,1)S(1)}, bf16[2,256,256]{2,1,0:T(8,128)(2,1)}, u32[]{:S(2)}, u32[]{:S(2)}) collective-permute-start(bf16[2,256,256]{2,1,0:T(8,128)(2,1)S(1)} %pad_maximum_fusion.1.refs_3_), channel_id=1, source_target_pairs={{0,12},{1,13},{2,14},{3,15},{16,28},{17,29},{18,30},{19,31}} | collective-permute-start | bytes 786440 | tf_op jit(solution)/shard_map/ppermute | solution.py:116
  5.2 17.3 %collective-permute-start.1 = (bf16[2,256,256]{2,1,0:T(8,128)(2,1)S(1)}, bf16[2,256,256]{2,1,0:T(8,128)(2,1)S(1)}, u32[]{:S(2)}, u32[]{:S(2)}) collective-permute-start(bf16[2,256,256]{2,1,0:T(8,128)(2,1)S(1)} %pad_maximum_fusion.1.refs_3_), channel_id=1, source_target_pairs={{0,8},{4,12},{1,9},{5,13},{2,10},{6,14},{3,11},{7,15},{16,24},{20,... | collective-permute-start | bytes 786440 | tf_op jit(solution)/shard_map/ppermute | solution.py:116
  6.5 26.1 %collective-permute-start.2 = (bf16[2,256,256]{2,1,0:T(8,128)(2,1)S(1)}, bf16[2,256,256]{2,1,0:T(8,128)(2,1)S(1)}, u32[]{:S(2)}, u32[]{:S(2)}) collective-permute-start(bf16[2,256,256]{2,1,0:T(8,128)(2,1)S(1)} %pad_maximum_fusion.1.refs_3_), channel_id=1, source_target_pairs={{0,4},{4,8},{8,12},{1,5},{5,9},{9,13},{2,6},{6,10},{10,14},{3,7},{... | collective-permute-start | bytes 786440 | tf_op jit(solution)/shard_map/ppermute | solution.py:116
  22.6 12.1 %copy-start.2 = (bf16[2,256,256]{2,1,0:T(8,128)(2,1)}, bf16[2,256,256]{2,1,0:T(8,128)(2,1)S(1)}, u32[]{:S(2)}) copy-start(bf16[2,256,256]{2,1,0:T(8,128)(2,1)S(1)} %collective-permute-done.1.refs_1_) | copy-start | bytes 786436
  32.6 2.1 %copy-start.3 = (bf16[2,256,256]{2,1,0:T(8,128)(2,1)}, bf16[2,256,256]{2,1,0:T(8,128)(2,1)S(1)}, u32[]{:S(2)}) copy-start(bf16[2,256,256]{2,1,0:T(8,128)(2,1)S(1)} %collective-permute-done.2.refs_2_) | copy-start | bytes 786436

commit v11 on v9

--- a/solution.py
+++ b/solution.py
@@ -35,9 +35,12 @@
     )
 
 
-def attend_kernel(scalars, q_ref, *refs, rows, span, group, nparts):
+def attend_kernel(scalars, q_ref, *refs, rows, span, group, nparts, slots):
     part_refs = refs[:nparts]
-    o_ref, bias_ref = refs[nparts:]
+    if slots:
+        o_ref, cache_ref, bias_ref = refs[nparts:]
+    else:
+        o_ref, bias_ref = refs[nparts:]
     seq_len = scalars[0]
     first_pos = scalars[1]
     key_start = pl.multiple_of(scalars[2], 256)
@@ -56,6 +59,12 @@
     else:
         k = jnp.concatenate([p[0] for p in part_refs], axis=0)
         v = jnp.concatenate([p[1] for p in part_refs], axis=0)
+    if slots:
+        slot_pos = scalars[4] + lax.broadcasted_iota(jnp.int32, (slots, span), 0)
+        held_pos = scalars[3] + lax.broadcasted_iota(jnp.int32, (slots, span), 1)
+        pick = ((held_pos == slot_pos) & (slot_pos >= 0)).astype(jnp.bfloat16)
+        cache_ref[0] = jnp.dot(pick, k, preferred_element_type=jnp.float32).astype(cache_ref.dtype)
+        cache_ref[1] = jnp.dot(pick, v, preferred_element_type=jnp.float32).astype(cache_ref.dtype)
     valid = (first_pos + lax.broadcasted_iota(jnp.int32, (rows, 1), 0)) < seq_len
     scale = 1.0 / math.sqrt(HD)
     for head in range(group):
@@ -71,26 +80,32 @@
         o_ref[:, cols] = jnp.where(valid, numer / denom, 0.0).astype(o_ref.dtype)
 
 
-def attention(scalars, rotated_q, parts, kv_heads_dev, group_size, span):
+def attention(scalars, rotated_q, parts, kv_heads_dev, group_size, span, slots):
     rows = rotated_q.shape[0]
     nparts = len(parts)
     kernel = functools.partial(
-        attend_kernel, rows=rows, span=span, group=group_size, nparts=nparts
+        attend_kernel, rows=rows, span=span, group=group_size, nparts=nparts, slots=slots
     )
     width = group_size * HD
+    out_specs = pl.BlockSpec((rows, width), lambda j, s: (0, j))
+    out_shape = jax.ShapeDtypeStruct((rows, kv_heads_dev * width), jnp.bfloat16)
+    if slots:
+        out_specs = [out_specs, pl.BlockSpec((2, slots, HD), lambda j, s: (0, 0, j))]
+        out_shape = [
+            out_shape,
+            jax.ShapeDtypeStruct((2, slots, kv_heads_dev * HD), jnp.bfloat16),
+        ]
     grid_spec = pltpu.PrefetchScalarGridSpec(
         num_scalar_prefetch=1,
         grid=(kv_heads_dev,),
         in_specs=[pl.BlockSpec((rows, width), lambda j, s: (0, j))]
         + [pl.BlockSpec((2, p.shape[1], HD), lambda j, s: (0, 0, j)) for p in parts],
-        out_specs=pl.BlockSpec((rows, width), lambda j, s: (0, j)),
+        out_specs=out_specs,
         scratch_shapes=[pltpu.VMEM((rows, span), jnp.float32)],
     )
-    return pl.pallas_call(
-        kernel,
-        grid_spec=grid_spec,
-        out_shape=jax.ShapeDtypeStruct((rows, kv_heads_dev * width), jnp.bfloat16),
-    )(scalars, rotated_q, *parts)
+    return pl.pallas_call(kernel, grid_spec=grid_spec, out_shape=out_shape)(
+        scalars, rotated_q, *parts
+    )
 
 
 def passed_along(x, by):
@@ -129,16 +144,6 @@
         parts = shifted
         key_index = jnp.zeros((), jnp.int32)
         key_first = first_pos - reach_count * shard_rows
-        shortest = min(WINDOW, tokens - shard_rows) + 1
-        cache_hops = 0
-        for index in range(seq_count):
-            if tokens - WINDOW + (index + 1) * slot_rows - 1 < 0:
-                continue
-            lowest = max(0, (shortest - WINDOW + index * slot_rows) // shard_rows)
-            cache_hops = max(cache_hops, index - lowest)
-        cache_hops = min(cache_hops, reach_count)
-        held = jnp.concatenate(shifted[reach_count - cache_hops:], axis=1)
-        held_first = first_pos - cache_hops * shard_rows
     else:
         outbox = jnp.broadcast_to(own_block[:, None], (2, seq_count, shard_rows, width))
         held = lax.all_to_all(
@@ -148,13 +153,18 @@
         held_first = 0
         key_index = jnp.maximum(first_pos - reach_count * shard_rows, 0)
         key_first = key_index
-    scalars = jnp.stack([seq_len, first_pos, key_index, key_first]).astype(jnp.int32)
-    attended = attention(scalars, rotated_q, parts, kv_heads_dev, group_size, span)
+    slot_first = seq_len - WINDOW + seq_index * slot_rows
+    scalars = jnp.stack([seq_len, first_pos, key_index, key_first, slot_first]).astype(jnp.int32)
+    if WINDOW >= tokens:
+        attended, window_cache = attention(
+            scalars, rotated_q, parts, kv_heads_dev, group_size, span, slot_rows
+        )
+    else:
+        attended = attention(scalars, rotated_q, parts, kv_heads_dev, group_size, span, 0)
+        padded = jnp.concatenate([jnp.zeros((2, slot_rows, width), jnp.bfloat16), held], axis=1)
+        begin_row = slot_first - held_first + slot_rows
+        window_cache = lax.dynamic_slice_in_dim(padded, jnp.maximum(begin_row, 0), slot_rows, 1)
     attended = attended.reshape(1, shard_rows, heads_dev * HD)
-
-    padded = jnp.concatenate([jnp.zeros((2, slot_rows, width), jnp.bfloat16), held], axis=1)
-    begin_row = seq_len - WINDOW - held_first + seq_index * slot_rows + slot_rows
-    window_cache = lax.dynamic_slice_in_dim(padded, jnp.maximum(begin_row, 0), slot_rows, 1)
     return (attended, window_cache[None])
 
 

time: 45.9 us -> 45.6 us (level)
  other arithmetic: 6.77 us -> 4.07 us
  local copies, waits for them, and re-layouts: 1.96 us -> 3.17 us
  Pallas kernels: 11.2 us -> 12.3 us
    broadcast_in_dim x1 -> x0, other arithmetic: 2.05 us -> none  [local(): return (attended, window_cache[None])]
    pallas_call x1, Pallas kernels: 11.2 us -> 12.3 us  [attention(): pl.pallas_call(kernel, grid_spec=grid_spec, out_shape=out_shape)]
    unnamed x10 -> x12, local copies, waits for them, and re-layouts: 1.65 us -> 2.37 us
    another operation x3 -> x2, other arithmetic: 1.9 us -> 1.24 us
    another operation x0 -> x1, local copies, waits for them, and re-layouts: none -> 0.57 us  [local(): jnp.stack([seq_len, first_pos, key_index, key_first, slot_first])]
  transfers between devices with their start and end apart: 3 -> 3, of which waited for: 2 -> 2; matrix products, arithmetic and copies ran while one was open for 13% -> 8% of each run, Pallas kernels for 0% -> 0%
where the time goes in v11:
time: 45.6 us; the launch traced here: 45.2 us
  waiting for transfers between devices  18.2 us (40%)
  Pallas kernels  12.3 us (27%)
  starting transfers between devices  6.07 us (13%)
  other arithmetic  4.07 us (9%)
  local copies, waits for them, and re-layouts  3.17 us (7%)
  between operations  1.44 us (3%)
    ppermute x3, waiting for transfers between devices, passed_along(): return lax.ppermute(x, 'seq', pairs)  18.2 us
    pallas_call x1, Pallas kernels, attention(): pl.pallas_call(kernel, grid_spec=grid_spec, out_shape=out_shape)  12.3 us
    ppermute x3, starting transfers between devices, passed_along(): return lax.ppermute(x, 'seq', pairs)  6.07 us
    unnamed x12, local copies, waits for them, and re-layouts  2.37 us
    another operation x2, other arithmetic  1.24 us
    convert_element_type x1, other arithmetic, local(): keys_values[0, 0].reshape(shard_rows, kv_heads_dev, HD).astype(jnp.float32)  1.08 us
    concatenate x2, other arithmetic, rotate(): jnp.concatenate([lower_half * cosine - upper_half * sine_part, upper_half...  0.94 us
  transfers between devices with their start and end apart: 3, of which 2 were waited for; matrix products, arithmetic and copies ran while one was open for 8% of the time, Pallas kernels for 0%

profile of v11, /device:TPU:20, one launch (start us, length us, event | category | flops | bytes accessed | tf_op | source)
XLA Modules:
  0.0 45.2 jit_solution(17517672460763562978)
XLA Ops:
  0.6 0.0 copy-start
  0.7 1.1 %slice_convert_fusion = (f32[1,1,256,256]{3,2,1,0:T(8,128)S(1)}, bf16[1,256,256]{2,1,0:T(8,128)(2,1)S(1)}) fusion(bf16[1,2,256,256]{3,2,1,0:T(8,128)(2,1)} %param.4), kind=kLoop, calls=%fused_computation.12 | loop fusion | flops 65536 | bytes 655360 | tf_op jit(solution)/shard_map/convert_element_type | solution.py:132
  1.8 0.1 reshape.86
  1.9 0.5 %multiply_cosine_fusion = (f32[256,64]{1,0:T(8,128)S(1)}, f32[256,64]{1,0:T(8,128)S(1)}) fusion(f32[64]{0:T(128)S(1)} %multiply_exponential_fusion, f32[256]{0:T(256)S(1)} %add_convert_fusion.2), kind=kLoop, calls=%fused_computation.9 | loop fusion | flops 16384 | bytes 132352 | tf_op jit(solution)/shard_map/cos | solution.py:25
  2.4 0.5 %subtract_convert_fusion.1 = (bf16[256,2,64]{2,1,0:T(2,128)(2,1)S(1)}, bf16[256,2,64]{2,1,0:T(2,128)(2,1)S(1)}) fusion(f32[256,2,128]{2,1,0:T(2,128)S(1)} %reshape.86, f32[256,64]{1,0:T(8,128)S(1)} %get-tuple-element.13, f32[256,64]{1,0:T(8,128)S(1)} %get-tuple-element.12), kind=kLoop, calls=%fused_computation.7 | loop fusion | flops 262144 | bytes 524288 | tf_op jit(solution)/shard_map/convert.2
  2.9 0.4 pad_maximum_fusion.2
  3.3 0.1 convert_element_type.42
  3.4 0.0 copy-start.1
  3.4 0.7 %collective-permute-start = (bf16[2,256,256]{2,1,0:T(8,128)(2,1)S(1)}, bf16[2,256,256]{2,1,0:T(8,128)(2,1)S(1)}, u32[]{:S(2)}, u32[]{:S(2)}) collective-permute-start(bf16[2,256,256]{2,1,0:T(8,128)(2,1)S(1)} %pad_maximum_fusion.1.refs_3_), channel_id=1, source_target_pairs={{0,12},{1,13},{2,14},{3,15},{16,28},{17,29},{18,30},{19,31}} | collective-permute-start | bytes 786440 | tf_op jit(solution)/shard_map/ppermute | solution.py:114
  4.1 1.3 %collective-permute-start.1 = (bf16[2,256,256]{2,1,0:T(8,128)(2,1)S(1)}, bf16[2,256,256]{2,1,0:T(8,128)(2,1)S(1)}, u32[]{:S(2)}, u32[]{:S(2)}) collective-permute-start(bf16[2,256,256]{2,1,0:T(8,128)(2,1)S(1)} %pad_maximum_fusion.1.refs_3_), channel_id=1, source_target_pairs={{0,8},{4,12},{1,9},{5,13},{2,10},{6,14},{3,11},{7,15},{16,24},{20,... | collective-permute-start | bytes 786440 | tf_op jit(solution)/shard_map/ppermute | solution.py:114
  5.4 4.1 %collective-permute-start.2 = (bf16[2,256,256]{2,1,0:T(8,128)(2,1)S(1)}, bf16[2,256,256]{2,1,0:T(8,128)(2,1)S(1)}, u32[]{:S(2)}, u32[]{:S(2)}) collective-permute-start(bf16[2,256,256]{2,1,0:T(8,128)(2,1)S(1)} %pad_maximum_fusion.1.refs_3_), channel_id=1, source_target_pairs={{0,4},{4,8},{8,12},{1,5},{5,9},{9,13},{2,6},{6,10},{10,14},{3,7},{... | collective-permute-start | bytes 786440 | tf_op jit(solution)/shard_map/ppermute | solution.py:114
  9.5 0.0 copy-done
  9.5 0.2 convert_bitcast_fusion
  9.8 0.4 copy.5
  10.2 0.0 copy-done.1
  10.2 0.8 %subtract_convert_fusion = (bf16[256,16,64]{2,1,0:T(8,128)(2,1)S(1)}, bf16[256,16,64]{2,1,0:T(8,128)(2,1)S(1)}) fusion(f32[256,16,128]{2,1,0:T(8,128)S(1)} %bitcast.18, f32[256,64]{1,0:T(8,128)S(1)} %get-tuple-element.13, f32[256,64]{1,0:T(8,128)S(1)} %get-tuple-element.12), kind=kLoop, calls=%fused_computation.2 | loop fusion | flops 2097152 | bytes 3276800 | tf_op jit(solution)/shard_map/convert.4
  11.6 0.6 %pad_maximum_fusion = bf16[256,16,128]{2,1,0:T(8,128)(2,1)S(1)} fusion(bf16[256,16,64]{2,1,0:T(8,128)(2,1)S(1)} %get-tuple-element.7, bf16[256,16,64]{2,1,0:T(8,128)(2,1)S(1)} %get-tuple-element.6), kind=kLoop, calls=%fused_computation.4 | loop fusion | flops 2097152 | bytes 2097152 | tf_op jit(solution)/shard_map/concatenate | solution.py:29
  12.2 1.2 %copy.8 = bf16[32,8,16,128]{3,1,2,0:T(8,128)(2,1)} copy(bf16[32,8,16,128]{3,2,1,0:T(8,128)(2,1)S(1)} %bitcast.19) | data formatting | bytes 2097152
  13.4 0.6 %stack.18.scalars = s32[5]{0:T(128)} concatenate(s32[1]{0:T(128)S(6)} %copy.9, s32[1]{0:T(128)} %bitcast, s32[1]{0:T(128)} %constant.15.clone.1, s32[1]{0:T(128)} %bitcast.1, s32[1]{0:T(128)} %bitcast.3), dimensions={0} | concatenate | bytes 40 | tf_op jit(solution)/shard_map/stack | solution.py:157
  14.0 0.0 collective-permute-done.refs_0_
  14.0 0.0 copy-start.2
  14.0 8.1 %collective-permute-done.1.refs_1_ = bf16[2,256,256]{2,1,0:T(8,128)(2,1)S(1)} collective-permute-done((bf16[2,256,256]{2,1,0:T(8,128)(2,1)S(1)}, bf16[2,256,256]{2,1,0:T(8,128)(2,1)S(1)}, u32[]{:S(2)}, u32[]{:S(2)}) %collective-permute-start.1) | collective-permute-done | bytes 262176 | tf_op jit(solution)/shard_map/ppermute | solution.py:114
  22.1 0.0 copy-start.3
  22.1 10.0 %collective-permute-done.2.refs_2_ = bf16[2,256,256]{2,1,0:T(8,128)(2,1)S(1)} collective-permute-done((bf16[2,256,256]{2,1,0:T(8,128)(2,1)S(1)}, bf16[2,256,256]{2,1,0:T(8,128)(2,1)S(1)}, u32[]{:S(2)}, u32[]{:S(2)}) %collective-permute-start.2) | collective-permute-done | bytes 262176 | tf_op jit(solution)/shard_map/ppermute | solution.py:114
  32.2 0.0 copy-start.4
  32.2 0.0 copy-done.2
  32.2 0.0 copy-done.3
  32.2 0.7 %copy-done.4 = bf16[2,256,256]{2,1,0:T(8,128)(2,1)} copy-done((bf16[2,256,256]{2,1,0:T(8,128)(2,1)}, bf16[2,256,256]{2,1,0:T(8,128)(2,1)S(1)}, u32[]{:S(2)}) %copy-start.4) | copy-done | bytes 262168
  32.9 12.3 %shard_map.50 = (bf16[256,2048]{1,0:T(8,128)(2,1)}, bf16[2,512,256]{2,1,0:T(8,128)(2,1)}) custom-call(s32[5]{0:T(128)} %stack.18.scalars, bf16[256,2048]{1,0:T(8,128)(2,1)} %bitcast.20, bf16[2,256,256]{2,1,0:T(8,128)(2,1)} %copy-done.2, bf16[2,256,256]{2,1,0:T(8,128)(2,1)} %copy-done.3, bf16[2,256,256]{2,1,0:T(8,128)(2,1)} %copy-done.4, ...), custom_call_target="tpu_custom_call" | custom-call | tf_op jit(solution)/shard_map/pallas_call | solution.py:106
  (3 shorter events, 0.0 us)
Async XLA Ops:
  0.6 8.9 %copy-start = (bf16[1,256,2048]{2,1,0:T(8,128)(2,1)S(1)}, bf16[1,256,2048]{2,1,0:T(8,128)(2,1)}, u32[]{:S(2)}) copy-start(bf16[1,256,2048]{2,1,0:T(8,128)(2,1)} %param.3) | copy-start | bytes 3145732
  3.4 6.8 %copy-start.1 = (bf16[2,256,256]{2,1,0:T(8,128)(2,1)}, bf16[2,256,256]{2,1,0:T(8,128)(2,1)S(1)}, u32[]{:S(2)}) copy-start(bf16[2,256,256]{2,1,0:T(8,128)(2,1)S(1)} %pad_maximum_fusion.1.refs_3_) | copy-start | bytes 786436
  3.4 10.6 %collective-permute-start = (bf16[2,256,256]{2,1,0:T(8,128)(2,1)S(1)}, bf16[2,256,256]{2,1,0:T(8,128)(2,1)S(1)}, u32[]{:S(2)}, u32[]{:S(2)}) collective-permute-start(bf16[2,256,256]{2,1,0:T(8,128)(2,1)S(1)} %pad_maximum_fusion.1.refs_3_), channel_id=1, source_target_pairs={{0,12},{1,13},{2,14},{3,15},{16,28},{17,29},{18,30},{19,31}} | collective-permute-start | bytes 786440 | tf_op jit(solution)/shard_map/ppermute | solution.py:114
  4.1 18.0 %collective-permute-start.1 = (bf16[2,256,256]{2,1,0:T(8,128)(2,1)S(1)}, bf16[2,256,256]{2,1,0:T(8,128)(2,1)S(1)}, u32[]{:S(2)}, u32[]{:S(2)}) collective-permute-start(bf16[2,256,256]{2,1,0:T(8,128)(2,1)S(1)} %pad_maximum_fusion.1.refs_3_), channel_id=1, source_target_pairs={{0,8},{4,12},{1,9},{5,13},{2,10},{6,14},{3,11},{7,15},{16,24},{20,... | collective-permute-start | bytes 786440 | tf_op jit(solution)/shard_map/ppermute | solution.py:114
  5.4 26.8 %collective-permute-start.2 = (bf16[2,256,256]{2,1,0:T(8,128)(2,1)S(1)}, bf16[2,256,256]{2,1,0:T(8,128)(2,1)S(1)}, u32[]{:S(2)}, u32[]{:S(2)}) collective-permute-start(bf16[2,256,256]{2,1,0:T(8,128)(2,1)S(1)} %pad_maximum_fusion.1.refs_3_), channel_id=1, source_target_pairs={{0,4},{4,8},{8,12},{1,5},{5,9},{9,13},{2,6},{6,10},{10,14},{3,7},{... | collective-permute-start | bytes 786440 | tf_op jit(solution)/shard_map/ppermute | solution.py:114
  14.0 18.2 %copy-start.2 = (bf16[2,256,256]{2,1,0:T(8,128)(2,1)}, bf16[2,256,256]{2,1,0:T(8,128)(2,1)S(1)}, u32[]{:S(2)}) copy-start(bf16[2,256,256]{2,1,0:T(8,128)(2,1)S(1)} %collective-permute-done.refs_0_) | copy-start | bytes 786436
  22.1 10.1 %copy-start.3 = (bf16[2,256,256]{2,1,0:T(8,128)(2,1)}, bf16[2,256,256]{2,1,0:T(8,128)(2,1)S(1)}, u32[]{:S(2)}) copy-start(bf16[2,256,256]{2,1,0:T(8,128)(2,1)S(1)} %collective-permute-done.1.refs_1_) | copy-start | bytes 786436
  32.2 0.7 %copy-start.4 = (bf16[2,256,256]{2,1,0:T(8,128)(2,1)}, bf16[2,256,256]{2,1,0:T(8,128)(2,1)S(1)}, u32[]{:S(2)}) copy-start(bf16[2,256,256]{2,1,0:T(8,128)(2,1)S(1)} %collective-permute-done.2.refs_2_) | copy-start | bytes 786436

commit v12 on v11

--- a/solution.py
+++ b/solution.py
@@ -65,30 +65,33 @@
         pick = ((held_pos == slot_pos) & (slot_pos >= 0)).astype(jnp.bfloat16)
         cache_ref[0] = jnp.dot(pick, k, preferred_element_type=jnp.float32).astype(cache_ref.dtype)
         cache_ref[1] = jnp.dot(pick, v, preferred_element_type=jnp.float32).astype(cache_ref.dtype)
-    valid = (first_pos + lax.broadcasted_iota(jnp.int32, (rows, 1), 0)) < seq_len
+    batch = 4 if group % 4 == 0 else 1
+    valid = (first_pos + lax.broadcasted_iota(jnp.int32, (batch, rows, 1), 1)) < seq_len
+    valid = valid.reshape(batch * rows, 1)
     scale = 1.0 / math.sqrt(HD)
-    for head in range(group):
-        cols = slice(head * HD, (head + 1) * HD)
+    for lead in range(0, group, batch):
+        heads = slice(lead * rows, (lead + batch) * rows)
         raw = lax.dot_general(
-            q_ref[:, cols], k, (((1,), (1,)), ((), ())), preferred_element_type=jnp.float32
-        ) + bias_ref[...]
+            q_ref[0, heads, :], k, (((1,), (1,)), ((), ())), preferred_element_type=jnp.float32
+        )
+        raw = (raw.reshape(batch, rows, span) + bias_ref[...][None]).reshape(batch * rows, span)
         row_top = jnp.max(raw, axis=-1, keepdims=True)
         weights = jnp.exp((raw - row_top) * scale)
         totals = jnp.sum(weights, axis=-1, keepdims=True)
         numer = jnp.dot(weights.astype(jnp.bfloat16), v, preferred_element_type=jnp.float32)
         denom = jnp.where(valid, totals, 1.0)
-        o_ref[:, cols] = jnp.where(valid, numer / denom, 0.0).astype(o_ref.dtype)
+        o_ref[0, heads, :] = jnp.where(valid, numer / denom, 0.0).astype(o_ref.dtype)
 
 
 def attention(scalars, rotated_q, parts, kv_heads_dev, group_size, span, slots):
-    rows = rotated_q.shape[0]
+    rows = rotated_q.shape[1] // group_size
     nparts = len(parts)
     kernel = functools.partial(
         attend_kernel, rows=rows, span=span, group=group_size, nparts=nparts, slots=slots
     )
     width = group_size * HD
-    out_specs = pl.BlockSpec((rows, width), lambda j, s: (0, j))
-    out_shape = jax.ShapeDtypeStruct((rows, kv_heads_dev * width), jnp.bfloat16)
+    out_specs = pl.BlockSpec((1, group_size * rows, HD), lambda j, s: (j, 0, 0))
+    out_shape = jax.ShapeDtypeStruct((kv_heads_dev, group_size * rows, HD), jnp.bfloat16)
     if slots:
         out_specs = [out_specs, pl.BlockSpec((2, slots, HD), lambda j, s: (0, 0, j))]
         out_shape = [
@@ -98,7 +101,7 @@
     grid_spec = pltpu.PrefetchScalarGridSpec(
         num_scalar_prefetch=1,
         grid=(kv_heads_dev,),
-        in_specs=[pl.BlockSpec((rows, width), lambda j, s: (0, j))]
+        in_specs=[pl.BlockSpec((1, group_size * rows, HD), lambda j, s: (j, 0, 0))]
         + [pl.BlockSpec((2, p.shape[1], HD), lambda j, s: (0, 0, j)) for p in parts],
         out_specs=out_specs,
         scratch_shapes=[pltpu.VMEM((rows, span), jnp.float32)],
@@ -127,7 +130,12 @@
     first_pos = seq_index * shard_rows
     positions = first_pos + jnp.arange(shard_rows, dtype=jnp.int32)
     rotated_q = rotate(queries[0].reshape(shard_rows, heads_dev, HD).astype(jnp.float32), positions)
-    rotated_q = rotated_q.astype(jnp.bfloat16).reshape(shard_rows, heads_dev * HD)
+    rotated_q = (
+        rotated_q.astype(jnp.bfloat16)
+        .reshape(shard_rows, kv_heads_dev, group_size, HD)
+        .transpose(1, 2, 0, 3)
+        .reshape(kv_heads_dev, group_size * shard_rows, HD)
+    )
     rotated_k = rotate(
         keys_values[0, 0].reshape(shard_rows, kv_heads_dev, HD).astype(jnp.float32), positions
     )
@@ -164,7 +172,11 @@
         padded = jnp.concatenate([jnp.zeros((2, slot_rows, width), jnp.bfloat16), held], axis=1)
         begin_row = slot_first - held_first + slot_rows
         window_cache = lax.dynamic_slice_in_dim(padded, jnp.maximum(begin_row, 0), slot_rows, 1)
-    attended = attended.reshape(1, shard_rows, heads_dev * HD)
+    attended = (
+        attended.reshape(kv_heads_dev, group_size, shard_rows, HD)
+        .transpose(2, 0, 1, 3)
+        .reshape(1, shard_rows, heads_dev * HD)
+    )
     return (attended, window_cache[None])
 
 

time: 45.6 us -> 48.4 us (1.061)
  local copies, waits for them, and re-layouts: 3.17 us -> 5 us
  other arithmetic: 4.07 us -> 5.04 us
    unnamed x12 -> x5, local copies, waits for them, and re-layouts: 2.37 us -> 0.39 us
    transpose x0 -> x1, local copies, waits for them, and re-layouts: none -> 1.9 us  [local(): attended = attended.reshape(kv_heads_dev, group_size, shard_rows, HD).tra...]
    reshape x0 -> x1, local copies, waits for them, and re-layouts: none -> 1.27 us  [local(): attended = attended.reshape(kv_heads_dev, group_size, shard_rows, HD).tra...]
    concatenate x2, other arithmetic: 0.94 us -> 1.91 us  [rotate(): jnp.concatenate([lower_half * cosine - upper_half * sine_part, upper_half...]
    another operation x0 -> x2, local copies, waits for them, and re-layouts: none -> 0.54 us
  transfers between devices with their start and end apart: 3 -> 3, of which waited for: 2 -> 2; matrix products, arithmetic and copies ran while one was open for 8% -> 9% of each run, Pallas kernels for 0% -> 0%
where the time goes in v12:
time: 48.4 us; the launch traced here: 47.9 us
  waiting for transfers between devices  17.9 us (37%)
  Pallas kernels  12.5 us (26%)
  starting transfers between devices  6.08 us (13%)
  other arithmetic  5.04 us (10%)
  local copies, waits for them, and re-layouts  5 us (10%)
  between operations  1.45 us (3%)
    ppermute x3, waiting for transfers between devices, passed_along(): return lax.ppermute(x, 'seq', pairs)  17.9 us
    pallas_call x1, Pallas kernels, attention(): pl.pallas_call(kernel, grid_spec=grid_spec, out_shape=out_shape)  12.5 us
    ppermute x3, starting transfers between devices, passed_along(): return lax.ppermute(x, 'seq', pairs)  6.08 us
    concatenate x2, other arithmetic, rotate(): jnp.concatenate([lower_half * cosine - upper_half * sine_part, upper_half...  1.91 us
    transpose x1, local copies, waits for them, and re-layouts, local(): attended = attended.reshape(kv_heads_dev, group_size, shard_rows, HD).tra...  1.9 us
    reshape x1, local copies, waits for them, and re-layouts, local(): attended = attended.reshape(kv_heads_dev, group_size, shard_rows, HD).tra...  1.27 us
    another operation x2, other arithmetic  1.24 us
    convert_element_type x1, other arithmetic, local(): keys_values[0, 0].reshape(shard_rows, kv_heads_dev, HD).astype(jnp.float32)  1.08 us
  transfers between devices with their start and end apart: 3, of which 2 were waited for; matrix products, arithmetic and copies ran while one was open for 9% of the time, Pallas kernels for 0%

profile of v12, /device:TPU:20, one launch (start us, length us, event | category | flops | bytes accessed | tf_op | source)
XLA Modules:
  0.0 47.9 jit_solution(4797145726170291436)
XLA Ops:
  0.6 0.0 copy-start
  0.7 1.1 %slice_convert_fusion = (f32[1,1,256,256]{3,2,1,0:T(8,128)S(1)}, bf16[1,256,256]{2,1,0:T(8,128)(2,1)S(1)}) fusion(bf16[1,2,256,256]{3,2,1,0:T(8,128)(2,1)} %param.4), kind=kLoop, calls=%fused_computation.11 | loop fusion | flops 65536 | bytes 655360 | tf_op jit(solution)/shard_map/convert_element_type | solution.py:140
  1.8 0.1 reshape.96
  1.9 0.5 %multiply_cosine_fusion = (f32[256,64]{1,0:T(8,128)S(1)}, f32[256,64]{1,0:T(8,128)S(1)}) fusion(f32[64]{0:T(128)S(1)} %multiply_exponential_fusion, f32[256]{0:T(256)S(1)} %add_convert_fusion.2), kind=kLoop, calls=%fused_computation.8 | loop fusion | flops 16384 | bytes 132352 | tf_op jit(solution)/shard_map/cos | solution.py:25
  2.4 0.5 subtract_convert_fusion.1
  2.9 0.4 pad_maximum_fusion.2
  3.3 0.1 convert_element_type.38
  3.4 0.0 copy-start.1
  3.4 1.4 %collective-permute-start = (bf16[2,256,256]{2,1,0:T(8,128)(2,1)S(1)}, bf16[2,256,256]{2,1,0:T(8,128)(2,1)}, u32[]{:S(2)}, u32[]{:S(2)}) collective-permute-start(bf16[2,256,256]{2,1,0:T(8,128)(2,1)S(1)} %pad_maximum_fusion.1.refs_3_), channel_id=1, source_target_pairs={{0,12},{1,13},{2,14},{3,15},{16,28},{17,29},{18,30},{19,31}} | collective-permute-start | bytes 786440 | tf_op jit(solution)/shard_map/ppermute | solution.py:117
  4.8 1.3 %collective-permute-start.1 = (bf16[2,256,256]{2,1,0:T(8,128)(2,1)S(1)}, bf16[2,256,256]{2,1,0:T(8,128)(2,1)}, u32[]{:S(2)}, u32[]{:S(2)}) collective-permute-start(bf16[2,256,256]{2,1,0:T(8,128)(2,1)S(1)} %pad_maximum_fusion.1.refs_3_), channel_id=1, source_target_pairs={{0,8},{4,12},{1,9},{5,13},{2,10},{6,14},{3,11},{7,15},{16,24},{20,... | collective-permute-start | bytes 786440 | tf_op jit(solution)/shard_map/ppermute | solution.py:117
  6.1 3.4 %collective-permute-start.2 = (bf16[2,256,256]{2,1,0:T(8,128)(2,1)S(1)}, bf16[2,256,256]{2,1,0:T(8,128)(2,1)}, u32[]{:S(2)}, u32[]{:S(2)}) collective-permute-start(bf16[2,256,256]{2,1,0:T(8,128)(2,1)S(1)} %pad_maximum_fusion.1.refs_3_), channel_id=1, source_target_pairs={{0,4},{4,8},{8,12},{1,5},{5,9},{9,13},{2,6},{6,10},{10,14},{3,7},{... | collective-permute-start | bytes 786440 | tf_op jit(solution)/shard_map/ppermute | solution.py:117
  9.5 0.0 copy-done
  9.5 0.2 convert_bitcast_fusion
  9.8 0.4 copy.8
  10.2 0.0 copy-done.1
  10.2 0.8 %subtract_convert_fusion = (bf16[256,16,64]{2,1,0:T(8,128)(2,1)S(1)}, bf16[256,16,64]{2,1,0:T(8,128)(2,1)S(1)}) fusion(f32[256,16,128]{2,1,0:T(8,128)S(1)} %bitcast.23, f32[256,64]{1,0:T(8,128)S(1)} %get-tuple-element.13, f32[256,64]{1,0:T(8,128)S(1)} %get-tuple-element.12), kind=kLoop, calls=%fused_computation.2 | loop fusion | flops 2097152 | bytes 3276800 | tf_op jit(solution)/shard_map/convert.7
  11.6 0.3 copy.6
  11.9 0.3 copy.5
  12.2 0.7 %stack.18.scalars = s32[5]{0:T(128)} concatenate(s32[1]{0:T(128)S(6)} %copy.9, s32[1]{0:T(128)} %bitcast, s32[1]{0:T(128)} %constant.15.clone.1, s32[1]{0:T(128)} %bitcast.1, s32[1]{0:T(128)} %bitcast.3), dimensions={0} | concatenate | bytes 40 | tf_op jit(solution)/shard_map/stack | solution.py:165
  12.8 1.5 %pad_maximum_fusion = bf16[256,2,8,128]{3,0,2,1:T(8,128)(2,1)} fusion(bf16[256,2,8,64]{3,0,2,1:T(8,128)(2,1)S(1)} %bitcast.25, bf16[256,2,8,64]{3,0,2,1:T(8,128)(2,1)S(1)} %bitcast.26), kind=kLoop, calls=%fused_computation.3 | loop fusion | flops 2097152 | bytes 2097152 | tf_op jit(solution)/shard_map/concatenate | solution.py:29
  14.4 0.0 collective-permute-done.refs_0_
  14.4 7.9 %collective-permute-done.1.refs_1_ = bf16[2,256,256]{2,1,0:T(8,128)(2,1)} collective-permute-done((bf16[2,256,256]{2,1,0:T(8,128)(2,1)S(1)}, bf16[2,256,256]{2,1,0:T(8,128)(2,1)}, u32[]{:S(2)}, u32[]{:S(2)}) %collective-permute-start.1) | collective-permute-done | bytes 262176 | tf_op jit(solution)/shard_map/ppermute | solution.py:117
  22.2 10.0 %collective-permute-done.2.refs_2_ = bf16[2,256,256]{2,1,0:T(8,128)(2,1)} collective-permute-done((bf16[2,256,256]{2,1,0:T(8,128)(2,1)S(1)}, bf16[2,256,256]{2,1,0:T(8,128)(2,1)}, u32[]{:S(2)}, u32[]{:S(2)}) %collective-permute-start.2) | collective-permute-done | bytes 262176 | tf_op jit(solution)/shard_map/ppermute | solution.py:117
  32.3 12.5 %shard_map.50 = (bf16[2,2048,128]{2,1,0:T(8,128)(2,1)}, bf16[2,512,256]{2,1,0:T(8,128)(2,1)}) custom-call(s32[5]{0:T(128)} %stack.18.scalars, bf16[2,2048,128]{2,1,0:T(8,128)(2,1)} %bitcast.24, bf16[2,256,256]{2,1,0:T(8,128)(2,1)} %collective-permute-done.refs_0_, bf16[2,256,256]{2,1,0:T(8,128)(2,1)} %collective-permute-done.1.refs_1_, ...), custom_call_target="tpu_custom_call" | custom-call | tf_op jit(solution)/shard_map/pallas_call | solution.py:109
  44.7 1.9 %copy.7 = bf16[256,2,8,128]{3,2,1,0:T(8,128)(2,1)S(1)} copy(bf16[256,2,8,128]{3,0,2,1:T(8,128)(2,1)} %bitcast.27) | data formatting | bytes 2097152 | tf_op jit(solution)/shard_map/transpose | solution.py:177
  46.6 1.3 %reshape.94 = bf16[1,256,2048]{2,1,0:T(8,128)(2,1)} reshape(bf16[256,2,8,128]{3,2,1,0:T(8,128)(2,1)S(1)} %copy.7) | data formatting | bytes 2097152 | tf_op jit(solution)/shard_map/reshape | solution.py:178
  (3 shorter events, 0.0 us)
Async XLA Ops:
  0.6 8.9 %copy-start = (bf16[1,256,2048]{2,1,0:T(8,128)(2,1)S(1)}, bf16[1,256,2048]{2,1,0:T(8,128)(2,1)}, u32[]{:S(2)}) copy-start(bf16[1,256,2048]{2,1,0:T(8,128)(2,1)} %param.3) | copy-start | bytes 3145732
  3.4 6.8 %copy-start.1 = (bf16[2,256,256]{2,1,0:T(8,128)(2,1)}, bf16[2,256,256]{2,1,0:T(8,128)(2,1)S(1)}, u32[]{:S(2)}) copy-start(bf16[2,256,256]{2,1,0:T(8,128)(2,1)S(1)} %pad_maximum_fusion.1.refs_3_) | copy-start | bytes 786436
  3.4 11.0 %collective-permute-start = (bf16[2,256,256]{2,1,0:T(8,128)(2,1)S(1)}, bf16[2,256,256]{2,1,0:T(8,128)(2,1)}, u32[]{:S(2)}, u32[]{:S(2)}) collective-permute-start(bf16[2,256,256]{2,1,0:T(8,128)(2,1)S(1)} %pad_maximum_fusion.1.refs_3_), channel_id=1, source_target_pairs={{0,12},{1,13},{2,14},{3,15},{16,28},{17,29},{18,30},{19,31}} | collective-permute-start | bytes 786440 | tf_op jit(solution)/shard_map/ppermute | solution.py:117
  4.8 17.4 %collective-permute-start.1 = (bf16[2,256,256]{2,1,0:T(8,128)(2,1)S(1)}, bf16[2,256,256]{2,1,0:T(8,128)(2,1)}, u32[]{:S(2)}, u32[]{:S(2)}) collective-permute-start(bf16[2,256,256]{2,1,0:T(8,128)(2,1)S(1)} %pad_maximum_fusion.1.refs_3_), channel_id=1, source_target_pairs={{0,8},{4,12},{1,9},{5,13},{2,10},{6,14},{3,11},{7,15},{16,24},{20,... | collective-permute-start | bytes 786440 | tf_op jit(solution)/shard_map/ppermute | solution.py:117
  6.1 26.2 %collective-permute-start.2 = (bf16[2,256,256]{2,1,0:T(8,128)(2,1)S(1)}, bf16[2,256,256]{2,1,0:T(8,128)(2,1)}, u32[]{:S(2)}, u32[]{:S(2)}) collective-permute-start(bf16[2,256,256]{2,1,0:T(8,128)(2,1)S(1)} %pad_maximum_fusion.1.refs_3_), channel_id=1, source_target_pairs={{0,4},{4,8},{8,12},{1,5},{5,9},{9,13},{2,6},{6,10},{10,14},{3,7},{... | collective-permute-start | bytes 786440 | tf_op jit(solution)/shard_map/ppermute | solution.py:117

commit v13 on v11

--- a/solution.py
+++ b/solution.py
@@ -38,7 +38,7 @@
 def attend_kernel(scalars, q_ref, *refs, rows, span, group, nparts, slots):
     part_refs = refs[:nparts]
     if slots:
-        o_ref, cache_ref, bias_ref = refs[nparts:]
+        o_ref, cache_ref, bias_ref, pick_ref = refs[nparts:]
     else:
         o_ref, bias_ref = refs[nparts:]
     seq_len = scalars[0]
@@ -52,7 +52,15 @@
         & (key_pos >= 0)
         & (key_pos < seq_len)
     )
-    bias_ref[...] = jnp.where(allowed, 0.0, neg_floor)
+
+    @pl.when(pl.program_id(0) == 0)
+    def _():
+        bias_ref[...] = jnp.where(allowed, 0.0, neg_floor)
+        if slots:
+            slot_pos = scalars[4] + lax.broadcasted_iota(jnp.int32, (slots, span), 0)
+            held_pos = scalars[3] + lax.broadcasted_iota(jnp.int32, (slots, span), 1)
+            pick_ref[...] = ((held_pos == slot_pos) & (slot_pos >= 0)).astype(jnp.bfloat16)
+
     if nparts == 1:
         k = part_refs[0][0, pl.ds(key_start, span), :]
         v = part_refs[0][1, pl.ds(key_start, span), :]
@@ -60,9 +68,7 @@
         k = jnp.concatenate([p[0] for p in part_refs], axis=0)
         v = jnp.concatenate([p[1] for p in part_refs], axis=0)
     if slots:
-        slot_pos = scalars[4] + lax.broadcasted_iota(jnp.int32, (slots, span), 0)
-        held_pos = scalars[3] + lax.broadcasted_iota(jnp.int32, (slots, span), 1)
-        pick = ((held_pos == slot_pos) & (slot_pos >= 0)).astype(jnp.bfloat16)
+        pick = pick_ref[...]
         cache_ref[0] = jnp.dot(pick, k, preferred_element_type=jnp.float32).astype(cache_ref.dtype)
         cache_ref[1] = jnp.dot(pick, v, preferred_element_type=jnp.float32).astype(cache_ref.dtype)
     valid = (first_pos + lax.broadcasted_iota(jnp.int32, (rows, 1), 0)) < seq_len
@@ -101,7 +107,8 @@
         in_specs=[pl.BlockSpec((rows, width), lambda j, s: (0, j))]
         + [pl.BlockSpec((2, p.shape[1], HD), lambda j, s: (0, 0, j)) for p in parts],
         out_specs=out_specs,
-        scratch_shapes=[pltpu.VMEM((rows, span), jnp.float32)],
+        scratch_shapes=[pltpu.VMEM((rows, span), jnp.float32)]
+        + ([pltpu.VMEM((slots, span), jnp.bfloat16)] if slots else []),
     )
     return pl.pallas_call(kernel, grid_spec=grid_spec, out_shape=out_shape)(
         scalars, rotated_q, *parts

time: 45.6 us -> 46.2 us (1.013)
  Pallas kernels: 12.3 us -> 12.8 us
    pallas_call x1, Pallas kernels: 12.3 us -> 12.8 us  [attention(): pl.pallas_call(kernel, grid_spec=grid_spec, out_shape=out_shape)]
where the time goes in v13:
time: 46.2 us; the launch traced here: 45.7 us
  waiting for transfers between devices  18.2 us (39%)
  Pallas kernels  12.8 us (28%)
  starting transfers between devices  6.07 us (13%)
  other arithmetic  4.07 us (9%)
  local copies, waits for them, and re-layouts  3.17 us (7%)
  between operations  1.44 us (3%)
    ppermute x3, waiting for transfers between devices, passed_along(): return lax.ppermute(x, 'seq', pairs)  18.2 us
    pallas_call x1, Pallas kernels, attention(): pl.pallas_call(kernel, grid_spec=grid_spec, out_shape=out_shape)  12.8 us
    ppermute x3, starting transfers between devices, passed_along(): return lax.ppermute(x, 'seq', pairs)  6.07 us
    unnamed x12, local copies, waits for them, and re-layouts  2.37 us
    another operation x2, other arithmetic  1.24 us
    convert_element_type x1, other arithmetic, local(): keys_values[0, 0].reshape(shard_rows, kv_heads_dev, HD).astype(jnp.float32)  1.08 us
    concatenate x2, other arithmetic, rotate(): jnp.concatenate([lower_half * cosine - upper_half * sine_part, upper_half...  0.94 us
  transfers between devices with their start and end apart: 3, of which 2 were waited for; matrix products, arithmetic and copies ran while one was open for 8% of the time, Pallas kernels for 0%

profile of v13, /device:TPU:20, one launch (start us, length us, event | category | flops | bytes accessed | tf_op | source)
XLA Modules:
  0.0 45.7 jit_solution(9532357402103287834)
XLA Ops:
  0.6 0.0 copy-start
  0.7 1.1 %slice_convert_fusion = (f32[1,1,256,256]{3,2,1,0:T(8,128)S(1)}, bf16[1,256,256]{2,1,0:T(8,128)(2,1)S(1)}) fusion(bf16[1,2,256,256]{3,2,1,0:T(8,128)(2,1)} %param.4), kind=kLoop, calls=%fused_computation.12 | loop fusion | flops 65536 | bytes 655360 | tf_op jit(solution)/shard_map/convert_element_type | solution.py:139
  1.8 0.1 reshape.86
  1.9 0.5 %multiply_cosine_fusion = (f32[256,64]{1,0:T(8,128)S(1)}, f32[256,64]{1,0:T(8,128)S(1)}) fusion(f32[64]{0:T(128)S(1)} %multiply_exponential_fusion, f32[256]{0:T(256)S(1)} %add_convert_fusion.2), kind=kLoop, calls=%fused_computation.9 | loop fusion | flops 16384 | bytes 132352 | tf_op jit(solution)/shard_map/cos | solution.py:25
  2.4 0.5 %subtract_convert_fusion.1 = (bf16[256,2,64]{2,1,0:T(2,128)(2,1)S(1)}, bf16[256,2,64]{2,1,0:T(2,128)(2,1)S(1)}) fusion(f32[256,2,128]{2,1,0:T(2,128)S(1)} %reshape.86, f32[256,64]{1,0:T(8,128)S(1)} %get-tuple-element.13, f32[256,64]{1,0:T(8,128)S(1)} %get-tuple-element.12), kind=kLoop, calls=%fused_computation.7 | loop fusion | flops 262144 | bytes 524288 | tf_op jit(solution)/shard_map/convert.2
  2.9 0.4 pad_maximum_fusion.2
  3.3 0.1 convert_element_type.42
  3.4 0.0 copy-start.1
  3.4 0.7 %collective-permute-start = (bf16[2,256,256]{2,1,0:T(8,128)(2,1)S(1)}, bf16[2,256,256]{2,1,0:T(8,128)(2,1)S(1)}, u32[]{:S(2)}, u32[]{:S(2)}) collective-permute-start(bf16[2,256,256]{2,1,0:T(8,128)(2,1)S(1)} %pad_maximum_fusion.1.refs_3_), channel_id=1, source_target_pairs={{0,12},{1,13},{2,14},{3,15},{16,28},{17,29},{18,30},{19,31}} | collective-permute-start | bytes 786440 | tf_op jit(solution)/shard_map/ppermute | solution.py:121
  4.1 1.3 %collective-permute-start.1 = (bf16[2,256,256]{2,1,0:T(8,128)(2,1)S(1)}, bf16[2,256,256]{2,1,0:T(8,128)(2,1)S(1)}, u32[]{:S(2)}, u32[]{:S(2)}) collective-permute-start(bf16[2,256,256]{2,1,0:T(8,128)(2,1)S(1)} %pad_maximum_fusion.1.refs_3_), channel_id=1, source_target_pairs={{0,8},{4,12},{1,9},{5,13},{2,10},{6,14},{3,11},{7,15},{16,24},{20,... | collective-permute-start | bytes 786440 | tf_op jit(solution)/shard_map/ppermute | solution.py:121
  5.4 4.1 %collective-permute-start.2 = (bf16[2,256,256]{2,1,0:T(8,128)(2,1)S(1)}, bf16[2,256,256]{2,1,0:T(8,128)(2,1)S(1)}, u32[]{:S(2)}, u32[]{:S(2)}) collective-permute-start(bf16[2,256,256]{2,1,0:T(8,128)(2,1)S(1)} %pad_maximum_fusion.1.refs_3_), channel_id=1, source_target_pairs={{0,4},{4,8},{8,12},{1,5},{5,9},{9,13},{2,6},{6,10},{10,14},{3,7},{... | collective-permute-start | bytes 786440 | tf_op jit(solution)/shard_map/ppermute | solution.py:121
  9.5 0.0 copy-done
  9.5 0.2 convert_bitcast_fusion
  9.8 0.4 copy.5
  10.2 0.0 copy-done.1
  10.2 0.8 %subtract_convert_fusion = (bf16[256,16,64]{2,1,0:T(8,128)(2,1)S(1)}, bf16[256,16,64]{2,1,0:T(8,128)(2,1)S(1)}) fusion(f32[256,16,128]{2,1,0:T(8,128)S(1)} %bitcast.18, f32[256,64]{1,0:T(8,128)S(1)} %get-tuple-element.13, f32[256,64]{1,0:T(8,128)S(1)} %get-tuple-element.12), kind=kLoop, calls=%fused_computation.2 | loop fusion | flops 2097152 | bytes 3276800 | tf_op jit(solution)/shard_map/convert.4
  11.6 0.6 %pad_maximum_fusion = bf16[256,16,128]{2,1,0:T(8,128)(2,1)S(1)} fusion(bf16[256,16,64]{2,1,0:T(8,128)(2,1)S(1)} %get-tuple-element.7, bf16[256,16,64]{2,1,0:T(8,128)(2,1)S(1)} %get-tuple-element.6), kind=kLoop, calls=%fused_computation.4 | loop fusion | flops 2097152 | bytes 2097152 | tf_op jit(solution)/shard_map/concatenate | solution.py:29
  12.2 1.2 %copy.8 = bf16[32,8,16,128]{3,1,2,0:T(8,128)(2,1)} copy(bf16[32,8,16,128]{3,2,1,0:T(8,128)(2,1)S(1)} %bitcast.19) | data formatting | bytes 2097152
  13.4 0.6 %stack.18.scalars = s32[5]{0:T(128)} concatenate(s32[1]{0:T(128)S(6)} %copy.9, s32[1]{0:T(128)} %bitcast, s32[1]{0:T(128)} %constant.15.clone.1, s32[1]{0:T(128)} %bitcast.1, s32[1]{0:T(128)} %bitcast.3), dimensions={0} | concatenate | bytes 40 | tf_op jit(solution)/shard_map/stack | solution.py:164
  14.0 0.0 collective-permute-done.refs_0_
  14.0 0.0 copy-start.2
  14.0 8.1 %collective-permute-done.1.refs_1_ = bf16[2,256,256]{2,1,0:T(8,128)(2,1)S(1)} collective-permute-done((bf16[2,256,256]{2,1,0:T(8,128)(2,1)S(1)}, bf16[2,256,256]{2,1,0:T(8,128)(2,1)S(1)}, u32[]{:S(2)}, u32[]{:S(2)}) %collective-permute-start.1) | collective-permute-done | bytes 262176 | tf_op jit(solution)/shard_map/ppermute | solution.py:121
  22.1 0.0 copy-start.3
  22.1 10.0 %collective-permute-done.2.refs_2_ = bf16[2,256,256]{2,1,0:T(8,128)(2,1)S(1)} collective-permute-done((bf16[2,256,256]{2,1,0:T(8,128)(2,1)S(1)}, bf16[2,256,256]{2,1,0:T(8,128)(2,1)S(1)}, u32[]{:S(2)}, u32[]{:S(2)}) %collective-permute-start.2) | collective-permute-done | bytes 262176 | tf_op jit(solution)/shard_map/ppermute | solution.py:121
  32.2 0.0 copy-start.4
  32.2 0.0 copy-done.2
  32.2 0.0 copy-done.3
  32.2 0.7 %copy-done.4 = bf16[2,256,256]{2,1,0:T(8,128)(2,1)} copy-done((bf16[2,256,256]{2,1,0:T(8,128)(2,1)}, bf16[2,256,256]{2,1,0:T(8,128)(2,1)S(1)}, u32[]{:S(2)}) %copy-start.4) | copy-done | bytes 262168
  32.9 12.8 %shard_map.50 = (bf16[256,2048]{1,0:T(8,128)(2,1)}, bf16[2,512,256]{2,1,0:T(8,128)(2,1)}) custom-call(s32[5]{0:T(128)} %stack.18.scalars, bf16[256,2048]{1,0:T(8,128)(2,1)} %bitcast.20, bf16[2,256,256]{2,1,0:T(8,128)(2,1)} %copy-done.2, bf16[2,256,256]{2,1,0:T(8,128)(2,1)} %copy-done.3, bf16[2,256,256]{2,1,0:T(8,128)(2,1)} %copy-done.4, ...), custom_call_target="tpu_custom_call" | custom-call | tf_op jit(solution)/shard_map/pallas_call | solution.py:113
  (3 shorter events, 0.0 us)
Async XLA Ops:
  0.6 8.9 %copy-start = (bf16[1,256,2048]{2,1,0:T(8,128)(2,1)S(1)}, bf16[1,256,2048]{2,1,0:T(8,128)(2,1)}, u32[]{:S(2)}) copy-start(bf16[1,256,2048]{2,1,0:T(8,128)(2,1)} %param.3) | copy-start | bytes 3145732
  3.4 6.8 %copy-start.1 = (bf16[2,256,256]{2,1,0:T(8,128)(2,1)}, bf16[2,256,256]{2,1,0:T(8,128)(2,1)S(1)}, u32[]{:S(2)}) copy-start(bf16[2,256,256]{2,1,0:T(8,128)(2,1)S(1)} %pad_maximum_fusion.1.refs_3_) | copy-start | bytes 786436
  3.4 10.6 %collective-permute-start = (bf16[2,256,256]{2,1,0:T(8,128)(2,1)S(1)}, bf16[2,256,256]{2,1,0:T(8,128)(2,1)S(1)}, u32[]{:S(2)}, u32[]{:S(2)}) collective-permute-start(bf16[2,256,256]{2,1,0:T(8,128)(2,1)S(1)} %pad_maximum_fusion.1.refs_3_), channel_id=1, source_target_pairs={{0,12},{1,13},{2,14},{3,15},{16,28},{17,29},{18,30},{19,31}} | collective-permute-start | bytes 786440 | tf_op jit(solution)/shard_map/ppermute | solution.py:121
  4.1 18.0 %collective-permute-start.1 = (bf16[2,256,256]{2,1,0:T(8,128)(2,1)S(1)}, bf16[2,256,256]{2,1,0:T(8,128)(2,1)S(1)}, u32[]{:S(2)}, u32[]{:S(2)}) collective-permute-start(bf16[2,256,256]{2,1,0:T(8,128)(2,1)S(1)} %pad_maximum_fusion.1.refs_3_), channel_id=1, source_target_pairs={{0,8},{4,12},{1,9},{5,13},{2,10},{6,14},{3,11},{7,15},{16,24},{20,... | collective-permute-start | bytes 786440 | tf_op jit(solution)/shard_map/ppermute | solution.py:121
  5.4 26.8 %collective-permute-start.2 = (bf16[2,256,256]{2,1,0:T(8,128)(2,1)S(1)}, bf16[2,256,256]{2,1,0:T(8,128)(2,1)S(1)}, u32[]{:S(2)}, u32[]{:S(2)}) collective-permute-start(bf16[2,256,256]{2,1,0:T(8,128)(2,1)S(1)} %pad_maximum_fusion.1.refs_3_), channel_id=1, source_target_pairs={{0,4},{4,8},{8,12},{1,5},{5,9},{9,13},{2,6},{6,10},{10,14},{3,7},{... | collective-permute-start | bytes 786440 | tf_op jit(solution)/shard_map/ppermute | solution.py:121
  14.0 18.2 %copy-start.2 = (bf16[2,256,256]{2,1,0:T(8,128)(2,1)}, bf16[2,256,256]{2,1,0:T(8,128)(2,1)S(1)}, u32[]{:S(2)}) copy-start(bf16[2,256,256]{2,1,0:T(8,128)(2,1)S(1)} %collective-permute-done.refs_0_) | copy-start | bytes 786436
  22.1 10.1 %copy-start.3 = (bf16[2,256,256]{2,1,0:T(8,128)(2,1)}, bf16[2,256,256]{2,1,0:T(8,128)(2,1)S(1)}, u32[]{:S(2)}) copy-start(bf16[2,256,256]{2,1,0:T(8,128)(2,1)S(1)} %collective-permute-done.1.refs_1_) | copy-start | bytes 786436
  32.2 0.7 %copy-start.4 = (bf16[2,256,256]{2,1,0:T(8,128)(2,1)}, bf16[2,256,256]{2,1,0:T(8,128)(2,1)S(1)}, u32[]{:S(2)}) copy-start(bf16[2,256,256]{2,1,0:T(8,128)(2,1)S(1)} %collective-permute-done.2.refs_2_) | copy-start | bytes 786436

commit v14 on v11

--- a/solution.py
+++ b/solution.py
@@ -53,12 +53,13 @@
         & (key_pos < seq_len)
     )
     bias_ref[...] = jnp.where(allowed, 0.0, neg_floor)
+    col = pl.ds(pl.multiple_of(pl.program_id(0) * HD, HD), HD)
     if nparts == 1:
-        k = part_refs[0][0, pl.ds(key_start, span), :]
-        v = part_refs[0][1, pl.ds(key_start, span), :]
+        k = part_refs[0][0, pl.ds(key_start, span), col]
+        v = part_refs[0][1, pl.ds(key_start, span), col]
     else:
-        k = jnp.concatenate([p[0] for p in part_refs], axis=0)
-        v = jnp.concatenate([p[1] for p in part_refs], axis=0)
+        k = jnp.concatenate([p[0, :, col] for p in part_refs], axis=0)
+        v = jnp.concatenate([p[1, :, col] for p in part_refs], axis=0)
     if slots:
         slot_pos = scalars[4] + lax.broadcasted_iota(jnp.int32, (slots, span), 0)
         held_pos = scalars[3] + lax.broadcasted_iota(jnp.int32, (slots, span), 1)
@@ -99,7 +100,7 @@
         num_scalar_prefetch=1,
         grid=(kv_heads_dev,),
         in_specs=[pl.BlockSpec((rows, width), lambda j, s: (0, j))]
-        + [pl.BlockSpec((2, p.shape[1], HD), lambda j, s: (0, 0, j)) for p in parts],
+        + [pl.BlockSpec(memory_space=pltpu.VMEM) for p in parts],
         out_specs=out_specs,
         scratch_shapes=[pltpu.VMEM((rows, span), jnp.float32)],
     )

time: 45.6 us -> 45.8 us (level)
  no operation moved by 1% of the time
where the time goes in v14:
time: 45.8 us; the launch traced here: 45.4 us
  waiting for transfers between devices  18.2 us (40%)
  Pallas kernels  12.5 us (27%)
  starting transfers between devices  6.07 us (13%)
  other arithmetic  4.07 us (9%)
  local copies, waits for them, and re-layouts  3.17 us (7%)
  between operations  1.44 us (3%)
    ppermute x3, waiting for transfers between devices, passed_along(): return lax.ppermute(x, 'seq', pairs)  18.2 us
    pallas_call x1, Pallas kernels, attention(): pl.pallas_call(kernel, grid_spec=grid_spec, out_shape=out_shape)  12.5 us
    ppermute x3, starting transfers between devices, passed_along(): return lax.ppermute(x, 'seq', pairs)  6.07 us
    unnamed x12, local copies, waits for them, and re-layouts  2.37 us
    another operation x2, other arithmetic  1.24 us
    convert_element_type x1, other arithmetic, local(): keys_values[0, 0].reshape(shard_rows, kv_heads_dev, HD).astype(jnp.float32)  1.08 us
    concatenate x2, other arithmetic, rotate(): jnp.concatenate([lower_half * cosine - upper_half * sine_part, upper_half...  0.94 us
  transfers between devices with their start and end apart: 3, of which 2 were waited for; matrix products, arithmetic and copies ran while one was open for 8% of the time, Pallas kernels for 0%

profile of v14, /device:TPU:20, one launch (start us, length us, event | category | flops | bytes accessed | tf_op | source)
XLA Modules:
  0.0 45.4 jit_solution(3777609795149291115)
XLA Ops:
  0.6 0.0 copy-start
  0.7 1.1 %slice_convert_fusion = (f32[1,1,256,256]{3,2,1,0:T(8,128)S(1)}, bf16[1,256,256]{2,1,0:T(8,128)(2,1)S(1)}) fusion(bf16[1,2,256,256]{3,2,1,0:T(8,128)(2,1)} %param.4), kind=kLoop, calls=%fused_computation.12 | loop fusion | flops 65536 | bytes 655360 | tf_op jit(solution)/shard_map/convert_element_type | solution.py:133
  1.8 0.1 reshape.86
  1.9 0.5 %multiply_cosine_fusion = (f32[256,64]{1,0:T(8,128)S(1)}, f32[256,64]{1,0:T(8,128)S(1)}) fusion(f32[64]{0:T(128)S(1)} %multiply_exponential_fusion, f32[256]{0:T(256)S(1)} %add_convert_fusion.2), kind=kLoop, calls=%fused_computation.9 | loop fusion | flops 16384 | bytes 132352 | tf_op jit(solution)/shard_map/cos | solution.py:25
  2.4 0.5 %subtract_convert_fusion.1 = (bf16[256,2,64]{2,1,0:T(2,128)(2,1)S(1)}, bf16[256,2,64]{2,1,0:T(2,128)(2,1)S(1)}) fusion(f32[256,2,128]{2,1,0:T(2,128)S(1)} %reshape.86, f32[256,64]{1,0:T(8,128)S(1)} %get-tuple-element.13, f32[256,64]{1,0:T(8,128)S(1)} %get-tuple-element.12), kind=kLoop, calls=%fused_computation.7 | loop fusion | flops 262144 | bytes 524288 | tf_op jit(solution)/shard_map/convert.2
  2.9 0.4 pad_maximum_fusion.2
  3.3 0.1 convert_element_type.42
  3.4 0.0 copy-start.1
  3.4 0.7 %collective-permute-start = (bf16[2,256,256]{2,1,0:T(8,128)(2,1)S(1)}, bf16[2,256,256]{2,1,0:T(8,128)(2,1)S(1)}, u32[]{:S(2)}, u32[]{:S(2)}) collective-permute-start(bf16[2,256,256]{2,1,0:T(8,128)(2,1)S(1)} %pad_maximum_fusion.1.refs_3_), channel_id=1, source_target_pairs={{0,12},{1,13},{2,14},{3,15},{16,28},{17,29},{18,30},{19,31}} | collective-permute-start | bytes 786440 | tf_op jit(solution)/shard_map/ppermute | solution.py:115
  4.1 1.3 %collective-permute-start.1 = (bf16[2,256,256]{2,1,0:T(8,128)(2,1)S(1)}, bf16[2,256,256]{2,1,0:T(8,128)(2,1)S(1)}, u32[]{:S(2)}, u32[]{:S(2)}) collective-permute-start(bf16[2,256,256]{2,1,0:T(8,128)(2,1)S(1)} %pad_maximum_fusion.1.refs_3_), channel_id=1, source_target_pairs={{0,8},{4,12},{1,9},{5,13},{2,10},{6,14},{3,11},{7,15},{16,24},{20,... | collective-permute-start | bytes 786440 | tf_op jit(solution)/shard_map/ppermute | solution.py:115
  5.4 4.1 %collective-permute-start.2 = (bf16[2,256,256]{2,1,0:T(8,128)(2,1)S(1)}, bf16[2,256,256]{2,1,0:T(8,128)(2,1)S(1)}, u32[]{:S(2)}, u32[]{:S(2)}) collective-permute-start(bf16[2,256,256]{2,1,0:T(8,128)(2,1)S(1)} %pad_maximum_fusion.1.refs_3_), channel_id=1, source_target_pairs={{0,4},{4,8},{8,12},{1,5},{5,9},{9,13},{2,6},{6,10},{10,14},{3,7},{... | collective-permute-start | bytes 786440 | tf_op jit(solution)/shard_map/ppermute | solution.py:115
  9.5 0.0 copy-done
  9.5 0.2 convert_bitcast_fusion
  9.8 0.4 copy.5
  10.2 0.0 copy-done.1
  10.2 0.8 %subtract_convert_fusion = (bf16[256,16,64]{2,1,0:T(8,128)(2,1)S(1)}, bf16[256,16,64]{2,1,0:T(8,128)(2,1)S(1)}) fusion(f32[256,16,128]{2,1,0:T(8,128)S(1)} %bitcast.18, f32[256,64]{1,0:T(8,128)S(1)} %get-tuple-element.13, f32[256,64]{1,0:T(8,128)S(1)} %get-tuple-element.12), kind=kLoop, calls=%fused_computation.2 | loop fusion | flops 2097152 | bytes 3276800 | tf_op jit(solution)/shard_map/convert.4
  11.6 0.6 %pad_maximum_fusion = bf16[256,16,128]{2,1,0:T(8,128)(2,1)S(1)} fusion(bf16[256,16,64]{2,1,0:T(8,128)(2,1)S(1)} %get-tuple-element.7, bf16[256,16,64]{2,1,0:T(8,128)(2,1)S(1)} %get-tuple-element.6), kind=kLoop, calls=%fused_computation.4 | loop fusion | flops 2097152 | bytes 2097152 | tf_op jit(solution)/shard_map/concatenate | solution.py:29
  12.2 1.2 %copy.8 = bf16[32,8,16,128]{3,1,2,0:T(8,128)(2,1)} copy(bf16[32,8,16,128]{3,2,1,0:T(8,128)(2,1)S(1)} %bitcast.19) | data formatting | bytes 2097152
  13.4 0.6 %stack.18.scalars = s32[5]{0:T(128)} concatenate(s32[1]{0:T(128)S(6)} %copy.9, s32[1]{0:T(128)} %bitcast, s32[1]{0:T(128)} %constant.15.clone.1, s32[1]{0:T(128)} %bitcast.1, s32[1]{0:T(128)} %bitcast.3), dimensions={0} | concatenate | bytes 40 | tf_op jit(solution)/shard_map/stack | solution.py:158
  14.0 0.0 collective-permute-done.refs_0_
  14.0 0.0 copy-start.2
  14.0 8.1 %collective-permute-done.1.refs_1_ = bf16[2,256,256]{2,1,0:T(8,128)(2,1)S(1)} collective-permute-done((bf16[2,256,256]{2,1,0:T(8,128)(2,1)S(1)}, bf16[2,256,256]{2,1,0:T(8,128)(2,1)S(1)}, u32[]{:S(2)}, u32[]{:S(2)}) %collective-permute-start.1) | collective-permute-done | bytes 262176 | tf_op jit(solution)/shard_map/ppermute | solution.py:115
  22.1 0.0 copy-start.3
  22.1 10.0 %collective-permute-done.2.refs_2_ = bf16[2,256,256]{2,1,0:T(8,128)(2,1)S(1)} collective-permute-done((bf16[2,256,256]{2,1,0:T(8,128)(2,1)S(1)}, bf16[2,256,256]{2,1,0:T(8,128)(2,1)S(1)}, u32[]{:S(2)}, u32[]{:S(2)}) %collective-permute-start.2) | collective-permute-done | bytes 262176 | tf_op jit(solution)/shard_map/ppermute | solution.py:115
  32.2 0.0 copy-start.4
  32.2 0.0 copy-done.2
  32.2 0.0 copy-done.3
  32.2 0.7 %copy-done.4 = bf16[2,256,256]{2,1,0:T(8,128)(2,1)} copy-done((bf16[2,256,256]{2,1,0:T(8,128)(2,1)}, bf16[2,256,256]{2,1,0:T(8,128)(2,1)S(1)}, u32[]{:S(2)}) %copy-start.4) | copy-done | bytes 262168
  32.9 12.5 %shard_map.50 = (bf16[256,2048]{1,0:T(8,128)(2,1)}, bf16[2,512,256]{2,1,0:T(8,128)(2,1)}) custom-call(s32[5]{0:T(128)} %stack.18.scalars, bf16[256,2048]{1,0:T(8,128)(2,1)} %bitcast.20, bf16[2,256,256]{2,1,0:T(8,128)(2,1)} %copy-done.2, bf16[2,256,256]{2,1,0:T(8,128)(2,1)} %copy-done.3, bf16[2,256,256]{2,1,0:T(8,128)(2,1)} %copy-done.4, ...), custom_call_target="tpu_custom_call" | custom-call | tf_op jit(solution)/shard_map/pallas_call | solution.py:107
  (3 shorter events, 0.0 us)
Async XLA Ops:
  0.6 8.9 %copy-start = (bf16[1,256,2048]{2,1,0:T(8,128)(2,1)S(1)}, bf16[1,256,2048]{2,1,0:T(8,128)(2,1)}, u32[]{:S(2)}) copy-start(bf16[1,256,2048]{2,1,0:T(8,128)(2,1)} %param.3) | copy-start | bytes 3145732
  3.4 6.8 %copy-start.1 = (bf16[2,256,256]{2,1,0:T(8,128)(2,1)}, bf16[2,256,256]{2,1,0:T(8,128)(2,1)S(1)}, u32[]{:S(2)}) copy-start(bf16[2,256,256]{2,1,0:T(8,128)(2,1)S(1)} %pad_maximum_fusion.1.refs_3_) | copy-start | bytes 786436
  3.4 10.6 %collective-permute-start = (bf16[2,256,256]{2,1,0:T(8,128)(2,1)S(1)}, bf16[2,256,256]{2,1,0:T(8,128)(2,1)S(1)}, u32[]{:S(2)}, u32[]{:S(2)}) collective-permute-start(bf16[2,256,256]{2,1,0:T(8,128)(2,1)S(1)} %pad_maximum_fusion.1.refs_3_), channel_id=1, source_target_pairs={{0,12},{1,13},{2,14},{3,15},{16,28},{17,29},{18,30},{19,31}} | collective-permute-start | bytes 786440 | tf_op jit(solution)/shard_map/ppermute | solution.py:115
  4.1 18.0 %collective-permute-start.1 = (bf16[2,256,256]{2,1,0:T(8,128)(2,1)S(1)}, bf16[2,256,256]{2,1,0:T(8,128)(2,1)S(1)}, u32[]{:S(2)}, u32[]{:S(2)}) collective-permute-start(bf16[2,256,256]{2,1,0:T(8,128)(2,1)S(1)} %pad_maximum_fusion.1.refs_3_), channel_id=1, source_target_pairs={{0,8},{4,12},{1,9},{5,13},{2,10},{6,14},{3,11},{7,15},{16,24},{20,... | collective-permute-start | bytes 786440 | tf_op jit(solution)/shard_map/ppermute | solution.py:115
  5.4 26.8 %collective-permute-start.2 = (bf16[2,256,256]{2,1,0:T(8,128)(2,1)S(1)}, bf16[2,256,256]{2,1,0:T(8,128)(2,1)S(1)}, u32[]{:S(2)}, u32[]{:S(2)}) collective-permute-start(bf16[2,256,256]{2,1,0:T(8,128)(2,1)S(1)} %pad_maximum_fusion.1.refs_3_), channel_id=1, source_target_pairs={{0,4},{4,8},{8,12},{1,5},{5,9},{9,13},{2,6},{6,10},{10,14},{3,7},{... | collective-permute-start | bytes 786440 | tf_op jit(solution)/shard_map/ppermute | solution.py:115
  14.0 18.2 %copy-start.2 = (bf16[2,256,256]{2,1,0:T(8,128)(2,1)}, bf16[2,256,256]{2,1,0:T(8,128)(2,1)S(1)}, u32[]{:S(2)}) copy-start(bf16[2,256,256]{2,1,0:T(8,128)(2,1)S(1)} %collective-permute-done.refs_0_) | copy-start | bytes 786436
  22.1 10.1 %copy-start.3 = (bf16[2,256,256]{2,1,0:T(8,128)(2,1)}, bf16[2,256,256]{2,1,0:T(8,128)(2,1)S(1)}, u32[]{:S(2)}) copy-start(bf16[2,256,256]{2,1,0:T(8,128)(2,1)S(1)} %collective-permute-done.1.refs_1_) | copy-start | bytes 786436
  32.2 0.7 %copy-start.4 = (bf16[2,256,256]{2,1,0:T(8,128)(2,1)}, bf16[2,256,256]{2,1,0:T(8,128)(2,1)S(1)}, u32[]{:S(2)}) copy-start(bf16[2,256,256]{2,1,0:T(8,128)(2,1)S(1)} %collective-permute-done.2.refs_2_) | copy-start | bytes 786436

commit v15 on v11

--- a/solution.py
+++ b/solution.py
@@ -76,8 +76,8 @@
         weights = jnp.exp((raw - row_top) * scale)
         totals = jnp.sum(weights, axis=-1, keepdims=True)
         numer = jnp.dot(weights.astype(jnp.bfloat16), v, preferred_element_type=jnp.float32)
-        denom = jnp.where(valid, totals, 1.0)
-        o_ref[:, cols] = jnp.where(valid, numer / denom, 0.0).astype(o_ref.dtype)
+        inverse = jnp.where(valid, 1.0 / jnp.where(valid, totals, 1.0), 0.0)
+        o_ref[:, cols] = (numer * inverse).astype(o_ref.dtype)
 
 
 def attention(scalars, rotated_q, parts, kv_heads_dev, group_size, span, slots):

time: 45.6 us -> 45.6 us (level)
  no operation moved by 1% of the time
where the time goes in v15:
time: 45.6 us; the launch traced here: 45.2 us
  waiting for transfers between devices  18.2 us (40%)
  Pallas kernels  12.3 us (27%)
  starting transfers between devices  6.07 us (13%)
  other arithmetic  4.07 us (9%)
  local copies, waits for them, and re-layouts  3.17 us (7%)
  between operations  1.44 us (3%)
    ppermute x3, waiting for transfers between devices, passed_along(): return lax.ppermute(x, 'seq', pairs)  18.2 us
    pallas_call x1, Pallas kernels, attention(): pl.pallas_call(kernel, grid_spec=grid_spec, out_shape=out_shape)  12.3 us
    ppermute x3, starting transfers between devices, passed_along(): return lax.ppermute(x, 'seq', pairs)  6.07 us
    unnamed x12, local copies, waits for them, and re-layouts  2.37 us
    another operation x2, other arithmetic  1.24 us
    convert_element_type x1, other arithmetic, local(): keys_values[0, 0].reshape(shard_rows, kv_heads_dev, HD).astype(jnp.float32)  1.08 us
    concatenate x2, other arithmetic, rotate(): jnp.concatenate([lower_half * cosine - upper_half * sine_part, upper_half...  0.94 us
  transfers between devices with their start and end apart: 3, of which 2 were waited for; matrix products, arithmetic and copies ran while one was open for 8% of the time, Pallas kernels for 0%

profile of v15, /device:TPU:20, one launch (start us, length us, event | category | flops | bytes accessed | tf_op | source)
XLA Modules:
  0.0 45.2 jit_solution(15969341339588843184)
XLA Ops:
  0.6 0.0 copy-start
  0.7 1.1 %slice_convert_fusion = (f32[1,1,256,256]{3,2,1,0:T(8,128)S(1)}, bf16[1,256,256]{2,1,0:T(8,128)(2,1)S(1)}) fusion(bf16[1,2,256,256]{3,2,1,0:T(8,128)(2,1)} %param.4), kind=kLoop, calls=%fused_computation.12 | loop fusion | flops 65536 | bytes 655360 | tf_op jit(solution)/shard_map/convert_element_type | solution.py:132
  1.8 0.1 reshape.86
  1.9 0.5 %multiply_cosine_fusion = (f32[256,64]{1,0:T(8,128)S(1)}, f32[256,64]{1,0:T(8,128)S(1)}) fusion(f32[64]{0:T(128)S(1)} %multiply_exponential_fusion, f32[256]{0:T(256)S(1)} %add_convert_fusion.2), kind=kLoop, calls=%fused_computation.9 | loop fusion | flops 16384 | bytes 132352 | tf_op jit(solution)/shard_map/cos | solution.py:25
  2.4 0.5 %subtract_convert_fusion.1 = (bf16[256,2,64]{2,1,0:T(2,128)(2,1)S(1)}, bf16[256,2,64]{2,1,0:T(2,128)(2,1)S(1)}) fusion(f32[256,2,128]{2,1,0:T(2,128)S(1)} %reshape.86, f32[256,64]{1,0:T(8,128)S(1)} %get-tuple-element.13, f32[256,64]{1,0:T(8,128)S(1)} %get-tuple-element.12), kind=kLoop, calls=%fused_computation.7 | loop fusion | flops 262144 | bytes 524288 | tf_op jit(solution)/shard_map/convert.2
  2.9 0.4 pad_maximum_fusion.2
  3.3 0.1 convert_element_type.42
  3.4 0.0 copy-start.1
  3.4 0.7 %collective-permute-start = (bf16[2,256,256]{2,1,0:T(8,128)(2,1)S(1)}, bf16[2,256,256]{2,1,0:T(8,128)(2,1)S(1)}, u32[]{:S(2)}, u32[]{:S(2)}) collective-permute-start(bf16[2,256,256]{2,1,0:T(8,128)(2,1)S(1)} %pad_maximum_fusion.1.refs_3_), channel_id=1, source_target_pairs={{0,12},{1,13},{2,14},{3,15},{16,28},{17,29},{18,30},{19,31}} | collective-permute-start | bytes 786440 | tf_op jit(solution)/shard_map/ppermute | solution.py:114
  4.1 1.3 %collective-permute-start.1 = (bf16[2,256,256]{2,1,0:T(8,128)(2,1)S(1)}, bf16[2,256,256]{2,1,0:T(8,128)(2,1)S(1)}, u32[]{:S(2)}, u32[]{:S(2)}) collective-permute-start(bf16[2,256,256]{2,1,0:T(8,128)(2,1)S(1)} %pad_maximum_fusion.1.refs_3_), channel_id=1, source_target_pairs={{0,8},{4,12},{1,9},{5,13},{2,10},{6,14},{3,11},{7,15},{16,24},{20,... | collective-permute-start | bytes 786440 | tf_op jit(solution)/shard_map/ppermute | solution.py:114
  5.4 4.1 %collective-permute-start.2 = (bf16[2,256,256]{2,1,0:T(8,128)(2,1)S(1)}, bf16[2,256,256]{2,1,0:T(8,128)(2,1)S(1)}, u32[]{:S(2)}, u32[]{:S(2)}) collective-permute-start(bf16[2,256,256]{2,1,0:T(8,128)(2,1)S(1)} %pad_maximum_fusion.1.refs_3_), channel_id=1, source_target_pairs={{0,4},{4,8},{8,12},{1,5},{5,9},{9,13},{2,6},{6,10},{10,14},{3,7},{... | collective-permute-start | bytes 786440 | tf_op jit(solution)/shard_map/ppermute | solution.py:114
  9.5 0.0 copy-done
  9.5 0.2 convert_bitcast_fusion
  9.8 0.4 copy.5
  10.2 0.0 copy-done.1
  10.2 0.8 %subtract_convert_fusion = (bf16[256,16,64]{2,1,0:T(8,128)(2,1)S(1)}, bf16[256,16,64]{2,1,0:T(8,128)(2,1)S(1)}) fusion(f32[256,16,128]{2,1,0:T(8,128)S(1)} %bitcast.18, f32[256,64]{1,0:T(8,128)S(1)} %get-tuple-element.13, f32[256,64]{1,0:T(8,128)S(1)} %get-tuple-element.12), kind=kLoop, calls=%fused_computation.2 | loop fusion | flops 2097152 | bytes 3276800 | tf_op jit(solution)/shard_map/convert.4
  11.6 0.6 %pad_maximum_fusion = bf16[256,16,128]{2,1,0:T(8,128)(2,1)S(1)} fusion(bf16[256,16,64]{2,1,0:T(8,128)(2,1)S(1)} %get-tuple-element.7, bf16[256,16,64]{2,1,0:T(8,128)(2,1)S(1)} %get-tuple-element.6), kind=kLoop, calls=%fused_computation.4 | loop fusion | flops 2097152 | bytes 2097152 | tf_op jit(solution)/shard_map/concatenate | solution.py:29
  12.2 1.2 %copy.8 = bf16[32,8,16,128]{3,1,2,0:T(8,128)(2,1)} copy(bf16[32,8,16,128]{3,2,1,0:T(8,128)(2,1)S(1)} %bitcast.19) | data formatting | bytes 2097152
  13.4 0.6 %stack.18.scalars = s32[5]{0:T(128)} concatenate(s32[1]{0:T(128)S(6)} %copy.9, s32[1]{0:T(128)} %bitcast, s32[1]{0:T(128)} %constant.15.clone.1, s32[1]{0:T(128)} %bitcast.1, s32[1]{0:T(128)} %bitcast.3), dimensions={0} | concatenate | bytes 40 | tf_op jit(solution)/shard_map/stack | solution.py:157
  14.0 0.0 collective-permute-done.refs_0_
  14.0 0.0 copy-start.2
  14.0 8.1 %collective-permute-done.1.refs_1_ = bf16[2,256,256]{2,1,0:T(8,128)(2,1)S(1)} collective-permute-done((bf16[2,256,256]{2,1,0:T(8,128)(2,1)S(1)}, bf16[2,256,256]{2,1,0:T(8,128)(2,1)S(1)}, u32[]{:S(2)}, u32[]{:S(2)}) %collective-permute-start.1) | collective-permute-done | bytes 262176 | tf_op jit(solution)/shard_map/ppermute | solution.py:114
  22.1 0.0 copy-start.3
  22.1 10.0 %collective-permute-done.2.refs_2_ = bf16[2,256,256]{2,1,0:T(8,128)(2,1)S(1)} collective-permute-done((bf16[2,256,256]{2,1,0:T(8,128)(2,1)S(1)}, bf16[2,256,256]{2,1,0:T(8,128)(2,1)S(1)}, u32[]{:S(2)}, u32[]{:S(2)}) %collective-permute-start.2) | collective-permute-done | bytes 262176 | tf_op jit(solution)/shard_map/ppermute | solution.py:114
  32.2 0.0 copy-start.4
  32.2 0.0 copy-done.2
  32.2 0.0 copy-done.3
  32.2 0.7 %copy-done.4 = bf16[2,256,256]{2,1,0:T(8,128)(2,1)} copy-done((bf16[2,256,256]{2,1,0:T(8,128)(2,1)}, bf16[2,256,256]{2,1,0:T(8,128)(2,1)S(1)}, u32[]{:S(2)}) %copy-start.4) | copy-done | bytes 262168
  32.9 12.3 %shard_map.50 = (bf16[256,2048]{1,0:T(8,128)(2,1)}, bf16[2,512,256]{2,1,0:T(8,128)(2,1)}) custom-call(s32[5]{0:T(128)} %stack.18.scalars, bf16[256,2048]{1,0:T(8,128)(2,1)} %bitcast.20, bf16[2,256,256]{2,1,0:T(8,128)(2,1)} %copy-done.2, bf16[2,256,256]{2,1,0:T(8,128)(2,1)} %copy-done.3, bf16[2,256,256]{2,1,0:T(8,128)(2,1)} %copy-done.4, ...), custom_call_target="tpu_custom_call" | custom-call | tf_op jit(solution)/shard_map/pallas_call | solution.py:106
  (3 shorter events, 0.0 us)
Async XLA Ops:
  0.6 8.9 %copy-start = (bf16[1,256,2048]{2,1,0:T(8,128)(2,1)S(1)}, bf16[1,256,2048]{2,1,0:T(8,128)(2,1)}, u32[]{:S(2)}) copy-start(bf16[1,256,2048]{2,1,0:T(8,128)(2,1)} %param.3) | copy-start | bytes 3145732
  3.4 6.8 %copy-start.1 = (bf16[2,256,256]{2,1,0:T(8,128)(2,1)}, bf16[2,256,256]{2,1,0:T(8,128)(2,1)S(1)}, u32[]{:S(2)}) copy-start(bf16[2,256,256]{2,1,0:T(8,128)(2,1)S(1)} %pad_maximum_fusion.1.refs_3_) | copy-start | bytes 786436
  3.4 10.6 %collective-permute-start = (bf16[2,256,256]{2,1,0:T(8,128)(2,1)S(1)}, bf16[2,256,256]{2,1,0:T(8,128)(2,1)S(1)}, u32[]{:S(2)}, u32[]{:S(2)}) collective-permute-start(bf16[2,256,256]{2,1,0:T(8,128)(2,1)S(1)} %pad_maximum_fusion.1.refs_3_), channel_id=1, source_target_pairs={{0,12},{1,13},{2,14},{3,15},{16,28},{17,29},{18,30},{19,31}} | collective-permute-start | bytes 786440 | tf_op jit(solution)/shard_map/ppermute | solution.py:114
  4.1 18.0 %collective-permute-start.1 = (bf16[2,256,256]{2,1,0:T(8,128)(2,1)S(1)}, bf16[2,256,256]{2,1,0:T(8,128)(2,1)S(1)}, u32[]{:S(2)}, u32[]{:S(2)}) collective-permute-start(bf16[2,256,256]{2,1,0:T(8,128)(2,1)S(1)} %pad_maximum_fusion.1.refs_3_), channel_id=1, source_target_pairs={{0,8},{4,12},{1,9},{5,13},{2,10},{6,14},{3,11},{7,15},{16,24},{20,... | collective-permute-start | bytes 786440 | tf_op jit(solution)/shard_map/ppermute | solution.py:114
  5.4 26.8 %collective-permute-start.2 = (bf16[2,256,256]{2,1,0:T(8,128)(2,1)S(1)}, bf16[2,256,256]{2,1,0:T(8,128)(2,1)S(1)}, u32[]{:S(2)}, u32[]{:S(2)}) collective-permute-start(bf16[2,256,256]{2,1,0:T(8,128)(2,1)S(1)} %pad_maximum_fusion.1.refs_3_), channel_id=1, source_target_pairs={{0,4},{4,8},{8,12},{1,5},{5,9},{9,13},{2,6},{6,10},{10,14},{3,7},{... | collective-permute-start | bytes 786440 | tf_op jit(solution)/shard_map/ppermute | solution.py:114
  14.0 18.2 %copy-start.2 = (bf16[2,256,256]{2,1,0:T(8,128)(2,1)}, bf16[2,256,256]{2,1,0:T(8,128)(2,1)S(1)}, u32[]{:S(2)}) copy-start(bf16[2,256,256]{2,1,0:T(8,128)(2,1)S(1)} %collective-permute-done.refs_0_) | copy-start | bytes 786436
  22.1 10.1 %copy-start.3 = (bf16[2,256,256]{2,1,0:T(8,128)(2,1)}, bf16[2,256,256]{2,1,0:T(8,128)(2,1)S(1)}, u32[]{:S(2)}) copy-start(bf16[2,256,256]{2,1,0:T(8,128)(2,1)S(1)} %collective-permute-done.1.refs_1_) | copy-start | bytes 786436
  32.2 0.7 %copy-start.4 = (bf16[2,256,256]{2,1,0:T(8,128)(2,1)}, bf16[2,256,256]{2,1,0:T(8,128)(2,1)S(1)}, u32[]{:S(2)}) copy-start(bf16[2,256,256]{2,1,0:T(8,128)(2,1)S(1)} %collective-permute-done.2.refs_2_) | copy-start | bytes 786436
